TPU v7x, 512 devices: a whole 4x8x8 slice. The times are simulated.
512 devices in a mesh: seq: 128 (over y, z, core), head: 4 (over x).
Axes of the slice: x: 4, y: 8, z: 8, core: 2. Of those that a mesh axis runs over, the one named last changes fastest.
Arguments:
- out_grad: bfloat16 [16384, 4096], P('seq', 'head'), may hold values from -6 to 6
- expert_ids: int32 [16384, 8], P('seq'), may hold values from 0 to 127, all different within a row; in each aligned block of 128 rows (0 to 127, 128 to 255, ...) at most 12 rows name the same one
- top_logits: float32 [16384, 8], P('seq'), may hold values from -10 to 310
- doc_start: int32 [16384], P('seq'), may hold values from 0 to 16383, as said below
- router: bfloat16 [128, 4096], P(None, 'head'), may hold values from -0.09375 to 0.09375
- w_down: bfloat16 [128, 768, 4096], P('seq', None, 'head'), may hold values from -0.21875 to 0.21875
- saved_gu: bfloat16 [128, 2, 768, 1536], P('seq', None, 'head'), may hold values from -6 to 6
- out_weight: bfloat16 [4096, 4096], P('head', 'seq'), may hold values from -0.09375 to 0.09375
- query: bfloat16 [16384, 32, 128], P('seq', 'head'), may hold values from -64 to 64
- key: bfloat16 [16384, 4, 128], P('seq', 'head'), may hold values from -8 to 8
- value: bfloat16 [16384, 4, 128], P('seq', 'head'), may hold values from -6 to 6
Outputs:
- gate_up_grad: bfloat16 [128, 2, 768, 1536], P('seq', None, 'head')
- route_grad: float32 [16384, 8], P('seq')
- query_grad: bfloat16 [16384, 32, 128], P('seq', 'head')
- key_grad: bfloat16 [16384, 4, 128], P('seq', 'head')
- value_grad: bfloat16 [16384, 4, 128], P('seq', 'head')
Inputs may be any that keep to these rules, and one draw needn't show every extreme that they name: `expert_ids`: each token names 8 different experts; among the 128 tokens of one index of seq no expert is named by more than 12 tokens. doc_start[t] is the first position of the document that holds t; documents lie end to end, each has at most 896 tokens and one has exactly 896.
All inputs are finite; a program needn't handle non-finite values.
Results may differ from a plain program's by a relative error of at most 0.03.
Values may be sent and summed in bfloat16 or wider, within the bound.
No kernel may reach another device: no remote copies, remote signals or barrier semaphores. Data moves between devices by JAX's collectives and lax.ppermute only.
A program may use at most 128 MiB of HBM per device.

v0:
```python
import jax
import jax.numpy as jnp
from jax import lax
from jax.sharding import PartitionSpec as P

REACH = 7


masked_score = -1e30
highest = lax.Precision.HIGHEST


def passed_along(array, axis, by):
    count = lax.axis_size(axis)
    pairs = [(i, i + by) for i in range(count) if 0 <= i + by < count]
    return lax.ppermute(array, axis, pairs)


def attend(queries, upstream, keys_all, values_all, query_pos, key_pos, doc_begin, score_scale):
    scores = (
        jnp.einsum("tkgd,lkd->kgtl", queries, keys_all, preferred_element_type=jnp.float32)
        * score_scale
    )
    valid = (key_pos[None, :] <= query_pos[:, None]) & (key_pos[None, :] >= doc_begin[:, None])
    scores = jnp.where(valid[None, None], scores, masked_score)
    row_max = jnp.max(scores, axis=3, keepdims=True)
    exponent = jnp.exp(scores - row_max)
    probs = exponent / jnp.sum(exponent, axis=3, keepdims=True)
    dprob = jnp.einsum("tkgd,lkd->kgtl", upstream, values_all, preferred_element_type=jnp.float32)
    row_dot = jnp.sum(probs * dprob, axis=3, keepdims=True)
    probs_b = probs.astype(jnp.bfloat16)
    dscore = (probs * (dprob - row_dot)).astype(jnp.bfloat16)
    query_part = (
        jnp.einsum("kgtl,lkd->tkgd", dscore, keys_all, preferred_element_type=jnp.float32)
        * score_scale
    )
    key_part = (
        jnp.einsum("kgtl,tkgd->lkd", dscore, queries, preferred_element_type=jnp.float32)
        * score_scale
    )
    value_part = jnp.einsum("kgtl,tkgd->lkd", probs_b, upstream, preferred_element_type=jnp.float32)
    return (query_part, key_part, value_part)


def per_device(
    out_grad,
    expert_ids,
    top_logits,
    doc_start,
    router,
    w_down,
    saved_gu,
    out_weight,
    query,
    key,
    value,
):
    seq_count = lax.axis_size("seq")
    seq_index = lax.axis_index("seq")
    tokens_here = out_grad.shape[0]
    features = out_grad.shape[1]
    slots_all = saved_gu.shape[3]
    capacity = slots_all // seq_count
    experts = router.shape[0]
    top_count = expert_ids.shape[1]
    weights = jax.nn.softmax(top_logits, axis=1)
    hits = (expert_ids[:, :, None] == jnp.arange(experts, dtype=jnp.int32)[None, None, :]).astype(
        jnp.float32
    )
    per_token = jnp.sum(hits, axis=1)
    earlier = (jnp.arange(tokens_here)[:, None] > jnp.arange(tokens_here)[None, :]).astype(
        jnp.float32
    )
    before = jnp.dot(earlier, per_token, precision=highest)
    rank = jnp.sum(hits * before[:, None, :], axis=2).astype(jnp.int32)
    target = expert_ids * capacity + rank
    placed = (
        target[None, :, :] == jnp.arange(experts * capacity, dtype=jnp.int32)[:, None, None]
    ).astype(jnp.float32)
    pick = jnp.sum(placed, axis=2).astype(jnp.bfloat16)
    send_rows = jnp.dot(pick, out_grad, preferred_element_type=jnp.float32).astype(jnp.bfloat16)
    send_weight = jnp.sum(placed * weights[None, :, :], axis=(1, 2)).astype(jnp.bfloat16)
    sent_rows, sent_weight = (
        lax.all_to_all(
            send_rows.reshape(experts, capacity, features),
            "seq",
            split_axis=0,
            concat_axis=0,
            tiled=True,
        ),
        lax.all_to_all(
            send_weight.reshape(experts, capacity), "seq", split_axis=0, concat_axis=0, tiled=True
        ),
    )
    slot_rows = sent_rows.reshape(slots_all, features)
    weight_here = w_down[0]
    raw = lax.psum_scatter(
        lax.dot_general(
            weight_here, slot_rows, (((1,), (1,)), ((), ())), preferred_element_type=jnp.float32
        ).astype(jnp.bfloat16),
        "head",
        scatter_dimension=0,
        tiled=True,
    ).astype(jnp.float32)
    gate = saved_gu[0, 0].astype(jnp.float32)
    up = saved_gu[0, 1].astype(jnp.float32)
    sig = jax.nn.sigmoid(gate)
    act = gate * sig
    hidden = act * up
    slot_part = jnp.sum(hidden * raw, axis=0)
    scaled = raw * sent_weight.reshape(slots_all).astype(jnp.float32)[None, :]
    gate_up_grad = jnp.stack([scaled * up * sig * (1.0 + gate * (1.0 - sig)), scaled * act])[
        None
    ].astype(jnp.bfloat16)
    slot_grad = lax.psum(slot_part, "head")
    returned = lax.all_to_all(
        slot_grad.reshape(seq_count, capacity), "seq", split_axis=0, concat_axis=0, tiled=True
    )
    route_grad = jnp.take(returned.reshape(-1), target.reshape(-1)).reshape(tokens_here, top_count)
    logit_grad = weights * (route_grad - jnp.sum(weights * route_grad, axis=1, keepdims=True))
    dense = jnp.einsum("tk,tke->te", logit_grad, hits, precision=highest)
    router_term = jnp.dot(dense, router.astype(jnp.float32), precision=highest)
    input_slice = (out_grad.astype(jnp.float32) + router_term).astype(jnp.bfloat16)
    input_grad = lax.all_gather(input_slice, "head", axis=1, tiled=True)
    attn_grad = lax.dot_general(
        input_grad,
        lax.all_gather(out_weight, "seq", axis=1, tiled=True),
        (((1,), (1,)), ((), ())),
        preferred_element_type=jnp.float32,
    ).astype(jnp.bfloat16)
    kv_heads = key.shape[1]
    head_dim = key.shape[2]
    group = query.shape[1] // kv_heads
    paired = jnp.stack([key, value])
    blocks = [paired]
    for distance in range(1, REACH + 1):
        blocks.append(passed_along(paired, "seq", distance))
    window = jnp.concatenate(blocks[::-1], axis=1)
    local_pos = jnp.arange(tokens_here, dtype=jnp.int32)
    key_pos = jnp.concatenate(
        [(seq_index - distance) * tokens_here + local_pos for distance in range(REACH, -1, -1)]
    )
    query_pos = seq_index * tokens_here + local_pos
    queries = query.reshape(tokens_here, kv_heads, group, head_dim)
    upstream = attn_grad.reshape(tokens_here, kv_heads, group, head_dim)
    query_part, key_part, value_part = attend(
        queries, upstream, window[0], window[1], query_pos, key_pos, doc_start, head_dim ** (-0.5)
    )
    query_grad = query_part.reshape(query.shape).astype(jnp.bfloat16)
    pieces = jnp.stack([key_part, value_part]).reshape(
        2, REACH + 1, tokens_here, kv_heads, head_dim
    )
    totals = pieces[:, REACH]
    for distance in range(1, REACH + 1):
        totals = totals + passed_along(
            pieces[:, REACH - distance].astype(jnp.bfloat16), "seq", -distance
        ).astype(jnp.float32)
    return (
        gate_up_grad,
        route_grad,
        query_grad,
        totals[0].astype(jnp.bfloat16),
        totals[1].astype(jnp.bfloat16),
    )


def solution(mesh):
    in_specs = (
        P("seq", "head"),
        P("seq", None),
        P("seq", None),
        P("seq"),
        P(None, "head"),
        P("seq", None, "head"),
        P("seq", None, "head", None),
        P("head", "seq"),
        P("seq", "head", None),
        P("seq", "head", None),
        P("seq", "head", None),
    )
    out_specs = (
        P("seq", None, "head", None),
        P("seq", None),
        P("seq", "head", None),
        P("seq", "head", None),
        P("seq", "head", None),
    )
    return jax.shard_map(
        per_device, mesh=mesh, in_specs=in_specs, out_specs=out_specs, check_vma=False
    )
```

profile of v0, /device:TPU:21, one launch (start us, length us, event | category | flops | bytes accessed | tf_op | source)
XLA Modules:
  0.0 433.5 jit_solution(12766835076325374561)
XLA Ops:
  11.8 11.6 %select_reduce_fusion = (bf16[1536]{0:T(1024)(128)(2,1)S(1)}, bf16[1536,128]{1,0:T(8,128)(2,1)S(1)}) fusion(f32[128,8]{0,1:T(8,128)S(1)} %fusion.47, s32[128,8]{0,1:T(8,128)S(1)} %convert_add_fusion), kind=kLoop, calls=%fused_computation.1 | loop fusion | flops 7666176 | bytes 404480 | tf_op jit(solution)/shard_map/reduce_sum | solution.py:82
  23.4 3.6 convolution_convert_fusion
  26.9 6.0 %reshape.372 = bf16[128,12,1024]{2,1,0:T(8,128)(2,1)} reshape(bf16[1536,1024]{1,0:T(8,128)(2,1)} %convolution_convert_fusion) | data formatting | bytes 6291456 | tf_op jit(solution)/shard_map/reshape | solution.py:85
  33.0 113.3 %all_to_all.20 = bf16[128,12,1024]{2,1,0:T(8,128)(2,1)} all-to-all(bf16[128,12,1024]{2,1,0:T(8,128)(2,1)} %reshape.372), channel_id=1, replica_groups=mesh['seq'=128,'head'=4] {'seq'}, dimensions={0} | all-to-all | bytes 6291456 | tf_op jit(solution)/shard_map/all_to_all | solution.py:84
  146.3 6.2 %reshape.373 = bf16[1536,1024]{1,0:T(8,128)(2,1)} reshape(bf16[128,12,1024]{2,1,0:T(8,128)(2,1)} %all_to_all.20) | data formatting | bytes 6291456 | tf_op jit(solution)/shard_map/reshape | solution.py:95
  152.5 6.0 %fusion.6 = bf16[768,1536]{0,1:T(8,128)(2,1)} fusion(bf16[1536,1024]{1,0:T(8,128)(2,1)} %reshape.373, bf16[1,768,1024]{2,1,0:T(8,128)(2,1)S(1)} %copy-done), kind=kOutput, calls=%fused_computation.16 | convolution fusion | flops 2417098752 | bytes 7077888 | tf_op jit(solution)/shard_map/dot_general | solution.py:98
  158.5 4.3 copy.125
  163.5 17.8 %all-to-all-start.1 = ((bf16[128,1,12]{2,1,0:T(2,128)(2,1)}), bf16[128,1,12]{2,1,0:T(2,128)(2,1)S(1)}, u32[]{:S(2)}, u32[]{:S(2)}) async-start(bf16[128,1,12]{2,1,0:T(2,128)(2,1)} %convert_element_type.271), calls=%async_computation.1 | async-start | bytes 131072 | tf_op jit(solution)/shard_map/all_to_all | solution.py:91
  185.4 5.7 %all-to-all-done.1 = bf16[128,1,12]{2,1,0:T(2,128)(2,1)S(1)} async-done(((bf16[128,1,12]{2,1,0:T(2,128)(2,1)}), bf16[128,1,12]{2,1,0:T(2,128)(2,1)S(1)}, u32[]{:S(2)}, u32[]{:S(2)}) %all-to-all-start.1) | async-done | bytes 3104 | tf_op jit(solution)/shard_map/all_to_all | solution.py:91
  191.4 11.6 %reduce-scatter.4.cloned.1.call-done = bf16[192,1536]{1,0:T(8,128)(2,1)} async-done(((bf16[768,1536]{1,0:T(8,128)(2,1)}), bf16[192,1536]{1,0:T(8,128)(2,1)}) %reduce-scatter.4.cloned.1.call-update) | async-done | bytes 589840
  205.2 3.5 fusion.10
  208.9 12.8 %psum.7 = f32[128,1,12]{2,0,1:T(8,128)} all-reduce(f32[128,1,12]{2,0,1:T(8,128)S(1)} %all_to_all.15), channel_id=1, replica_groups=mesh['seq'=128,'head'=4] {'head'}, use_global_device_ids=true, to_apply=%region_8.0 | all-reduce | flops 1536 | bytes 12288 | tf_op jit(solution)/shard_map/psum | solution.py:115
  221.6 18.2 %all-to-all-start.2 = ((f32[128,1,12]{2,1,0:T(1,128)}), f32[128,1,12]{2,1,0:T(1,128)S(1)}, u32[]{:S(2)}, u32[]{:S(2)}) async-start(f32[128,1,12]{2,1,0:T(1,128)} %bitcast.8), calls=%async_computation.2 | async-start | bytes 131072 | tf_op jit(solution)/shard_map/all_to_all | solution.py:116
  239.9 9.7 %all-to-all-done.2 = f32[128,1,12]{2,1,0:T(1,128)S(1)} async-done(((f32[128,1,12]{2,1,0:T(1,128)}), f32[128,1,12]{2,1,0:T(1,128)S(1)}, u32[]{:S(2)}, u32[]{:S(2)}) %all-to-all-start.2) | async-done | bytes 6176 | tf_op jit(solution)/shard_map/all_to_all | solution.py:116
  251.0 6.2 %gather_fusion = f32[1024]{0:T(1024)S(1)} fusion(f32[1536]{0:T(1024)S(1)} %reshape.374, s32[1024]{0:T(1024)S(1)} %broadcast_clamp_fusion), kind=kCustom, calls=%fused_computation | custom fusion | bytes 12288 | tf_op jit(solution)/shard_map/jit(_take)/gather | solution.py:119
  260.0 3.1 collective-permute-start
  263.2 4.6 %collective-permute-start.1 = (bf16[2,128,1,128]{3,1,2,0:T(8,128)(2,1)S(1)}, bf16[2,128,1,128]{3,1,2,0:T(8,128)(2,1)S(1)}, u32[]{:S(2)}, u32[]{:S(2)}) collective-permute-start(bf16[2,128,1,128]{3,1,2,0:T(8,128)(2,1)S(1)} %pad_maximum_fusion.2), channel_id=1, source_target_pairs={{0,24},{4,28},{8,32},{12,36},{16,40},{20,44},{24,48},{28,52},{32,5... | collective-permute-start | bytes 196616 | tf_op jit(solution)/shard_map/ppermute | solution.py:16
  267.8 4.5 %collective-permute-start.2 = (bf16[2,128,1,128]{3,1,2,0:T(8,128)(2,1)S(1)}, bf16[2,128,1,128]{3,1,2,0:T(8,128)(2,1)S(1)}, u32[]{:S(2)}, u32[]{:S(2)}) collective-permute-start(bf16[2,128,1,128]{3,1,2,0:T(8,128)(2,1)S(1)} %pad_maximum_fusion.2), channel_id=1, source_target_pairs={{0,20},{4,24},{8,28},{12,32},{16,36},{20,40},{24,44},{28,48},{32,5... | collective-permute-start | bytes 196616 | tf_op jit(solution)/shard_map/ppermute | solution.py:16
  274.5 3.7 collective-permute-start.4
  278.6 3.0 collective-permute-start.5
  281.6 2.5 collective-permute-start.6
  289.6 84.2 %all-gather.5.cloned.1.call-done = bf16[1024,4096]{0,1:T(8,128)(2,1)} async-done(((bf16[1024,32]{0,1:T(8,128)(2,1)}), bf16[1024,4096]{0,1:T(8,128)(2,1)}) %all-gather.5.cloned.1.call-update) | async-done | bytes 8388624 | tf_op jit(solution)/shard_map/all_gather | solution.py:127
  373.8 5.1 %convolution_convert_fusion.2 = bf16[128,1024]{1,0:T(8,128)(2,1)S(1)} fusion(bf16[128,4096]{1,0:T(8,128)(2,1)} %all-gather.3.cloned.1.call-done, bf16[1024,4096]{0,1:T(8,128)(2,1)} %all-gather.5.cloned.1.call-done), kind=kOutput, calls=%fused_computation.46 | convolution fusion | flops 1073872896 | bytes 9699328 | tf_op jit(solution)/shard_map/dot_general | solution.py:125
  380.3 3.4 convert_bitcast_fusion
  383.8 4.2 copy.113
  390.3 2.5 fusion.19
  393.6 3.9 collective-permute-start.13
  397.5 4.5 %collective-permute-start.12 = (bf16[2,128,1,128]{3,1,0,2:T(8,128)(2,1)S(1)}, bf16[2,128,1,128]{3,1,0,2:T(8,128)(2,1)}, u32[]{:S(2)}, u32[]{:S(2)}) collective-permute-start(bf16[2,128,1,128]{3,1,0,2:T(8,128)(2,1)S(1)} %get-tuple-element.43), channel_id=1, source_target_pairs={{24,0},{28,4},{32,8},{36,12},{40,16},{44,20},{48,24},{52,28},{56,3... | collective-permute-start | bytes 196616 | tf_op jit(solution)/shard_map/ppermute | solution.py:16
  405.2 4.8 %collective-permute-start.11 = (bf16[2,128,1,128]{3,1,0,2:T(8,128)(2,1)S(1)}, bf16[2,128,1,128]{3,1,0,2:T(8,128)(2,1)S(1)}, u32[]{:S(2)}, u32[]{:S(2)}) collective-permute-start(bf16[2,128,1,128]{3,1,0,2:T(8,128)(2,1)S(1)} %get-tuple-element.44), channel_id=1, source_target_pairs={{20,0},{24,4},{28,8},{32,12},{36,16},{40,20},{44,24},{48,28},{52,3... | collective-permute-start | bytes 196616 | tf_op jit(solution)/shard_map/ppermute | solution.py:16
  410.0 3.0 collective-permute-start.10
  413.0 3.3 collective-permute-start.9
  416.4 3.3 collective-permute-start.8
  (115 shorter events, 38.9 us)
Async XLA Ops:
  7.2 145.3 %copy-start = (bf16[1,768,1024]{2,1,0:T(8,128)(2,1)S(1)}, bf16[1,768,1024]{2,1,0:T(8,128)(2,1)}, u32[]{:S(2)}) copy-start(bf16[1,768,1024]{2,1,0:T(8,128)(2,1)} %param.16) | copy-start | bytes 4718596
  7.2 195.8 %reduce-scatter.4.cloned.1.call-start = ((), (), s32[]{:S(2)}) async-start(), calls=%async_computation.6 | async-start | bytes 2949120
  163.5 27.6 %all-to-all-start.1 = ((bf16[128,1,12]{2,1,0:T(2,128)(2,1)}), bf16[128,1,12]{2,1,0:T(2,128)(2,1)S(1)}, u32[]{:S(2)}, u32[]{:S(2)}) async-start(bf16[128,1,12]{2,1,0:T(2,128)(2,1)} %convert_element_type.271), calls=%async_computation.1 | async-start | bytes 131072 | tf_op jit(solution)/shard_map/all_to_all | solution.py:91
  205.2 52.1 %copy-start.11 = (f32[128,8]{0,1:T(8,128)S(1)}, f32[128,8]{0,1:T(8,128)}, u32[]{:S(2)}) copy-start(f32[128,8]{0,1:T(8,128)} %param.13) | copy-start | bytes 12292
  205.2 52.9 %copy-start.6 = (bf16[128,1024]{1,0:T(8,128)(2,1)S(1)}, bf16[128,1024]{1,0:T(8,128)(2,1)}, u32[]{:S(2)}) copy-start(bf16[128,1024]{1,0:T(8,128)(2,1)} %param.11) | copy-start | bytes 786436
  208.7 49.4 %copy-start.8 = (bf16[128,1024]{1,0:T(8,128)(2,1)S(1)}, bf16[128,1024]{1,0:T(8,128)(2,1)}, u32[]{:S(2)}) copy-start(bf16[128,1024]{1,0:T(8,128)(2,1)} %param.15) | copy-start | bytes 786436
  208.7 51.2 %copy-start.9 = (bf16[128,1,128]{2,0,1:T(8,128)(2,1)S(1)}, bf16[128,1,128]{2,0,1:T(8,128)(2,1)}, u32[]{:S(2)}) copy-start(bf16[128,1,128]{2,0,1:T(8,128)(2,1)} %param.21) | copy-start | bytes 98308
  208.7 51.3 %copy-start.10 = (bf16[128,1,128]{2,0,1:T(8,128)(2,1)S(1)}, bf16[128,1,128]{2,0,1:T(8,128)(2,1)}, u32[]{:S(2)}) copy-start(bf16[128,1,128]{2,0,1:T(8,128)(2,1)} %param.20) | copy-start | bytes 98308
  208.7 69.7 %copy-start.13 = (s32[128]{0:T(128)S(1)}, s32[128]{0:T(128)}, u32[]{:S(2)}) copy-start(s32[128]{0:T(128)} %param.14) | copy-start | bytes 1540
  221.6 64.3 %copy-start.5 = (bf16[128,8,128]{2,1,0:T(8,128)(2,1)S(1)}, bf16[128,8,128]{2,1,0:T(8,128)(2,1)}, u32[]{:S(2)}) copy-start(bf16[128,8,128]{2,1,0:T(8,128)(2,1)} %param.19) | copy-start | bytes 786436
  221.6 27.9 %all-to-all-start.2 = ((f32[128,1,12]{2,1,0:T(1,128)}), f32[128,1,12]{2,1,0:T(1,128)S(1)}, u32[]{:S(2)}, u32[]{:S(2)}) async-start(f32[128,1,12]{2,1,0:T(1,128)} %bitcast.8), calls=%async_computation.2 | async-start | bytes 131072 | tf_op jit(solution)/shard_map/all_to_all | solution.py:116
  239.8 49.8 %all-gather.3.cloned.1.call-start = ((), (), s32[]{:S(2)}) async-start(), calls=%async_computation.4 | async-start | bytes 1310720 | tf_op jit(solution)/shard_map/all_gather | solution.py:124
  257.4 29.4 %copy-start.12 = (f32[128,8]{0,1:T(8,128)}, f32[128,8]{0,1:T(8,128)S(1)}, u32[]{:S(2)}) copy-start(f32[128,8]{0,1:T(8,128)S(1)} %get-tuple-element.33) | copy-start | bytes 12292
  259.2 114.6 %all-gather.5.cloned.1.call-start = ((), (), s32[]{:S(2)}) async-start(), calls=%async_computation.5 | async-start | bytes 8454144 | tf_op jit(solution)/shard_map/all_gather | solution.py:127
  260.0 18.6 %collective-permute-start = (bf16[2,128,1,128]{3,1,2,0:T(8,128)(2,1)S(1)}, bf16[2,128,1,128]{3,1,2,0:T(8,128)(2,1)S(1)}, u32[]{:S(2)}, u32[]{:S(2)}) collective-permute-start(bf16[2,128,1,128]{3,1,2,0:T(8,128)(2,1)S(1)} %pad_maximum_fusion.2), channel_id=1, source_target_pairs={{0,28},{4,32},{8,36},{12,40},{16,44},{20,48},{24,52},{28,56},{32,6... | collective-permute-start | bytes 196616 | tf_op jit(solution)/shard_map/ppermute | solution.py:16
  263.2 18.4 %collective-permute-start.1 = (bf16[2,128,1,128]{3,1,2,0:T(8,128)(2,1)S(1)}, bf16[2,128,1,128]{3,1,2,0:T(8,128)(2,1)S(1)}, u32[]{:S(2)}, u32[]{:S(2)}) collective-permute-start(bf16[2,128,1,128]{3,1,2,0:T(8,128)(2,1)S(1)} %pad_maximum_fusion.2), channel_id=1, source_target_pairs={{0,24},{4,28},{8,32},{12,36},{16,40},{20,44},{24,48},{28,52},{32,5... | collective-permute-start | bytes 196616 | tf_op jit(solution)/shard_map/ppermute | solution.py:16
  267.8 16.3 %collective-permute-start.2 = (bf16[2,128,1,128]{3,1,2,0:T(8,128)(2,1)S(1)}, bf16[2,128,1,128]{3,1,2,0:T(8,128)(2,1)S(1)}, u32[]{:S(2)}, u32[]{:S(2)}) collective-permute-start(bf16[2,128,1,128]{3,1,2,0:T(8,128)(2,1)S(1)} %pad_maximum_fusion.2), channel_id=1, source_target_pairs={{0,20},{4,24},{8,28},{12,32},{16,36},{20,40},{24,44},{28,48},{32,5... | collective-permute-start | bytes 196616 | tf_op jit(solution)/shard_map/ppermute | solution.py:16
  272.3 11.9 %collective-permute-start.3 = (bf16[2,128,1,128]{3,1,2,0:T(8,128)(2,1)S(1)}, bf16[2,128,1,128]{3,1,2,0:T(8,128)(2,1)S(1)}, u32[]{:S(2)}, u32[]{:S(2)}) collective-permute-start(bf16[2,128,1,128]{3,1,2,0:T(8,128)(2,1)S(1)} %pad_maximum_fusion.2), channel_id=1, source_target_pairs={{0,16},{4,20},{8,24},{12,28},{16,32},{20,36},{24,40},{28,44},{32,4... | collective-permute-start | bytes 196616 | tf_op jit(solution)/shard_map/ppermute | solution.py:16
  274.5 9.7 %collective-permute-start.4 = (bf16[2,128,1,128]{3,1,2,0:T(8,128)(2,1)S(1)}, bf16[2,128,1,128]{3,1,2,0:T(8,128)(2,1)S(1)}, u32[]{:S(2)}, u32[]{:S(2)}) collective-permute-start(bf16[2,128,1,128]{3,1,2,0:T(8,128)(2,1)S(1)} %pad_maximum_fusion.2), channel_id=1, source_target_pairs={{0,12},{4,16},{8,20},{12,24},{16,28},{20,32},{24,36},{28,40},{32,4... | collective-permute-start | bytes 196616 | tf_op jit(solution)/shard_map/ppermute | solution.py:16
  278.6 7.3 %collective-permute-start.5 = (bf16[2,128,1,128]{3,1,2,0:T(8,128)(2,1)S(1)}, bf16[2,128,1,128]{3,1,2,0:T(8,128)(2,1)S(1)}, u32[]{:S(2)}, u32[]{:S(2)}) collective-permute-start(bf16[2,128,1,128]{3,1,2,0:T(8,128)(2,1)S(1)} %pad_maximum_fusion.2), channel_id=1, source_target_pairs={{0,8},{4,12},{8,16},{12,20},{16,24},{20,28},{24,32},{28,36},{32,40... | collective-permute-start | bytes 196616 | tf_op jit(solution)/shard_map/ppermute | solution.py:16
  281.6 4.3 collective-permute-start.6
  286.0 93.0 %copy-start.7 = (bf16[2,1024,1,128]{3,1,2,0:T(8,128)(2,1)}, bf16[2,1024,1,128]{3,1,2,0:T(8,128)(2,1)S(1)}, u32[]{:S(2)}) copy-start(bf16[2,1024,1,128]{3,1,2,0:T(8,128)(2,1)S(1)} %constant_dynamic-update-slice_fusion) | copy-start | bytes 1572868
  373.8 5.1 %copy-start.2 = (f32[1024,128,8]{1,0,2:T(8,128)S(1)}, f32[1024,128,8]{1,0,2:T(8,128)}, u32[]{:S(2)}) copy-start(f32[1024,128,8]{1,0,2:T(8,128)} %copy-done.1) | copy-start | bytes 12582916
  390.3 11.8 %copy-start.3 = (f32[1024,1,128]{2,0,1:T(8,128)}, f32[1024,1,128]{2,0,1:T(8,128)S(1)}, u32[]{:S(2)}) copy-start(f32[1024,1,128]{2,0,1:T(8,128)S(1)} %copy.124) | copy-start | bytes 1572868
  392.8 9.3 %copy-start.4 = (f32[1024,128]{1,0:T(8,128)}, f32[1024,128]{1,0:T(8,128)S(1)}, u32[]{:S(2)}) copy-start(f32[1024,128]{1,0:T(8,128)S(1)} %fusion.19) | copy-start | bytes 1572868
  393.6 22.8 %collective-permute-start.13 = (bf16[2,128,1,128]{3,1,2,0:T(8,128)(2,1)}, bf16[2,128,1,128]{3,1,2,0:T(8,128)(2,1)}, u32[]{:S(2)}, u32[]{:S(2)}) collective-permute-start(bf16[2,128,1,128]{3,1,2,0:T(8,128)(2,1)} %get-tuple-element.42), channel_id=1, source_target_pairs={{28,0},{32,4},{36,8},{40,12},{44,16},{48,20},{52,24},{56,28},{60,3... | collective-permute-start | bytes 196616 | tf_op jit(solution)/shard_map/ppermute | solution.py:16
  397.5 22.2 %collective-permute-start.12 = (bf16[2,128,1,128]{3,1,0,2:T(8,128)(2,1)S(1)}, bf16[2,128,1,128]{3,1,0,2:T(8,128)(2,1)}, u32[]{:S(2)}, u32[]{:S(2)}) collective-permute-start(bf16[2,128,1,128]{3,1,0,2:T(8,128)(2,1)S(1)} %get-tuple-element.43), channel_id=1, source_target_pairs={{24,0},{28,4},{32,8},{36,12},{40,16},{44,20},{48,24},{52,28},{56,3... | collective-permute-start | bytes 196616 | tf_op jit(solution)/shard_map/ppermute | solution.py:16
  405.2 20.0 %collective-permute-start.11 = (bf16[2,128,1,128]{3,1,0,2:T(8,128)(2,1)S(1)}, bf16[2,128,1,128]{3,1,0,2:T(8,128)(2,1)S(1)}, u32[]{:S(2)}, u32[]{:S(2)}) collective-permute-start(bf16[2,128,1,128]{3,1,0,2:T(8,128)(2,1)S(1)} %get-tuple-element.44), channel_id=1, source_target_pairs={{20,0},{24,4},{28,8},{32,12},{36,16},{40,20},{44,24},{48,28},{52,3... | collective-permute-start | bytes 196616 | tf_op jit(solution)/shard_map/ppermute | solution.py:16
  410.0 15.2 %collective-permute-start.10 = (bf16[2,128,1,128]{3,1,0,2:T(8,128)(2,1)S(1)}, bf16[2,128,1,128]{3,1,0,2:T(8,128)(2,1)S(1)}, u32[]{:S(2)}, u32[]{:S(2)}) collective-permute-start(bf16[2,128,1,128]{3,1,0,2:T(8,128)(2,1)S(1)} %get-tuple-element.45), channel_id=1, source_target_pairs={{16,0},{20,4},{24,8},{28,12},{32,16},{36,20},{40,24},{44,28},{48,3... | collective-permute-start | bytes 196616 | tf_op jit(solution)/shard_map/ppermute | solution.py:16
  413.0 12.2 %collective-permute-start.9 = (bf16[2,128,1,128]{3,1,0,2:T(8,128)(2,1)S(1)}, bf16[2,128,1,128]{3,1,0,2:T(8,128)(2,1)S(1)}, u32[]{:S(2)}, u32[]{:S(2)}) collective-permute-start(bf16[2,128,1,128]{3,1,0,2:T(8,128)(2,1)S(1)} %get-tuple-element.46), channel_id=1, source_target_pairs={{12,0},{16,4},{20,8},{24,12},{28,16},{32,20},{36,24},{40,28},{44,3... | collective-permute-start | bytes 196616 | tf_op jit(solution)/shard_map/ppermute | solution.py:16
  416.4 8.8 %collective-permute-start.8 = (bf16[2,128,1,128]{3,1,0,2:T(8,128)(2,1)S(1)}, bf16[2,128,1,128]{3,1,0,2:T(8,128)(2,1)S(1)}, u32[]{:S(2)}, u32[]{:S(2)}) collective-permute-start(bf16[2,128,1,128]{3,1,0,2:T(8,128)(2,1)S(1)} %get-tuple-element.47), channel_id=1, source_target_pairs={{8,0},{12,4},{16,8},{20,12},{24,16},{28,20},{32,24},{36,28},{40,32... | collective-permute-start | bytes 196616 | tf_op jit(solution)/shard_map/ppermute | solution.py:16
  419.7 5.6 %collective-permute-start.7 = (bf16[2,128,1,128]{3,1,0,2:T(8,128)(2,1)S(1)}, bf16[2,128,1,128]{3,1,0,2:T(8,128)(2,1)S(1)}, u32[]{:S(2)}, u32[]{:S(2)}) collective-permute-start(bf16[2,128,1,128]{3,1,0,2:T(8,128)(2,1)S(1)} %get-tuple-element.41), channel_id=1, source_target_pairs={{4,0},{8,4},{12,8},{16,12},{20,16},{24,20},{28,24},{32,28},{36,32}... | collective-permute-start | bytes 196616 | tf_op jit(solution)/shard_map/ppermute | solution.py:16
  (1 other events, 2.0 us)
Sparse Core Ops, SparseCore 0:
  162.9 40.0 reduce-scatter.3
  259.4 20.7 all-gather.2
  283.3 90.4 all-gather.4
where the time goes:
time: 436 us; the launch traced here: 433 us
  blocking collectives  126 us (29%)
  waiting for transfers between devices  114 us (26%)
  starting transfers between devices  85.1 us (20%)
  local copies, waits for them, and re-layouts  41.9 us (10%)
  other arithmetic  27 us (6%)
  matrix products  25.3 us (6%)
  between operations  14.4 us (3%)
    all_to_all x1, blocking collectives, per_device(): lax.all_to_all(send_rows.reshape(experts, capacity, features), 'seq', spl...  113 us
    all_gather x1, waiting for transfers between devices, per_device(): lax.all_gather(out_weight, 'seq', axis=1, tiled=True)  84.2 us
    ppermute x14, starting transfers between devices, passed_along(): return lax.ppermute(array, axis, pairs)  49 us
    all_to_all x1, starting transfers between devices, per_device(): lax.all_to_all(slot_grad.reshape(seq_count, capacity), 'seq', split_axis=...  18.2 us
    all_to_all x1, starting transfers between devices, per_device(): lax.all_to_all(send_weight.reshape(experts, capacity), 'seq', split_axis=...  17.8 us
    unnamed x43, local copies, waits for them, and re-layouts  13.4 us
    psum x1, blocking collectives, per_device(): slot_grad = lax.psum(slot_part, 'head')  12.8 us
    unnamed x4, waiting for transfers between devices  12.3 us
  transfers between devices with their start and end apart: 19, of which 5 were waited for; matrix products, arithmetic and copies ran while one was open for 3% of the time, Pallas kernels for 0%

commit v1 on v0

--- a/solution.py
+++ b/solution.py
@@ -80,19 +80,28 @@
     pick = jnp.sum(placed, axis=2).astype(jnp.bfloat16)
     send_rows = jnp.dot(pick, out_grad, preferred_element_type=jnp.float32).astype(jnp.bfloat16)
     send_weight = jnp.sum(placed * weights[None, :, :], axis=(1, 2)).astype(jnp.bfloat16)
-    sent_rows, sent_weight = (
-        lax.all_to_all(
-            send_rows.reshape(experts, capacity, features),
-            "seq",
-            split_axis=0,
-            concat_axis=0,
-            tiled=True,
-        ),
-        lax.all_to_all(
-            send_weight.reshape(experts, capacity), "seq", split_axis=0, concat_axis=0, tiled=True
-        ),
+    weight_lanes = jnp.zeros((experts * capacity, 128), jnp.bfloat16).at[:, 0].set(send_weight)
+    payload = jnp.concatenate([send_rows, weight_lanes], axis=1)
+    weight_full = lax.all_gather(out_weight, "seq", axis=1, tiled=True)
+    kv_heads = key.shape[1]
+    head_dim = key.shape[2]
+    group = query.shape[1] // kv_heads
+    paired = jnp.stack([key, value])
+    blocks = [paired]
+    for distance in range(1, REACH + 1):
+        blocks.append(passed_along(paired, "seq", distance))
+    sent_payload = lax.all_to_all(
+        payload.reshape(experts, capacity, features + 128),
+        "seq",
+        split_axis=0,
+        concat_axis=0,
+        tiled=True,
+    ).reshape(slots_all, features + 128)
+    sent_payload, weight_full, blocks = lax.optimization_barrier(
+        (sent_payload, weight_full, tuple(blocks))
     )
-    slot_rows = sent_rows.reshape(slots_all, features)
+    slot_rows = sent_payload[:, :features]
+    sent_weight = sent_payload[:, features]
     weight_here = w_down[0]
     raw = lax.psum_scatter(
         lax.dot_general(
@@ -124,17 +133,10 @@
     input_grad = lax.all_gather(input_slice, "head", axis=1, tiled=True)
     attn_grad = lax.dot_general(
         input_grad,
-        lax.all_gather(out_weight, "seq", axis=1, tiled=True),
+        weight_full,
         (((1,), (1,)), ((), ())),
         preferred_element_type=jnp.float32,
     ).astype(jnp.bfloat16)
-    kv_heads = key.shape[1]
-    head_dim = key.shape[2]
-    group = query.shape[1] // kv_heads
-    paired = jnp.stack([key, value])
-    blocks = [paired]
-    for distance in range(1, REACH + 1):
-        blocks.append(passed_along(paired, "seq", distance))
     window = jnp.concatenate(blocks[::-1], axis=1)
     local_pos = jnp.arange(tokens_here, dtype=jnp.int32)
     key_pos = jnp.concatenate(

time: 436 us -> 406 us (0.931)
  the two profiles are of different devices: /device:TPU:21 before, /device:TPU:49 now
where the time goes in v1:
time: 406 us; the launch traced here: 404 us
  waiting for transfers between devices  167 us (41%)
  starting transfers between devices  112 us (28%)
  local copies, waits for them, and re-layouts  44.5 us (11%)
  other arithmetic  29.2 us (7%)
  matrix products  23.8 us (6%)
  between operations  14.7 us (4%)
  blocking collectives  12.9 us (3%)
    ppermute x14, waiting for transfers between devices, passed_along(): return lax.ppermute(array, axis, pairs)  101 us
    ppermute x14, starting transfers between devices, passed_along(): return lax.ppermute(array, axis, pairs)  75.1 us
    unnamed x4, waiting for transfers between devices  30.9 us
    all_to_all x1, starting transfers between devices, per_device(): lax.all_to_all(slot_grad.reshape(seq_count, capacity), 'seq', split_axis=...  18.4 us
    all_to_all x1, starting transfers between devices, per_device(): lax.all_to_all(payload.reshape(experts, capacity, features + 128), 'seq',...  18.2 us
    all_gather x1, waiting for transfers between devices, per_device(): input_grad = lax.all_gather(input_slice, 'head', axis=1, tiled=True)  17.6 us
    psum x1, blocking collectives, per_device(): slot_grad = lax.psum(slot_part, 'head')  12.9 us
    unnamed x77, local copies, waits for them, and re-layouts  12.3 us
  transfers between devices with their start and end apart: 19, of which 7 were waited for; matrix products, arithmetic and copies ran while one was open for 12% of the time, Pallas kernels for 0%

profile of v1, /device:TPU:49, one launch (start us, length us, event | category | flops | bytes accessed | tf_op | source)
XLA Modules:
  0.0 403.8 jit_solution(11382594335718541829)
XLA Ops:
  13.0 11.6 %convert_reduce_fusion = (bf16[1536,128]{1,0:T(8,128)(2,1)S(1)}, bf16[1536]{0:T(1024)(128)(2,1)S(1)}) fusion(s32[128,8]{0,1:T(8,128)S(1)} %convert_add_fusion, f32[128,8]{0,1:T(8,128)S(1)} %fusion.52), kind=kLoop, calls=%fused_computation.4 | loop fusion | flops 7666176 | bytes 404480 | tf_op jit(solution)/shard_map/reduce_sum | solution.py:80
  29.2 5.8 %copy.124 = bf16[1536,1152]{1,0:T(8,128)(2,1)} copy(bf16[1536,1152]{0,1:T(8,128)(2,1)} %fusion.6) | data formatting | bytes 7077888 | tf_op jit(solution)/shard_map/concatenate | solution.py:84
  35.1 6.5 %reshape.395 = bf16[128,12,1152]{2,1,0:T(8,128)(2,1)} reshape(bf16[1536,1152]{1,0:T(8,128)(2,1)} %copy.124) | data formatting | bytes 7077888 | tf_op jit(solution)/shard_map/reshape | solution.py:94
  41.6 18.2 %all-to-all-start = ((bf16[128,12,1152]{2,1,0:T(8,128)(2,1)}), bf16[128,12,1152]{2,1,0:T(8,128)(2,1)}, u32[]{:S(2)}, u32[]{:S(2)}) async-start(bf16[128,12,1152]{2,1,0:T(8,128)(2,1)} %reshape.395), calls=%async_computation | async-start | bytes 9437184 | tf_op jit(solution)/shard_map/all_to_all | solution.py:93
  59.8 3.4 collective-permute-start
  63.2 3.1 collective-permute-start.1
  66.3 3.2 collective-permute-start.2
  69.6 4.3 %collective-permute-start.3 = (bf16[2,128,1,128]{3,1,2,0:T(8,128)(2,1)S(1)}, bf16[2,128,1,128]{3,1,2,0:T(8,128)(2,1)S(1)}, u32[]{:S(2)}, u32[]{:S(2)}) collective-permute-start(bf16[2,128,1,128]{3,1,2,0:T(8,128)(2,1)S(1)} %pad_maximum_fusion.2), channel_id=1, source_target_pairs={{0,16},{4,20},{8,24},{12,28},{16,32},{20,36},{24,40},{28,44},{32,4... | collective-permute-start | bytes 196616 | tf_op jit(solution)/shard_map/ppermute | solution.py:16
  73.9 2.6 collective-permute-start.4
  76.6 96.6 %collective-permute-done = bf16[2,128,1,128]{3,1,2,0:T(8,128)(2,1)S(1)} collective-permute-done((bf16[2,128,1,128]{3,1,2,0:T(8,128)(2,1)S(1)}, bf16[2,128,1,128]{3,1,2,0:T(8,128)(2,1)S(1)}, u32[]{:S(2)}, u32[]{:S(2)}) %collective-permute-start) | collective-permute-done | bytes 65568 | tf_op jit(solution)/shard_map/ppermute | solution.py:16
  177.7 27.2 %collective-permute-start.6 = (bf16[2,128,1,128]{3,1,2,0:T(8,128)(2,1)S(1)}, bf16[2,128,1,128]{3,1,2,0:T(8,128)(2,1)S(1)}, u32[]{:S(2)}, u32[]{:S(2)}) collective-permute-start(bf16[2,128,1,128]{3,1,2,0:T(8,128)(2,1)S(1)} %pad_maximum_fusion.2), channel_id=1, source_target_pairs={{0,28},{4,32},{8,36},{12,40},{16,44},{20,48},{24,52},{28,56},{32,6... | collective-permute-start | bytes 196616 | tf_op jit(solution)/shard_map/ppermute | solution.py:16
  204.9 6.7 %reshape.396 = bf16[1536,1152]{1,0:T(8,128)(2,1)} reshape(bf16[128,12,1152]{2,1,0:T(8,128)(2,1)} %all-to-all-done) | data formatting | bytes 7077888 | tf_op jit(solution)/shard_map/reshape | solution.py:99
  211.7 9.7 %all-gather.3.cloned.1.call-done = bf16[1024,4096]{0,1:T(8,128)(2,1)} async-done(((bf16[1024,32]{0,1:T(8,128)(2,1)}), bf16[1024,4096]{0,1:T(8,128)(2,1)}) %all-gather.3.cloned.1.call-update) | async-done | bytes 8388624 | tf_op jit(solution)/shard_map/all_gather | solution.py:85
  221.5 6.0 %fusion.9 = bf16[768,1536]{0,1:T(8,128)(2,1)} fusion(bf16[1536,1152]{1,0:T(8,128)(2,1)} %reshape.396, bf16[1,768,1024]{2,1,0:T(8,128)(2,1)S(1)} %copy-done), kind=kOutput, calls=%fused_computation.20 | convolution fusion | flops 2417098752 | bytes 7077888 | tf_op jit(solution)/shard_map/dot_general | solution.py:107
  227.6 4.4 %copy.147 = bf16[768,1536]{1,0:T(8,128)(2,1)} copy(bf16[768,1536]{0,1:T(8,128)(2,1)} %fusion.9) | data formatting | bytes 4718592
  235.0 30.1 %reduce-scatter.4.cloned.1.call-done = bf16[192,1536]{1,0:T(8,128)(2,1)} async-done(((bf16[768,1536]{1,0:T(8,128)(2,1)}), bf16[192,1536]{1,0:T(8,128)(2,1)}) %reduce-scatter.4.cloned.1.call-update) | async-done | bytes 589840
  266.5 2.3 fusion.15
  268.9 12.9 %psum.7 = f32[128,1,12]{2,0,1:T(8,128)} all-reduce(f32[128,1,12]{2,0,1:T(8,128)S(1)} %all_to_all.10), channel_id=1, replica_groups=mesh['seq'=128,'head'=4] {'head'}, use_global_device_ids=true, to_apply=%region_9.0 | all-reduce | flops 1536 | bytes 12288 | tf_op jit(solution)/shard_map/psum | solution.py:124
  281.9 18.4 %all-to-all-start.1 = ((f32[128,1,12]{2,1,0:T(1,128)}), f32[128,1,12]{2,1,0:T(1,128)S(1)}, u32[]{:S(2)}, u32[]{:S(2)}) async-start(f32[128,1,12]{2,1,0:T(1,128)} %bitcast.10), calls=%async_computation.1 | async-start | bytes 131072 | tf_op jit(solution)/shard_map/all_to_all | solution.py:125
  300.6 7.9 %all-to-all-done.1 = f32[128,1,12]{2,1,0:T(1,128)S(1)} async-done(((f32[128,1,12]{2,1,0:T(1,128)}), f32[128,1,12]{2,1,0:T(1,128)S(1)}, u32[]{:S(2)}, u32[]{:S(2)}) %all-to-all-start.1) | async-done | bytes 6176 | tf_op jit(solution)/shard_map/all_to_all | solution.py:125
  310.0 6.2 %gather_fusion = f32[1024]{0:T(1024)S(1)} fusion(f32[1536]{0:T(1024)S(1)} %reshape.397, s32[1024]{0:T(1024)S(1)} %broadcast_clamp_fusion), kind=kCustom, calls=%fused_computation | custom fusion | bytes 12288 | tf_op jit(solution)/shard_map/jit(_take)/gather | solution.py:128
  322.1 17.6 %all-gather.5.cloned.1.call-done = bf16[128,4096]{1,0:T(8,128)(2,1)} async-done(((bf16[128,1024]{1,0:T(8,128)(2,1)}), bf16[128,4096]{1,0:T(8,128)(2,1)}) %all-gather.5.cloned.1.call-update) | async-done | bytes 1048592 | tf_op jit(solution)/shard_map/all_gather | solution.py:133
  339.7 5.1 %convolution_convert_fusion.2 = bf16[128,1024]{1,0:T(8,128)(2,1)S(1)} fusion(bf16[128,4096]{1,0:T(8,128)(2,1)} %all-gather.5.cloned.1.call-done, bf16[1024,4096]{0,1:T(8,128)(2,1)} %all-gather.3.cloned.1.call-done), kind=kOutput, calls=%fused_computation.50 | convolution fusion | flops 1073872896 | bytes 9699328 | tf_op jit(solution)/shard_map/dot_general | solution.py:134
  346.1 3.4 convert_bitcast_fusion
  349.6 4.2 %copy.135 = bf16[8,128,1024]{2,0,1:T(8,128)(2,1)} copy(bf16[8,128,1024]{1,2,0:T(8,128)(2,1)} %get-tuple-element.71) | data formatting | bytes 4194304 | tf_op jit(solution)/shard_map/reshape.58
  356.2 2.5 fusion.24
  359.5 7.2 %collective-permute-start.10 = (bf16[2,128,1,128]{3,1,0,2:T(8,128)(2,1)}, bf16[2,128,1,128]{3,1,0,2:T(8,128)(2,1)}, u32[]{:S(2)}, u32[]{:S(2)}) collective-permute-start(bf16[2,128,1,128]{3,1,0,2:T(8,128)(2,1)} %get-tuple-element.82), channel_id=1, source_target_pairs={{16,0},{20,4},{24,8},{28,12},{32,16},{36,20},{40,24},{44,28},{48,3... | collective-permute-start | bytes 196616 | tf_op jit(solution)/shard_map/ppermute | solution.py:16
  366.7 5.4 %collective-permute-start.11 = (bf16[2,128,1,128]{3,1,0,2:T(8,128)(2,1)S(1)}, bf16[2,128,1,128]{3,1,0,2:T(8,128)(2,1)}, u32[]{:S(2)}, u32[]{:S(2)}) collective-permute-start(bf16[2,128,1,128]{3,1,0,2:T(8,128)(2,1)S(1)} %get-tuple-element.81), channel_id=1, source_target_pairs={{20,0},{24,4},{28,8},{32,12},{36,16},{40,20},{44,24},{48,28},{52,3... | collective-permute-start | bytes 196616 | tf_op jit(solution)/shard_map/ppermute | solution.py:16
  375.8 6.2 %collective-permute-start.13 = (bf16[2,128,1,128]{3,1,2,0:T(8,128)(2,1)S(1)}, bf16[2,128,1,128]{3,1,2,0:T(8,128)(2,1)S(1)}, u32[]{:S(2)}, u32[]{:S(2)}) collective-permute-start(bf16[2,128,1,128]{3,1,2,0:T(8,128)(2,1)S(1)} %get-tuple-element.79), channel_id=1, source_target_pairs={{28,0},{32,4},{36,8},{40,12},{44,16},{48,20},{52,24},{56,28},{60,3... | collective-permute-start | bytes 196616 | tf_op jit(solution)/shard_map/ppermute | solution.py:16
  382.0 3.5 collective-permute-start.7
  385.5 2.9 collective-permute-start.8
  388.5 2.2 collective-permute-start.9
  (151 shorter events, 41.5 us)
Async XLA Ops:
  7.2 214.3 %copy-start = (bf16[1,768,1024]{2,1,0:T(8,128)(2,1)S(1)}, bf16[1,768,1024]{2,1,0:T(8,128)(2,1)}, u32[]{:S(2)}) copy-start(bf16[1,768,1024]{2,1,0:T(8,128)(2,1)} %param.18) | copy-start | bytes 4718596
  7.2 214.3 %all-gather.3.cloned.1.call-start = ((), (), s32[]{:S(2)}) async-start(), calls=%async_computation.3 | async-start | bytes 8454144 | tf_op jit(solution)/shard_map/all_gather | solution.py:85
  41.6 18.2 %copy-start.28 = (bf16[128,1,128]{2,0,1:T(8,128)(2,1)S(1)}, bf16[128,1,128]{2,0,1:T(8,128)(2,1)}, u32[]{:S(2)}) copy-start(bf16[128,1,128]{2,0,1:T(8,128)(2,1)} %param.23) | copy-start | bytes 98308
  41.6 18.3 %copy-start.29 = (bf16[128,1,128]{2,0,1:T(8,128)(2,1)S(1)}, bf16[128,1,128]{2,0,1:T(8,128)(2,1)}, u32[]{:S(2)}) copy-start(bf16[128,1,128]{2,0,1:T(8,128)(2,1)} %param.22) | copy-start | bytes 98308
  41.6 163.4 %all-to-all-start = ((bf16[128,12,1152]{2,1,0:T(8,128)(2,1)}), bf16[128,12,1152]{2,1,0:T(8,128)(2,1)}, u32[]{:S(2)}, u32[]{:S(2)}) async-start(bf16[128,12,1152]{2,1,0:T(8,128)(2,1)} %reshape.395), calls=%async_computation | async-start | bytes 9437184 | tf_op jit(solution)/shard_map/all_to_all | solution.py:93
  59.7 205.4 %reduce-scatter.4.cloned.1.call-start = ((), (), s32[]{:S(2)}) async-start(), calls=%async_computation.5 | async-start | bytes 2949120
  59.8 113.4 %collective-permute-start = (bf16[2,128,1,128]{3,1,2,0:T(8,128)(2,1)S(1)}, bf16[2,128,1,128]{3,1,2,0:T(8,128)(2,1)S(1)}, u32[]{:S(2)}, u32[]{:S(2)}) collective-permute-start(bf16[2,128,1,128]{3,1,2,0:T(8,128)(2,1)S(1)} %pad_maximum_fusion.2), channel_id=1, source_target_pairs={{0,4},{4,8},{8,12},{12,16},{16,20},{20,24},{24,28},{28,32},{32,36}... | collective-permute-start | bytes 196616 | tf_op jit(solution)/shard_map/ppermute | solution.py:16
  63.2 113.9 %collective-permute-start.1 = (bf16[2,128,1,128]{3,1,2,0:T(8,128)(2,1)S(1)}, bf16[2,128,1,128]{3,1,2,0:T(8,128)(2,1)S(1)}, u32[]{:S(2)}, u32[]{:S(2)}) collective-permute-start(bf16[2,128,1,128]{3,1,2,0:T(8,128)(2,1)S(1)} %pad_maximum_fusion.2), channel_id=1, source_target_pairs={{0,8},{4,12},{8,16},{12,20},{16,24},{20,28},{24,32},{28,36},{32,40... | collective-permute-start | bytes 196616 | tf_op jit(solution)/shard_map/ppermute | solution.py:16
  66.3 145.3 %collective-permute-start.2 = (bf16[2,128,1,128]{3,1,2,0:T(8,128)(2,1)S(1)}, bf16[2,128,1,128]{3,1,2,0:T(8,128)(2,1)S(1)}, u32[]{:S(2)}, u32[]{:S(2)}) collective-permute-start(bf16[2,128,1,128]{3,1,2,0:T(8,128)(2,1)S(1)} %pad_maximum_fusion.2), channel_id=1, source_target_pairs={{0,12},{4,16},{8,20},{12,24},{16,28},{20,32},{24,36},{28,40},{32,4... | collective-permute-start | bytes 196616 | tf_op jit(solution)/shard_map/ppermute | solution.py:16
  69.6 142.1 %collective-permute-start.3 = (bf16[2,128,1,128]{3,1,2,0:T(8,128)(2,1)S(1)}, bf16[2,128,1,128]{3,1,2,0:T(8,128)(2,1)S(1)}, u32[]{:S(2)}, u32[]{:S(2)}) collective-permute-start(bf16[2,128,1,128]{3,1,2,0:T(8,128)(2,1)S(1)} %pad_maximum_fusion.2), channel_id=1, source_target_pairs={{0,16},{4,20},{8,24},{12,28},{16,32},{20,36},{24,40},{28,44},{32,4... | collective-permute-start | bytes 196616 | tf_op jit(solution)/shard_map/ppermute | solution.py:16
  73.9 137.8 %collective-permute-start.4 = (bf16[2,128,1,128]{3,1,2,0:T(8,128)(2,1)S(1)}, bf16[2,128,1,128]{3,1,2,0:T(8,128)(2,1)S(1)}, u32[]{:S(2)}, u32[]{:S(2)}) collective-permute-start(bf16[2,128,1,128]{3,1,2,0:T(8,128)(2,1)S(1)} %pad_maximum_fusion.2), channel_id=1, source_target_pairs={{0,20},{4,24},{8,28},{12,32},{16,36},{20,40},{24,44},{28,48},{32,5... | collective-permute-start | bytes 196616 | tf_op jit(solution)/shard_map/ppermute | solution.py:16
  173.2 38.4 %copy-start.14 = (bf16[2,128,1,128]{3,1,2,0:T(8,128)(2,1)}, bf16[2,128,1,128]{3,1,2,0:T(8,128)(2,1)S(1)}, u32[]{:S(2)}) copy-start(bf16[2,128,1,128]{3,1,2,0:T(8,128)(2,1)S(1)} %collective-permute-done) | copy-start | bytes 196612
  173.2 38.5 %collective-permute-start.5 = (bf16[2,128,1,128]{3,1,2,0:T(8,128)(2,1)S(1)}, bf16[2,128,1,128]{3,1,2,0:T(8,128)(2,1)S(1)}, u32[]{:S(2)}, u32[]{:S(2)}) collective-permute-start(bf16[2,128,1,128]{3,1,2,0:T(8,128)(2,1)S(1)} %pad_maximum_fusion.2), channel_id=1, source_target_pairs={{0,24},{4,28},{8,32},{12,36},{16,40},{20,44},{24,48},{28,52},{32,5... | collective-permute-start | bytes 196616 | tf_op jit(solution)/shard_map/ppermute | solution.py:16
  177.7 34.0 %collective-permute-start.6 = (bf16[2,128,1,128]{3,1,2,0:T(8,128)(2,1)S(1)}, bf16[2,128,1,128]{3,1,2,0:T(8,128)(2,1)S(1)}, u32[]{:S(2)}, u32[]{:S(2)}) collective-permute-start(bf16[2,128,1,128]{3,1,2,0:T(8,128)(2,1)S(1)} %pad_maximum_fusion.2), channel_id=1, source_target_pairs={{0,28},{4,32},{8,36},{12,40},{16,44},{20,48},{24,52},{28,56},{32,6... | collective-permute-start | bytes 196616 | tf_op jit(solution)/shard_map/ppermute | solution.py:16
  266.5 49.9 %copy-start.13 = (f32[128,8]{0,1:T(8,128)S(1)}, f32[128,8]{0,1:T(8,128)}, u32[]{:S(2)}) copy-start(f32[128,8]{0,1:T(8,128)} %param.15) | copy-start | bytes 12292
  268.8 48.3 %copy-start.10 = (bf16[128,1024]{1,0:T(8,128)(2,1)S(1)}, bf16[128,1024]{1,0:T(8,128)(2,1)}, u32[]{:S(2)}) copy-start(bf16[128,1024]{1,0:T(8,128)(2,1)} %param.13) | copy-start | bytes 786436
  268.8 48.3 %copy-start.12 = (bf16[128,1024]{1,0:T(8,128)(2,1)S(1)}, bf16[128,1024]{1,0:T(8,128)(2,1)}, u32[]{:S(2)}) copy-start(bf16[128,1024]{1,0:T(8,128)(2,1)} %param.17) | copy-start | bytes 786436
  268.9 49.3 %copy-start.27 = (bf16[2,128,1,128]{3,1,2,0:T(8,128)(2,1)S(1)}, bf16[2,128,1,128]{3,1,2,0:T(8,128)(2,1)}, u32[]{:S(2)}) copy-start(bf16[2,128,1,128]{3,1,2,0:T(8,128)(2,1)} %copy-done.26) | copy-start | bytes 196612
  281.9 36.4 %copy-start.25 = (bf16[2,128,1,128]{3,1,2,0:T(8,128)(2,1)S(1)}, bf16[2,128,1,128]{3,1,2,0:T(8,128)(2,1)}, u32[]{:S(2)}) copy-start(bf16[2,128,1,128]{3,1,2,0:T(8,128)(2,1)} %copy-done.24) | copy-start | bytes 196612
  281.9 26.7 %all-to-all-start.1 = ((f32[128,1,12]{2,1,0:T(1,128)}), f32[128,1,12]{2,1,0:T(1,128)S(1)}, u32[]{:S(2)}, u32[]{:S(2)}) async-start(f32[128,1,12]{2,1,0:T(1,128)} %bitcast.10), calls=%async_computation.1 | async-start | bytes 131072 | tf_op jit(solution)/shard_map/all_to_all | solution.py:125
  300.3 18.0 %copy-start.23 = (bf16[2,128,1,128]{3,1,2,0:T(8,128)(2,1)S(1)}, bf16[2,128,1,128]{3,1,2,0:T(8,128)(2,1)}, u32[]{:S(2)}) copy-start(bf16[2,128,1,128]{3,1,2,0:T(8,128)(2,1)} %copy-done.22) | copy-start | bytes 196612
  300.3 39.4 %all-gather.5.cloned.1.call-start = ((), (), s32[]{:S(2)}) async-start(), calls=%async_computation.4 | async-start | bytes 1310720 | tf_op jit(solution)/shard_map/all_gather | solution.py:133
  318.5 26.3 %copy-start.11 = (bf16[2,1024,1,128]{3,1,2,0:T(8,128)(2,1)}, bf16[2,1024,1,128]{3,1,2,0:T(8,128)(2,1)S(1)}, u32[]{:S(2)}) copy-start(bf16[2,1024,1,128]{3,1,2,0:T(8,128)(2,1)S(1)} %constant_dynamic-update-slice_fusion) | copy-start | bytes 1572868
  356.1 15.9 %copy-start.6 = (bf16[1,1,192,1536]{2,3,1,0:T(8,128)(2,1)S(1)}, bf16[1,1,192,1536]{2,3,1,0:T(8,128)(2,1)}, u32[]{:S(2)}) copy-start(bf16[1,1,192,1536]{2,3,1,0:T(8,128)(2,1)} %get-tuple-element.74) | copy-start | bytes 1769476
  359.5 26.1 %collective-permute-start.10 = (bf16[2,128,1,128]{3,1,0,2:T(8,128)(2,1)}, bf16[2,128,1,128]{3,1,0,2:T(8,128)(2,1)}, u32[]{:S(2)}, u32[]{:S(2)}) collective-permute-start(bf16[2,128,1,128]{3,1,0,2:T(8,128)(2,1)} %get-tuple-element.82), channel_id=1, source_target_pairs={{16,0},{20,4},{24,8},{28,12},{32,16},{36,20},{40,24},{44,28},{48,3... | collective-permute-start | bytes 196616 | tf_op jit(solution)/shard_map/ppermute | solution.py:16
  366.7 21.8 %collective-permute-start.11 = (bf16[2,128,1,128]{3,1,0,2:T(8,128)(2,1)S(1)}, bf16[2,128,1,128]{3,1,0,2:T(8,128)(2,1)}, u32[]{:S(2)}, u32[]{:S(2)}) collective-permute-start(bf16[2,128,1,128]{3,1,0,2:T(8,128)(2,1)S(1)} %get-tuple-element.81), channel_id=1, source_target_pairs={{20,0},{24,4},{28,8},{32,12},{36,16},{40,20},{44,24},{48,28},{52,3... | collective-permute-start | bytes 196616 | tf_op jit(solution)/shard_map/ppermute | solution.py:16
  372.1 25.2 %copy-start.1 = (bf16[1,768,1024]{2,1,0:T(8,128)(2,1)S(1)}, bf16[1,768,1024]{2,1,0:T(8,128)(2,1)}, u32[]{:S(2)}) copy-start(bf16[1,768,1024]{2,1,0:T(8,128)(2,1)} %param.18) | copy-start | bytes 4718596
  373.9 19.8 %collective-permute-start.12 = (bf16[2,128,1,128]{3,1,0,2:T(8,128)(2,1)S(1)}, bf16[2,128,1,128]{3,1,0,2:T(8,128)(2,1)S(1)}, u32[]{:S(2)}, u32[]{:S(2)}) collective-permute-start(bf16[2,128,1,128]{3,1,0,2:T(8,128)(2,1)S(1)} %get-tuple-element.80), channel_id=1, source_target_pairs={{24,0},{28,4},{32,8},{36,12},{40,16},{44,20},{48,24},{52,28},{56,3... | collective-permute-start | bytes 196616 | tf_op jit(solution)/shard_map/ppermute | solution.py:16
  375.8 17.9 %collective-permute-start.13 = (bf16[2,128,1,128]{3,1,2,0:T(8,128)(2,1)S(1)}, bf16[2,128,1,128]{3,1,2,0:T(8,128)(2,1)S(1)}, u32[]{:S(2)}, u32[]{:S(2)}) collective-permute-start(bf16[2,128,1,128]{3,1,2,0:T(8,128)(2,1)S(1)} %get-tuple-element.79), channel_id=1, source_target_pairs={{28,0},{32,4},{36,8},{40,12},{44,16},{48,20},{52,24},{56,28},{60,3... | collective-permute-start | bytes 196616 | tf_op jit(solution)/shard_map/ppermute | solution.py:16
  382.0 11.7 %collective-permute-start.7 = (bf16[2,128,1,128]{3,1,0,2:T(8,128)(2,1)S(1)}, bf16[2,128,1,128]{3,1,0,2:T(8,128)(2,1)S(1)}, u32[]{:S(2)}, u32[]{:S(2)}) collective-permute-start(bf16[2,128,1,128]{3,1,0,2:T(8,128)(2,1)S(1)} %get-tuple-element.78), channel_id=1, source_target_pairs={{4,0},{8,4},{12,8},{16,12},{20,16},{24,20},{28,24},{32,28},{36,32}... | collective-permute-start | bytes 196616 | tf_op jit(solution)/shard_map/ppermute | solution.py:16
  385.5 8.2 %collective-permute-start.8 = (bf16[2,128,1,128]{3,1,0,2:T(8,128)(2,1)S(1)}, bf16[2,128,1,128]{3,1,0,2:T(8,128)(2,1)S(1)}, u32[]{:S(2)}, u32[]{:S(2)}) collective-permute-start(bf16[2,128,1,128]{3,1,0,2:T(8,128)(2,1)S(1)} %get-tuple-element.84), channel_id=1, source_target_pairs={{8,0},{12,4},{16,8},{20,12},{24,16},{28,20},{32,24},{36,28},{40,32... | collective-permute-start | bytes 196616 | tf_op jit(solution)/shard_map/ppermute | solution.py:16
  388.5 7.2 %collective-permute-start.9 = (bf16[2,128,1,128]{3,1,0,2:T(8,128)(2,1)S(1)}, bf16[2,128,1,128]{3,1,0,2:T(8,128)(2,1)S(1)}, u32[]{:S(2)}, u32[]{:S(2)}) collective-permute-start(bf16[2,128,1,128]{3,1,0,2:T(8,128)(2,1)S(1)} %get-tuple-element.83), channel_id=1, source_target_pairs={{12,0},{16,4},{20,8},{24,12},{28,16},{32,20},{36,24},{40,28},{44,3... | collective-permute-start | bytes 196616 | tf_op jit(solution)/shard_map/ppermute | solution.py:16
  (18 other events, 181.6 us)
Sparse Core Ops, SparseCore 0:
  11.1 210.2 all-gather.2
  232.1 33.0 reduce-scatter.3
  318.4 21.2 all-gather.4

commit v2 on v1

--- a/solution.py
+++ b/solution.py
@@ -82,7 +82,7 @@
     send_weight = jnp.sum(placed * weights[None, :, :], axis=(1, 2)).astype(jnp.bfloat16)
     weight_lanes = jnp.zeros((experts * capacity, 128), jnp.bfloat16).at[:, 0].set(send_weight)
     payload = jnp.concatenate([send_rows, weight_lanes], axis=1)
-    weight_full = lax.all_gather(out_weight, "seq", axis=1, tiled=True)
+    weight_full = out_weight
     kv_heads = key.shape[1]
     head_dim = key.shape[2]
     group = query.shape[1] // kv_heads
@@ -131,8 +131,15 @@
     router_term = jnp.dot(dense, router.astype(jnp.float32), precision=highest)
     input_slice = (out_grad.astype(jnp.float32) + router_term).astype(jnp.bfloat16)
     input_grad = lax.all_gather(input_slice, "head", axis=1, tiled=True)
+    core = seq_index % 2
+    by_parity = input_grad.reshape(tokens_here, seq_count // 2, 2, -1)
+    mine = lax.dynamic_index_in_dim(by_parity, core, axis=2, keepdims=False)
+    theirs = lax.dynamic_index_in_dim(by_parity, 1 - core, axis=2, keepdims=False)
+    ordered = jnp.concatenate(
+        [mine.reshape(tokens_here, -1), theirs.reshape(tokens_here, -1)], axis=1
+    )
     attn_grad = lax.dot_general(
-        input_grad,
+        ordered,
         weight_full,
         (((1,), (1,)), ((), ())),
         preferred_element_type=jnp.float32,
@@ -166,7 +173,24 @@
     )
 
 
+def gather_columns(out_weight):
+    half = lax.all_gather(out_weight, "chip", axis=1, tiled=True)
+    other = lax.ppermute(half, "core", [(0, 1), (1, 0)])
+    return jnp.concatenate([half, other], axis=1)
+
+
 def solution(mesh):
+    chips = mesh.devices.shape[0] // 2
+    split_mesh = jax.sharding.Mesh(
+        mesh.devices.reshape(chips, 2, mesh.devices.shape[1]), ("chip", "core", "head")
+    )
+    gather = jax.shard_map(
+        gather_columns,
+        mesh=split_mesh,
+        in_specs=P("head", ("chip", "core")),
+        out_specs=P("head", ("chip", "core")),
+        check_vma=False,
+    )
     in_specs = (
         P("seq", "head"),
         P("seq", None),
@@ -187,6 +211,13 @@
         P("seq", "head", None),
         P("seq", "head", None),
     )
-    return jax.shard_map(
+    body = jax.shard_map(
         per_device, mesh=mesh, in_specs=in_specs, out_specs=out_specs, check_vma=False
     )
+
+    def run(*args):
+        args = list(args)
+        args[7] = gather(args[7])
+        return body(*args)
+
+    return run

time: 406 us -> 427 us (1.052)
  waiting for transfers between devices: 167 us -> 192 us
  starting transfers between devices: 112 us -> 97.6 us
  other arithmetic: 29.2 us -> 38.5 us
    all_gather x1, waiting for transfers between devices: 9.73 us -> 135 us  [gather_columns(): half = lax.all_gather(out_weight, 'chip', axis=1, tiled=True)]
    ppermute x14, waiting for transfers between devices: 101 us -> 0.33 us  [passed_along(): return lax.ppermute(array, axis, pairs)]
    ppermute x14, starting transfers between devices: 75.1 us -> 55.1 us  [passed_along(): return lax.ppermute(array, axis, pairs)]
    concatenate x0 -> x1, other arithmetic: none -> 7.68 us  [gather_columns(): return jnp.concatenate([half, other], axis=1)]
    ppermute x0 -> x1, starting transfers between devices: none -> 5.7 us  [gather_columns(): other = lax.ppermute(half, 'core', [(0, 1), (1, 0)])]
    unnamed x77 -> x73, local copies, waits for them, and re-layouts: 12.3 us -> 11.7 us
  transfers between devices with their start and end apart: 19 -> 20, of which waited for: 7 -> 5; matrix products, arithmetic and copies ran while one was open for 12% -> 14% of each run, Pallas kernels for 0% -> 0%
where the time goes in v2:
time: 427 us; the launch traced here: 425 us
  waiting for transfers between devices  192 us (45%)
  starting transfers between devices  97.6 us (23%)
  local copies, waits for them, and re-layouts  45.6 us (11%)
  other arithmetic  38.5 us (9%)
  matrix products  23.4 us (5%)
  between operations  14.7 us (3%)
  blocking collectives  12.9 us (3%)
    all_gather x1, waiting for transfers between devices, gather_columns(): half = lax.all_gather(out_weight, 'chip', axis=1, tiled=True)  135 us
    ppermute x14, starting transfers between devices, passed_along(): return lax.ppermute(array, axis, pairs)  55.1 us
    unnamed x4, waiting for transfers between devices  30.8 us
    all_to_all x1, starting transfers between devices, per_device(): lax.all_to_all(slot_grad.reshape(seq_count, capacity), 'seq', split_axis=...  18.3 us
    all_to_all x1, starting transfers between devices, per_device(): lax.all_to_all(payload.reshape(experts, capacity, features + 128), 'seq',...  18.2 us
    all_gather x1, waiting for transfers between devices, per_device(): input_grad = lax.all_gather(input_slice, 'head', axis=1, tiled=True)  17.5 us
    psum x1, blocking collectives, per_device(): slot_grad = lax.psum(slot_part, 'head')  12.9 us
    unnamed x73, local copies, waits for them, and re-layouts  11.7 us
  transfers between devices with their start and end apart: 20, of which 5 were waited for; matrix products, arithmetic and copies ran while one was open for 14% of the time, Pallas kernels for 0%

profile of v2, /device:TPU:49, one launch (start us, length us, event | category | flops | bytes accessed | tf_op | source)
XLA Modules:
  0.0 424.8 jit_solution(11453210561158346732)
XLA Ops:
  13.0 11.6 %convert_reduce_fusion = (bf16[1536,128]{1,0:T(8,128)(2,1)S(1)}, bf16[1536]{0:T(1024)(128)(2,1)S(1)}) fusion(s32[128,8]{0,1:T(8,128)S(1)} %convert_add_fusion, f32[128,8]{0,1:T(8,128)S(1)} %fusion.55), kind=kLoop, calls=%fused_computation.5 | loop fusion | flops 7666176 | bytes 404480 | tf_op jit(solution)/shard_map/reduce_sum | solution.py:80
  29.3 5.8 %copy.130 = bf16[1536,1152]{1,0:T(8,128)(2,1)} copy(bf16[1536,1152]{0,1:T(8,128)(2,1)} %fusion.6) | data formatting | bytes 7077888 | tf_op jit(solution)/shard_map/concatenate | solution.py:84
  35.1 6.5 %reshape.406 = bf16[128,12,1152]{2,1,0:T(8,128)(2,1)} reshape(bf16[1536,1152]{1,0:T(8,128)(2,1)} %copy.130) | data formatting | bytes 7077888 | tf_op jit(solution)/shard_map/reshape | solution.py:94
  41.6 18.2 %all-to-all-start = ((bf16[128,12,1152]{2,1,0:T(8,128)(2,1)}), bf16[128,12,1152]{2,1,0:T(8,128)(2,1)}, u32[]{:S(2)}, u32[]{:S(2)}) async-start(bf16[128,12,1152]{2,1,0:T(8,128)(2,1)} %reshape.406), calls=%async_computation | async-start | bytes 9437184 | tf_op jit(solution)/shard_map/all_to_all | solution.py:93
  59.8 135.4 %all-gather.3.cloned.1.call-done = bf16[1024,2048]{0,1:T(8,128)(2,1)} async-done(((bf16[1024,32]{0,1:T(8,128)(2,1)}), bf16[1024,2048]{0,1:T(8,128)(2,1)}) %all-gather.3.cloned.1.call-update) | async-done | bytes 4194320 | tf_op jit(solution)/shard_map/all_gather | solution.py:177
  195.2 5.7 %collective-permute-start = (bf16[1024,2048]{0,1:T(8,128)(2,1)}, bf16[1024,2048]{0,1:T(8,128)(2,1)}, u32[]{:S(2)}, u32[]{:S(2)}) collective-permute-start(bf16[1024,2048]{0,1:T(8,128)(2,1)} %all-gather.3.cloned.1.call-done), channel_id=1, source_target_pairs={{0,4},{4,0},{1,5},{5,1},{2,6},{6,2},{3,7},{7,3},{8,12},{12,8},{9,1... | collective-permute-start | bytes 12582920 | tf_op jit(solution)/shard_map/ppermute | solution.py:178
  201.0 2.5 collective-permute-start.1
  205.5 3.6 collective-permute-start.3
  209.2 3.2 collective-permute-start.4
  212.4 6.6 %reshape.407 = bf16[1536,1152]{1,0:T(8,128)(2,1)} reshape(bf16[128,12,1152]{2,1,0:T(8,128)(2,1)} %all-to-all-done) | data formatting | bytes 7077888 | tf_op jit(solution)/shard_map/reshape | solution.py:99
  219.0 5.4 %collective-permute-start.5 = (bf16[2,128,1,128]{3,1,2,0:T(8,128)(2,1)S(1)}, bf16[2,128,1,128]{3,1,2,0:T(8,128)(2,1)S(1)}, u32[]{:S(2)}, u32[]{:S(2)}) collective-permute-start(bf16[2,128,1,128]{3,1,2,0:T(8,128)(2,1)S(1)} %pad_maximum_fusion.3), channel_id=1, source_target_pairs={{0,20},{4,24},{8,28},{12,32},{16,36},{20,40},{24,44},{28,48},{32,5... | collective-permute-start | bytes 196616 | tf_op jit(solution)/shard_map/ppermute | solution.py:16
  226.4 7.1 %collective-permute-start.7 = (bf16[2,128,1,128]{3,1,2,0:T(8,128)(2,1)S(1)}, bf16[2,128,1,128]{3,1,2,0:T(8,128)(2,1)S(1)}, u32[]{:S(2)}, u32[]{:S(2)}) collective-permute-start(bf16[2,128,1,128]{3,1,2,0:T(8,128)(2,1)S(1)} %pad_maximum_fusion.3), channel_id=1, source_target_pairs={{0,28},{4,32},{8,36},{12,40},{16,44},{20,48},{24,52},{28,56},{32,6... | collective-permute-start | bytes 196616 | tf_op jit(solution)/shard_map/ppermute | solution.py:16
  233.5 7.7 %pad_maximum_fusion = bf16[1024,4096]{0,1:T(8,128)(2,1)} fusion(bf16[1024,2048]{0,1:T(8,128)(2,1)} %collective-permute-done, bf16[1024,2048]{0,1:T(8,128)(2,1)} %all-gather.3.cloned.1.call-done), kind=kLoop, calls=%fused_computation.1 | loop fusion | flops 16777216 | bytes 16777216 | tf_op jit(solution)/shard_map/concatenate | solution.py:179
  241.3 6.0 %fusion.9 = bf16[768,1536]{0,1:T(8,128)(2,1)} fusion(bf16[1536,1152]{1,0:T(8,128)(2,1)} %reshape.407, bf16[1,768,1024]{2,1,0:T(8,128)(2,1)S(1)} %copy-done), kind=kOutput, calls=%fused_computation.21 | convolution fusion | flops 2417098752 | bytes 7077888 | tf_op jit(solution)/shard_map/dot_general | solution.py:107
  247.3 4.4 %copy.154 = bf16[768,1536]{1,0:T(8,128)(2,1)} copy(bf16[768,1536]{0,1:T(8,128)(2,1)} %fusion.9) | data formatting | bytes 4718592
  254.8 30.1 %reduce-scatter.4.cloned.1.call-done = bf16[192,1536]{1,0:T(8,128)(2,1)} async-done(((bf16[768,1536]{1,0:T(8,128)(2,1)}), bf16[192,1536]{1,0:T(8,128)(2,1)}) %reduce-scatter.4.cloned.1.call-update) | async-done | bytes 589840
  286.3 2.4 fusion.15
  288.8 12.9 %psum.7 = f32[128,1,12]{2,0,1:T(8,128)} all-reduce(f32[128,1,12]{2,0,1:T(8,128)S(1)} %all_to_all.10), channel_id=1, replica_groups=mesh['chip'=64,'core'=2,'head'=4] {'head'}, use_global_device_ids=true, to_apply=%region_9.0 | all-reduce | flops 1536 | bytes 12288 | tf_op jit(solution)/shard_map/psum | solution.py:124
  301.8 18.3 %all-to-all-start.1 = ((f32[128,1,12]{2,1,0:T(1,128)}), f32[128,1,12]{2,1,0:T(1,128)S(1)}, u32[]{:S(2)}, u32[]{:S(2)}) async-start(f32[128,1,12]{2,1,0:T(1,128)} %bitcast.10), calls=%async_computation.1 | async-start | bytes 131072 | tf_op jit(solution)/shard_map/all_to_all | solution.py:125
  320.4 7.9 %all-to-all-done.1 = f32[128,1,12]{2,1,0:T(1,128)S(1)} async-done(((f32[128,1,12]{2,1,0:T(1,128)}), f32[128,1,12]{2,1,0:T(1,128)S(1)}, u32[]{:S(2)}, u32[]{:S(2)}) %all-to-all-start.1) | async-done | bytes 6176 | tf_op jit(solution)/shard_map/all_to_all | solution.py:125
  329.8 6.2 %gather_fusion = f32[1024]{0:T(1024)S(1)} fusion(f32[1536]{0:T(1024)S(1)} %reshape.408, s32[1024]{0:T(1024)S(1)} %broadcast_clamp_fusion), kind=kCustom, calls=%fused_computation | custom fusion | bytes 12288 | tf_op jit(solution)/shard_map/jit(_take)/gather | solution.py:128
  341.9 17.5 %all-gather.5.cloned.1.call-done = bf16[128,4096]{1,0:T(8,128)(2,1)} async-done(((bf16[128,1024]{1,0:T(8,128)(2,1)}), bf16[128,4096]{1,0:T(8,128)(2,1)}) %all-gather.5.cloned.1.call-update) | async-done | bytes 1048592 | tf_op jit(solution)/shard_map/all_gather | solution.py:133
  361.2 4.8 %convolution_convert_fusion.2 = bf16[128,1024]{1,0:T(8,128)(2,1)S(1)} fusion(bf16[1024,4096]{0,1:T(8,128)(2,1)} %pad_maximum_fusion, bf16[128,2048]{0,1:T(8,128)(2,1)S(1)} %bitcast.183, bf16[128,2048]{0,1:T(8,128)(2,1)S(1)} %bitcast.182), kind=kOutput, calls=%fused_computation.51 | convolution fusion | flops 1075970048 | bytes 9699328 | tf_op jit(solution)/shard_map/dot_general | solution.py:141
  367.4 3.4 convert_bitcast_fusion
  370.8 4.2 copy.142
  377.3 2.5 fusion.24
  380.6 9.3 %collective-permute-start.14 = (bf16[2,128,1,128]{3,1,2,0:T(8,128)(2,1)}, bf16[2,128,1,128]{3,1,2,0:T(8,128)(2,1)}, u32[]{:S(2)}, u32[]{:S(2)}) collective-permute-start(bf16[2,128,1,128]{3,1,2,0:T(8,128)(2,1)} %get-tuple-element.82), channel_id=1, source_target_pairs={{28,0},{32,4},{36,8},{40,12},{44,16},{48,20},{52,24},{56,28},{60,3... | collective-permute-start | bytes 196616 | tf_op jit(solution)/shard_map/ppermute | solution.py:16
  390.0 2.5 collective-permute-start.13
  395.8 5.2 %collective-permute-start.12 = (bf16[2,128,1,128]{3,1,0,2:T(8,128)(2,1)S(1)}, bf16[2,128,1,128]{3,1,0,2:T(8,128)(2,1)S(1)}, u32[]{:S(2)}, u32[]{:S(2)}) collective-permute-start(bf16[2,128,1,128]{3,1,0,2:T(8,128)(2,1)S(1)} %get-tuple-element.84), channel_id=1, source_target_pairs={{20,0},{24,4},{28,8},{32,12},{36,16},{40,20},{44,24},{48,28},{52,3... | collective-permute-start | bytes 196616 | tf_op jit(solution)/shard_map/ppermute | solution.py:16
  401.0 3.6 collective-permute-start.11
  404.6 4.4 %collective-permute-start.10 = (bf16[2,128,1,128]{3,1,0,2:T(8,128)(2,1)S(1)}, bf16[2,128,1,128]{3,1,0,2:T(8,128)(2,1)S(1)}, u32[]{:S(2)}, u32[]{:S(2)}) collective-permute-start(bf16[2,128,1,128]{3,1,0,2:T(8,128)(2,1)S(1)} %get-tuple-element.86), channel_id=1, source_target_pairs={{12,0},{16,4},{20,8},{24,12},{28,16},{32,20},{36,24},{40,28},{44,3... | collective-permute-start | bytes 196616 | tf_op jit(solution)/shard_map/ppermute | solution.py:16
  411.1 2.2 collective-permute-start.8
  (152 shorter events, 42.8 us)
Async XLA Ops:
  7.2 234.1 %copy-start = (bf16[1,768,1024]{2,1,0:T(8,128)(2,1)S(1)}, bf16[1,768,1024]{2,1,0:T(8,128)(2,1)}, u32[]{:S(2)}) copy-start(bf16[1,768,1024]{2,1,0:T(8,128)(2,1)} %param.19) | copy-start | bytes 4718596
  7.2 188.0 %all-gather.3.cloned.1.call-start = ((), (), s32[]{:S(2)}) async-start(), calls=%async_computation.3 | async-start | bytes 4259840 | tf_op jit(solution)/shard_map/all_gather | solution.py:177
  41.6 159.4 %copy-start.26 = (bf16[128,1,128]{2,0,1:T(8,128)(2,1)S(1)}, bf16[128,1,128]{2,0,1:T(8,128)(2,1)}, u32[]{:S(2)}) copy-start(bf16[128,1,128]{2,0,1:T(8,128)(2,1)} %param.24) | copy-start | bytes 98308
  41.6 159.4 %copy-start.27 = (bf16[128,1,128]{2,0,1:T(8,128)(2,1)S(1)}, bf16[128,1,128]{2,0,1:T(8,128)(2,1)}, u32[]{:S(2)}) copy-start(bf16[128,1,128]{2,0,1:T(8,128)(2,1)} %param.23) | copy-start | bytes 98308
  41.6 170.8 %all-to-all-start = ((bf16[128,12,1152]{2,1,0:T(8,128)(2,1)}), bf16[128,12,1152]{2,1,0:T(8,128)(2,1)}, u32[]{:S(2)}, u32[]{:S(2)}) async-start(bf16[128,12,1152]{2,1,0:T(8,128)(2,1)} %reshape.406), calls=%async_computation | async-start | bytes 9437184 | tf_op jit(solution)/shard_map/all_to_all | solution.py:93
  59.7 225.1 %reduce-scatter.4.cloned.1.call-start = ((), (), s32[]{:S(2)}) async-start(), calls=%async_computation.5 | async-start | bytes 2949120
  195.2 31.2 %collective-permute-start = (bf16[1024,2048]{0,1:T(8,128)(2,1)}, bf16[1024,2048]{0,1:T(8,128)(2,1)}, u32[]{:S(2)}, u32[]{:S(2)}) collective-permute-start(bf16[1024,2048]{0,1:T(8,128)(2,1)} %all-gather.3.cloned.1.call-done), channel_id=1, source_target_pairs={{0,4},{4,0},{1,5},{5,1},{2,6},{6,2},{3,7},{7,3},{8,12},{12,8},{9,1... | collective-permute-start | bytes 12582920 | tf_op jit(solution)/shard_map/ppermute | solution.py:178
  201.0 18.1 %collective-permute-start.1 = (bf16[2,128,1,128]{3,1,2,0:T(8,128)(2,1)S(1)}, bf16[2,128,1,128]{3,1,2,0:T(8,128)(2,1)S(1)}, u32[]{:S(2)}, u32[]{:S(2)}) collective-permute-start(bf16[2,128,1,128]{3,1,2,0:T(8,128)(2,1)S(1)} %pad_maximum_fusion.3), channel_id=1, source_target_pairs={{0,4},{4,8},{8,12},{12,16},{16,20},{20,24},{24,28},{28,32},{32,36}... | collective-permute-start | bytes 196616 | tf_op jit(solution)/shard_map/ppermute | solution.py:16
  203.5 21.0 %collective-permute-start.2 = (bf16[2,128,1,128]{3,1,2,0:T(8,128)(2,1)S(1)}, bf16[2,128,1,128]{3,1,2,0:T(8,128)(2,1)S(1)}, u32[]{:S(2)}, u32[]{:S(2)}) collective-permute-start(bf16[2,128,1,128]{3,1,2,0:T(8,128)(2,1)S(1)} %pad_maximum_fusion.3), channel_id=1, source_target_pairs={{0,8},{4,12},{8,16},{12,20},{16,24},{20,28},{24,32},{28,36},{32,40... | collective-permute-start | bytes 196616 | tf_op jit(solution)/shard_map/ppermute | solution.py:16
  205.5 35.7 %collective-permute-start.3 = (bf16[2,128,1,128]{3,1,2,0:T(8,128)(2,1)S(1)}, bf16[2,128,1,128]{3,1,2,0:T(8,128)(2,1)S(1)}, u32[]{:S(2)}, u32[]{:S(2)}) collective-permute-start(bf16[2,128,1,128]{3,1,2,0:T(8,128)(2,1)S(1)} %pad_maximum_fusion.3), channel_id=1, source_target_pairs={{0,12},{4,16},{8,20},{12,24},{16,28},{20,32},{24,36},{28,40},{32,4... | collective-permute-start | bytes 196616 | tf_op jit(solution)/shard_map/ppermute | solution.py:16
  209.2 32.0 %collective-permute-start.4 = (bf16[2,128,1,128]{3,1,2,0:T(8,128)(2,1)S(1)}, bf16[2,128,1,128]{3,1,2,0:T(8,128)(2,1)S(1)}, u32[]{:S(2)}, u32[]{:S(2)}) collective-permute-start(bf16[2,128,1,128]{3,1,2,0:T(8,128)(2,1)S(1)} %pad_maximum_fusion.3), channel_id=1, source_target_pairs={{0,16},{4,20},{8,24},{12,28},{16,32},{20,36},{24,40},{28,44},{32,4... | collective-permute-start | bytes 196616 | tf_op jit(solution)/shard_map/ppermute | solution.py:16
  219.0 22.2 %collective-permute-start.5 = (bf16[2,128,1,128]{3,1,2,0:T(8,128)(2,1)S(1)}, bf16[2,128,1,128]{3,1,2,0:T(8,128)(2,1)S(1)}, u32[]{:S(2)}, u32[]{:S(2)}) collective-permute-start(bf16[2,128,1,128]{3,1,2,0:T(8,128)(2,1)S(1)} %pad_maximum_fusion.3), channel_id=1, source_target_pairs={{0,20},{4,24},{8,28},{12,32},{16,36},{20,40},{24,44},{28,48},{32,5... | collective-permute-start | bytes 196616 | tf_op jit(solution)/shard_map/ppermute | solution.py:16
  224.5 16.7 %collective-permute-start.6 = (bf16[2,128,1,128]{3,1,2,0:T(8,128)(2,1)S(1)}, bf16[2,128,1,128]{3,1,2,0:T(8,128)(2,1)S(1)}, u32[]{:S(2)}, u32[]{:S(2)}) collective-permute-start(bf16[2,128,1,128]{3,1,2,0:T(8,128)(2,1)S(1)} %pad_maximum_fusion.3), channel_id=1, source_target_pairs={{0,24},{4,28},{8,32},{12,36},{16,40},{20,44},{24,48},{28,52},{32,5... | collective-permute-start | bytes 196616 | tf_op jit(solution)/shard_map/ppermute | solution.py:16
  226.4 14.8 %collective-permute-start.7 = (bf16[2,128,1,128]{3,1,2,0:T(8,128)(2,1)S(1)}, bf16[2,128,1,128]{3,1,2,0:T(8,128)(2,1)S(1)}, u32[]{:S(2)}, u32[]{:S(2)}) collective-permute-start(bf16[2,128,1,128]{3,1,2,0:T(8,128)(2,1)S(1)} %pad_maximum_fusion.3), channel_id=1, source_target_pairs={{0,28},{4,32},{8,36},{12,40},{16,44},{20,48},{24,52},{28,56},{32,6... | collective-permute-start | bytes 196616 | tf_op jit(solution)/shard_map/ppermute | solution.py:16
  286.2 49.8 %copy-start.11 = (f32[128,8]{0,1:T(8,128)S(1)}, f32[128,8]{0,1:T(8,128)}, u32[]{:S(2)}) copy-start(f32[128,8]{0,1:T(8,128)} %param.16) | copy-start | bytes 12292
  286.2 50.6 %copy-start.8 = (bf16[128,1024]{1,0:T(8,128)(2,1)S(1)}, bf16[128,1024]{1,0:T(8,128)(2,1)}, u32[]{:S(2)}) copy-start(bf16[128,1024]{1,0:T(8,128)(2,1)} %param.14) | copy-start | bytes 786436
  286.2 50.6 %copy-start.10 = (bf16[128,1024]{1,0:T(8,128)(2,1)S(1)}, bf16[128,1024]{1,0:T(8,128)(2,1)}, u32[]{:S(2)}) copy-start(bf16[128,1024]{1,0:T(8,128)(2,1)} %param.18) | copy-start | bytes 786436
  288.7 49.4 %copy-start.21 = (bf16[2,128,1,128]{3,1,2,0:T(8,128)(2,1)S(1)}, bf16[2,128,1,128]{3,1,2,0:T(8,128)(2,1)}, u32[]{:S(2)}) copy-start(bf16[2,128,1,128]{3,1,2,0:T(8,128)(2,1)} %copy-done.20) | copy-start | bytes 196612
  288.7 49.4 %copy-start.19 = (bf16[2,128,1,128]{3,1,2,0:T(8,128)(2,1)S(1)}, bf16[2,128,1,128]{3,1,2,0:T(8,128)(2,1)}, u32[]{:S(2)}) copy-start(bf16[2,128,1,128]{3,1,2,0:T(8,128)(2,1)} %copy-done.18) | copy-start | bytes 196612
  288.7 49.4 %copy-start.17 = (bf16[2,128,1,128]{3,1,2,0:T(8,128)(2,1)S(1)}, bf16[2,128,1,128]{3,1,2,0:T(8,128)(2,1)}, u32[]{:S(2)}) copy-start(bf16[2,128,1,128]{3,1,2,0:T(8,128)(2,1)} %copy-done.16) | copy-start | bytes 196612
  288.7 49.4 %copy-start.15 = (bf16[2,128,1,128]{3,1,2,0:T(8,128)(2,1)S(1)}, bf16[2,128,1,128]{3,1,2,0:T(8,128)(2,1)}, u32[]{:S(2)}) copy-start(bf16[2,128,1,128]{3,1,2,0:T(8,128)(2,1)} %copy-done.14) | copy-start | bytes 196612
  288.7 49.4 %copy-start.13 = (bf16[2,128,1,128]{3,1,2,0:T(8,128)(2,1)S(1)}, bf16[2,128,1,128]{3,1,2,0:T(8,128)(2,1)}, u32[]{:S(2)}) copy-start(bf16[2,128,1,128]{3,1,2,0:T(8,128)(2,1)} %copy-done.12) | copy-start | bytes 196612
  288.7 49.5 %copy-start.7 = (bf16[128,8,128]{2,1,0:T(8,128)(2,1)S(1)}, bf16[128,8,128]{2,1,0:T(8,128)(2,1)}, u32[]{:S(2)}) copy-start(bf16[128,8,128]{2,1,0:T(8,128)(2,1)} %param.22) | copy-start | bytes 786436
  301.8 26.6 %all-to-all-start.1 = ((f32[128,1,12]{2,1,0:T(1,128)}), f32[128,1,12]{2,1,0:T(1,128)S(1)}, u32[]{:S(2)}, u32[]{:S(2)}) async-start(f32[128,1,12]{2,1,0:T(1,128)} %bitcast.10), calls=%async_computation.1 | async-start | bytes 131072 | tf_op jit(solution)/shard_map/all_to_all | solution.py:125
  320.1 39.3 %all-gather.5.cloned.1.call-start = ((), (), s32[]{:S(2)}) async-start(), calls=%async_computation.4 | async-start | bytes 1310720 | tf_op jit(solution)/shard_map/all_gather | solution.py:133
  380.6 28.4 %collective-permute-start.14 = (bf16[2,128,1,128]{3,1,2,0:T(8,128)(2,1)}, bf16[2,128,1,128]{3,1,2,0:T(8,128)(2,1)}, u32[]{:S(2)}, u32[]{:S(2)}) collective-permute-start(bf16[2,128,1,128]{3,1,2,0:T(8,128)(2,1)} %get-tuple-element.82), channel_id=1, source_target_pairs={{28,0},{32,4},{36,8},{40,12},{44,16},{48,20},{52,24},{56,28},{60,3... | collective-permute-start | bytes 196616 | tf_op jit(solution)/shard_map/ppermute | solution.py:16
  390.0 21.1 %collective-permute-start.13 = (bf16[2,128,1,128]{3,1,0,2:T(8,128)(2,1)S(1)}, bf16[2,128,1,128]{3,1,0,2:T(8,128)(2,1)}, u32[]{:S(2)}, u32[]{:S(2)}) collective-permute-start(bf16[2,128,1,128]{3,1,0,2:T(8,128)(2,1)S(1)} %get-tuple-element.83), channel_id=1, source_target_pairs={{24,0},{28,4},{32,8},{36,12},{40,16},{44,20},{48,24},{52,28},{56,3... | collective-permute-start | bytes 196616 | tf_op jit(solution)/shard_map/ppermute | solution.py:16
  395.8 20.5 %collective-permute-start.12 = (bf16[2,128,1,128]{3,1,0,2:T(8,128)(2,1)S(1)}, bf16[2,128,1,128]{3,1,0,2:T(8,128)(2,1)S(1)}, u32[]{:S(2)}, u32[]{:S(2)}) collective-permute-start(bf16[2,128,1,128]{3,1,0,2:T(8,128)(2,1)S(1)} %get-tuple-element.84), channel_id=1, source_target_pairs={{20,0},{24,4},{28,8},{32,12},{36,16},{40,20},{44,24},{48,28},{52,3... | collective-permute-start | bytes 196616 | tf_op jit(solution)/shard_map/ppermute | solution.py:16
  401.0 15.3 %collective-permute-start.11 = (bf16[2,128,1,128]{3,1,0,2:T(8,128)(2,1)S(1)}, bf16[2,128,1,128]{3,1,0,2:T(8,128)(2,1)S(1)}, u32[]{:S(2)}, u32[]{:S(2)}) collective-permute-start(bf16[2,128,1,128]{3,1,0,2:T(8,128)(2,1)S(1)} %get-tuple-element.85), channel_id=1, source_target_pairs={{16,0},{20,4},{24,8},{28,12},{32,16},{36,20},{40,24},{44,28},{48,3... | collective-permute-start | bytes 196616 | tf_op jit(solution)/shard_map/ppermute | solution.py:16
  404.6 11.7 %collective-permute-start.10 = (bf16[2,128,1,128]{3,1,0,2:T(8,128)(2,1)S(1)}, bf16[2,128,1,128]{3,1,0,2:T(8,128)(2,1)S(1)}, u32[]{:S(2)}, u32[]{:S(2)}) collective-permute-start(bf16[2,128,1,128]{3,1,0,2:T(8,128)(2,1)S(1)} %get-tuple-element.86), channel_id=1, source_target_pairs={{12,0},{16,4},{20,8},{24,12},{28,16},{32,20},{36,24},{40,28},{44,3... | collective-permute-start | bytes 196616 | tf_op jit(solution)/shard_map/ppermute | solution.py:16
  409.0 7.3 %collective-permute-start.9 = (bf16[2,128,1,128]{3,1,0,2:T(8,128)(2,1)S(1)}, bf16[2,128,1,128]{3,1,0,2:T(8,128)(2,1)S(1)}, u32[]{:S(2)}, u32[]{:S(2)}) collective-permute-start(bf16[2,128,1,128]{3,1,0,2:T(8,128)(2,1)S(1)} %get-tuple-element.87), channel_id=1, source_target_pairs={{8,0},{12,4},{16,8},{20,12},{24,16},{28,20},{32,24},{36,28},{40,32... | collective-permute-start | bytes 196616 | tf_op jit(solution)/shard_map/ppermute | solution.py:16
  411.1 5.6 %collective-permute-start.8 = (bf16[2,128,1,128]{3,1,0,2:T(8,128)(2,1)S(1)}, bf16[2,128,1,128]{3,1,0,2:T(8,128)(2,1)S(1)}, u32[]{:S(2)}, u32[]{:S(2)}) collective-permute-start(bf16[2,128,1,128]{3,1,0,2:T(8,128)(2,1)S(1)} %get-tuple-element.81), channel_id=1, source_target_pairs={{4,0},{8,4},{12,8},{16,12},{20,16},{24,20},{28,24},{32,28},{36,32}... | collective-permute-start | bytes 196616 | tf_op jit(solution)/shard_map/ppermute | solution.py:16
  (17 other events, 266.5 us)
Sparse Core Ops, SparseCore 0:
  11.0 184.1 all-gather.2
  251.8 32.9 reduce-scatter.3
  338.1 21.2 all-gather.4

commit v3 on v1

--- a/solution.py
+++ b/solution.py
@@ -74,14 +74,24 @@
     before = jnp.dot(earlier, per_token, precision=highest)
     rank = jnp.sum(hits * before[:, None, :], axis=2).astype(jnp.int32)
     target = expert_ids * capacity + rank
-    placed = (
-        target[None, :, :] == jnp.arange(experts * capacity, dtype=jnp.int32)[:, None, None]
-    ).astype(jnp.float32)
-    pick = jnp.sum(placed, axis=2).astype(jnp.bfloat16)
-    send_rows = jnp.dot(pick, out_grad, preferred_element_type=jnp.float32).astype(jnp.bfloat16)
-    send_weight = jnp.sum(placed * weights[None, :, :], axis=(1, 2)).astype(jnp.bfloat16)
-    weight_lanes = jnp.zeros((experts * capacity, 128), jnp.bfloat16).at[:, 0].set(send_weight)
-    payload = jnp.concatenate([send_rows, weight_lanes], axis=1)
+    pad = -(-(capacity + 1) // 16) * 16
+    padded_target = (expert_ids * pad + rank).reshape(-1)
+    onehot = padded_target[None, :] == jnp.arange(experts * pad, dtype=jnp.int32)[:, None]
+    token_of = (
+        jnp.arange(tokens_here * top_count, dtype=jnp.int32)[:, None] // top_count
+        == jnp.arange(tokens_here, dtype=jnp.int32)[None, :]
+    ).astype(jnp.bfloat16)
+    pick = jnp.dot(
+        onehot.astype(jnp.bfloat16), token_of, preferred_element_type=jnp.float32
+    ).astype(jnp.bfloat16)
+    send_rows = jnp.dot(pick, out_grad, preferred_element_type=jnp.float32)
+    send_weight = jnp.sum(jnp.where(onehot, weights.reshape(-1)[None, :], 0.0), axis=1)
+    weight_plane = (
+        jnp.zeros((experts, pad, features), jnp.float32)
+        .at[:, capacity, :pad]
+        .set(send_weight.reshape(experts, pad))
+    )
+    payload = (send_rows.reshape(experts, pad, features) + weight_plane).astype(jnp.bfloat16)
     weight_full = lax.all_gather(out_weight, "seq", axis=1, tiled=True)
     kv_heads = key.shape[1]
     head_dim = key.shape[2]
@@ -90,18 +100,12 @@
     blocks = [paired]
     for distance in range(1, REACH + 1):
         blocks.append(passed_along(paired, "seq", distance))
-    sent_payload = lax.all_to_all(
-        payload.reshape(experts, capacity, features + 128),
-        "seq",
-        split_axis=0,
-        concat_axis=0,
-        tiled=True,
-    ).reshape(slots_all, features + 128)
+    sent_payload = lax.all_to_all(payload, "seq", split_axis=0, concat_axis=0, tiled=True)
     sent_payload, weight_full, blocks = lax.optimization_barrier(
         (sent_payload, weight_full, tuple(blocks))
     )
-    slot_rows = sent_payload[:, :features]
-    sent_weight = sent_payload[:, features]
+    slot_rows = sent_payload[:, :capacity, :].reshape(slots_all, features)
+    sent_weight = sent_payload[:, capacity, :capacity].reshape(slots_all)
     weight_here = w_down[0]
     raw = lax.psum_scatter(
         lax.dot_general(

time: 406 us -> 390 us (0.961)
  waiting for transfers between devices: 167 us -> 154 us
  other arithmetic: 29.2 us -> 22.9 us
  matrix products: 23.8 us -> 30 us
    ppermute x14, waiting for transfers between devices: 101 us -> 87.8 us  [passed_along(): return lax.ppermute(array, axis, pairs)]
    reduce_sum x1, other arithmetic: 11.6 us -> 0.93 us  [per_device(): jnp.sum(jnp.where(onehot, weights.reshape(-1)[None, :], 0.0), axis=1)]
    dot_general x1, matrix products: 1.98 us -> 8.33 us  [per_device(): send_rows = jnp.dot(pick, out_grad, preferred_element_type=jnp.float32)]
    add x0 -> x2, local copies, waits for them, and re-layouts: none -> 6.13 us  [the longest x1 6.02 us: per_device(): send_rows.reshape(experts, pad, features) + weight_plane]
    convert_element_type x0 -> x1, other arithmetic: none -> 6.08 us  [per_device(): (send_rows.reshape(experts, pad, features) + weight_plane).astype(jnp.bfl...]
    reshape x2, local copies, waits for them, and re-layouts: 13.2 us -> 7.25 us  [the longest x1 6.15 us: per_device(): slot_rows = sent_payload[:, :capacity, :].reshape(slots_all, features)]
    concatenate x1 -> x0, local copies, waits for them, and re-layouts: 5.82 us -> none  [per_device(): payload = jnp.concatenate([send_rows, weight_lanes], axis=1)]
    unnamed x77 -> x65, local copies, waits for them, and re-layouts: 12.3 us -> 13.7 us
  transfers between devices with their start and end apart: 19 -> 19, of which waited for: 7 -> 8; matrix products, arithmetic and copies ran while one was open for 12% -> 10% of each run, Pallas kernels for 0% -> 0%
where the time goes in v3:
time: 390 us; the launch traced here: 389 us
  waiting for transfers between devices  154 us (39%)
  starting transfers between devices  114 us (29%)
  local copies, waits for them, and re-layouts  40.7 us (10%)
  matrix products  30 us (8%)
  other arithmetic  22.9 us (6%)
  between operations  14.6 us (4%)
  blocking collectives  12.9 us (3%)
    ppermute x14, waiting for transfers between devices, passed_along(): return lax.ppermute(array, axis, pairs)  87.8 us
    ppermute x14, starting transfers between devices, passed_along(): return lax.ppermute(array, axis, pairs)  77 us
    unnamed x4, waiting for transfers between devices  30.5 us
    all_to_all x1, starting transfers between devices, per_device(): lax.all_to_all(slot_grad.reshape(seq_count, capacity), 'seq', split_axis=...  18.3 us
    all_to_all x1, starting transfers between devices, per_device(): lax.all_to_all(payload, 'seq', split_axis=0, concat_axis=0, tiled=True)  18.2 us
    all_gather x1, waiting for transfers between devices, per_device(): input_grad = lax.all_gather(input_slice, 'head', axis=1, tiled=True)  16.8 us
    unnamed x65, local copies, waits for them, and re-layouts  13.7 us
    psum x1, blocking collectives, per_device(): slot_grad = lax.psum(slot_part, 'head')  12.9 us
  transfers between devices with their start and end apart: 19, of which 8 were waited for; matrix products, arithmetic and copies ran while one was open for 10% of the time, Pallas kernels for 0%

profile of v3, /device:TPU:49, one launch (start us, length us, event | category | flops | bytes accessed | tf_op | source)
XLA Modules:
  0.0 388.8 jit_solution(8672951283829105998)
XLA Ops:
  13.8 8.3 %fusion.22 = f32[2048,1024]{1,0:T(8,128)} fusion(bf16[128,1024]{1,0:T(8,128)(2,1)} %param.13, s32[1024]{0:T(1024)S(1)} %eq.44, s32[1024]{0:T(1024)S(1)} %add_select_fusion), kind=kOutput, calls=%fused_computation.42 | convolution fusion | flops 1076232192 | bytes 8658944 | tf_op jit(solution)/shard_map/dot_general | solution.py:87
  23.2 6.0 %add.136 = f32[128,16,1024]{2,1,0:T(8,128)} dynamic-update-slice(f32[128,16,1024]{2,1,0:T(8,128)} %bitcast.180, f32[128,1,16]{2,1,0:T(1,128)S(1)} %bitcast.187, s32[]{:T(128)} %constant.90.clone.1, s32[]{:T(128)} %constant.94.clone.1, s32[]{:T(128)} %constant.90.clone.1) | dynamic-update-slice | bytes 16388 | tf_op jit(solution)/shard_map/add | solution.py:94
  29.3 6.1 %convert_element_type.215 = bf16[128,16,1024]{2,1,0:T(8,128)(2,1)} convert(f32[128,16,1024]{2,1,0:T(8,128)} %add.136) | non-fusion elementwise | flops 2097152 | bytes 12582912 | tf_op jit(solution)/shard_map/convert_element_type | solution.py:94
  35.3 18.2 %all-to-all-start = ((bf16[128,16,1024]{2,1,0:T(8,128)(2,1)}), bf16[128,16,1024]{2,1,0:T(8,128)(2,1)}, u32[]{:S(2)}, u32[]{:S(2)}) async-start(bf16[128,16,1024]{2,1,0:T(8,128)(2,1)} %convert_element_type.215), calls=%async_computation | async-start | bytes 8388608 | tf_op jit(solution)/shard_map/all_to_all | solution.py:103
  53.6 3.4 collective-permute-start
  57.0 3.1 collective-permute-start.1
  60.1 3.2 collective-permute-start.2
  63.3 4.3 %collective-permute-start.3 = (bf16[2,128,1,128]{3,1,2,0:T(8,128)(2,1)S(1)}, bf16[2,128,1,128]{3,1,2,0:T(8,128)(2,1)S(1)}, u32[]{:S(2)}, u32[]{:S(2)}) collective-permute-start(bf16[2,128,1,128]{3,1,2,0:T(8,128)(2,1)S(1)} %pad_maximum_fusion.2), channel_id=1, source_target_pairs={{0,16},{4,20},{8,24},{12,28},{16,32},{20,36},{24,40},{28,44},{32,4... | collective-permute-start | bytes 196616 | tf_op jit(solution)/shard_map/ppermute | solution.py:16
  67.7 2.6 collective-permute-start.4
  70.3 75.1 %collective-permute-done = bf16[2,128,1,128]{3,1,2,0:T(8,128)(2,1)S(1)} collective-permute-done((bf16[2,128,1,128]{3,1,2,0:T(8,128)(2,1)S(1)}, bf16[2,128,1,128]{3,1,2,0:T(8,128)(2,1)S(1)}, u32[]{:S(2)}, u32[]{:S(2)}) %collective-permute-start) | collective-permute-done | bytes 65568 | tf_op jit(solution)/shard_map/ppermute | solution.py:16
  147.4 9.7 %collective-permute-done.1 = bf16[2,128,1,128]{3,1,2,0:T(8,128)(2,1)S(1)} collective-permute-done((bf16[2,128,1,128]{3,1,2,0:T(8,128)(2,1)S(1)}, bf16[2,128,1,128]{3,1,2,0:T(8,128)(2,1)S(1)}, u32[]{:S(2)}, u32[]{:S(2)}) %collective-permute-start.1) | collective-permute-done | bytes 65568 | tf_op jit(solution)/shard_map/ppermute | solution.py:16
  157.0 29.2 %collective-permute-start.6 = (bf16[2,128,1,128]{3,1,2,0:T(8,128)(2,1)S(1)}, bf16[2,128,1,128]{3,1,2,0:T(8,128)(2,1)}, u32[]{:S(2)}, u32[]{:S(2)}) collective-permute-start(bf16[2,128,1,128]{3,1,2,0:T(8,128)(2,1)S(1)} %pad_maximum_fusion.2), channel_id=1, source_target_pairs={{0,28},{4,32},{8,36},{12,40},{16,44},{20,48},{24,52},{28,56},{32,6... | collective-permute-start | bytes 196616 | tf_op jit(solution)/shard_map/ppermute | solution.py:16
  188.6 10.8 %all-gather.3.cloned.1.call-done = bf16[1024,4096]{0,1:T(8,128)(2,1)} async-done(((bf16[1024,32]{0,1:T(8,128)(2,1)}), bf16[1024,4096]{0,1:T(8,128)(2,1)}) %all-gather.3.cloned.1.call-update) | async-done | bytes 8388624 | tf_op jit(solution)/shard_map/all_gather | solution.py:95
  199.4 6.1 %reshape.440 = bf16[1536,1024]{1,0:T(8,128)(2,1)} reshape(bf16[128,12,1024]{2,1,0:T(8,128)(2,1)} %bitcast.178) | data formatting | bytes 6291456 | tf_op jit(solution)/shard_map/reshape | solution.py:107
  205.5 6.0 %fusion.8 = bf16[768,1536]{0,1:T(8,128)(2,1)} fusion(bf16[1536,1024]{1,0:T(8,128)(2,1)} %reshape.440, bf16[1,768,1024]{2,1,0:T(8,128)(2,1)S(1)} %copy-done), kind=kOutput, calls=%fused_computation.16 | convolution fusion | flops 2417098752 | bytes 7077888 | tf_op jit(solution)/shard_map/dot_general | solution.py:111
  211.5 4.4 %copy.132 = bf16[768,1536]{1,0:T(8,128)(2,1)} copy(bf16[768,1536]{0,1:T(8,128)(2,1)} %fusion.8) | data formatting | bytes 4718592
  219.1 29.8 %reduce-scatter.4.cloned.1.call-done = bf16[192,1536]{1,0:T(8,128)(2,1)} async-done(((bf16[768,1536]{1,0:T(8,128)(2,1)}), bf16[192,1536]{1,0:T(8,128)(2,1)}) %reduce-scatter.4.cloned.1.call-update) | async-done | bytes 589840
  250.2 2.3 fusion.13
  252.7 12.9 %psum.7 = f32[128,1,12]{2,0,1:T(8,128)} all-reduce(f32[128,1,12]{2,0,1:T(8,128)S(1)} %all_to_all.10), channel_id=1, replica_groups=mesh['seq'=128,'head'=4] {'head'}, use_global_device_ids=true, to_apply=%region_7.8 | all-reduce | flops 1536 | bytes 12288 | tf_op jit(solution)/shard_map/psum | solution.py:128
  265.6 18.3 %all-to-all-start.1 = ((f32[128,1,12]{2,1,0:T(1,128)}), f32[128,1,12]{2,1,0:T(1,128)S(1)}, u32[]{:S(2)}, u32[]{:S(2)}) async-start(f32[128,1,12]{2,1,0:T(1,128)} %bitcast.12), calls=%async_computation.1 | async-start | bytes 131072 | tf_op jit(solution)/shard_map/all_to_all | solution.py:129
  284.2 8.0 %all-to-all-done.1 = f32[128,1,12]{2,1,0:T(1,128)S(1)} async-done(((f32[128,1,12]{2,1,0:T(1,128)}), f32[128,1,12]{2,1,0:T(1,128)S(1)}, u32[]{:S(2)}, u32[]{:S(2)}) %all-to-all-start.1) | async-done | bytes 6176 | tf_op jit(solution)/shard_map/all_to_all | solution.py:129
  293.6 6.2 %gather_fusion = f32[1024]{0:T(1024)S(1)} fusion(f32[1536]{0:T(1024)S(1)} %reshape.441, s32[1024]{0:T(1024)S(1)} %broadcast_clamp_fusion), kind=kCustom, calls=%fused_computation | custom fusion | bytes 12288 | tf_op jit(solution)/shard_map/jit(_take)/gather | solution.py:132
  306.5 16.8 %all-gather.5.cloned.1.call-done = bf16[128,4096]{1,0:T(8,128)(2,1)} async-done(((bf16[128,1024]{1,0:T(8,128)(2,1)}), bf16[128,4096]{1,0:T(8,128)(2,1)}) %all-gather.5.cloned.1.call-update) | async-done | bytes 1048592 | tf_op jit(solution)/shard_map/all_gather | solution.py:137
  323.3 5.1 %convolution_convert_fusion.1 = bf16[128,1024]{1,0:T(8,128)(2,1)S(1)} fusion(bf16[128,4096]{1,0:T(8,128)(2,1)} %all-gather.5.cloned.1.call-done, bf16[1024,4096]{0,1:T(8,128)(2,1)} %all-gather.3.cloned.1.call-done), kind=kOutput, calls=%fused_computation.48 | convolution fusion | flops 1073872896 | bytes 9699328 | tf_op jit(solution)/shard_map/dot_general | solution.py:138
  329.7 3.4 convert_bitcast_fusion
  333.1 4.2 %copy.120 = bf16[8,128,1024]{2,0,1:T(8,128)(2,1)} copy(bf16[8,128,1024]{1,2,0:T(8,128)(2,1)} %get-tuple-element.64) | data formatting | bytes 4194304 | tf_op jit(solution)/shard_map/reshape.71
  339.7 2.5 fusion.23
  343.0 7.2 %collective-permute-start.10 = (bf16[2,128,1,128]{3,1,0,2:T(8,128)(2,1)}, bf16[2,128,1,128]{3,1,0,2:T(8,128)(2,1)}, u32[]{:S(2)}, u32[]{:S(2)}) collective-permute-start(bf16[2,128,1,128]{3,1,0,2:T(8,128)(2,1)} %get-tuple-element.75), channel_id=1, source_target_pairs={{16,0},{20,4},{24,8},{28,12},{32,16},{36,20},{40,24},{44,28},{48,3... | collective-permute-start | bytes 196616 | tf_op jit(solution)/shard_map/ppermute | solution.py:16
  350.2 5.4 %collective-permute-start.11 = (bf16[2,128,1,128]{3,1,0,2:T(8,128)(2,1)S(1)}, bf16[2,128,1,128]{3,1,0,2:T(8,128)(2,1)}, u32[]{:S(2)}, u32[]{:S(2)}) collective-permute-start(bf16[2,128,1,128]{3,1,0,2:T(8,128)(2,1)S(1)} %get-tuple-element.74), channel_id=1, source_target_pairs={{20,0},{24,4},{28,8},{32,12},{36,16},{40,20},{44,24},{48,28},{52,3... | collective-permute-start | bytes 196616 | tf_op jit(solution)/shard_map/ppermute | solution.py:16
  360.8 6.2 %collective-permute-start.13 = (bf16[2,128,1,128]{3,1,2,0:T(8,128)(2,1)S(1)}, bf16[2,128,1,128]{3,1,2,0:T(8,128)(2,1)S(1)}, u32[]{:S(2)}, u32[]{:S(2)}) collective-permute-start(bf16[2,128,1,128]{3,1,2,0:T(8,128)(2,1)S(1)} %get-tuple-element.72), channel_id=1, source_target_pairs={{28,0},{32,4},{36,8},{40,12},{44,16},{48,20},{52,24},{56,28},{60,3... | collective-permute-start | bytes 196616 | tf_op jit(solution)/shard_map/ppermute | solution.py:16
  367.0 3.5 collective-permute-start.7
  370.5 2.9 collective-permute-start.8
  (144 shorter events, 43.1 us)
Async XLA Ops:
  7.2 198.4 %copy-start = (bf16[1,768,1024]{2,1,0:T(8,128)(2,1)S(1)}, bf16[1,768,1024]{2,1,0:T(8,128)(2,1)}, u32[]{:S(2)}) copy-start(bf16[1,768,1024]{2,1,0:T(8,128)(2,1)} %param.18) | copy-start | bytes 4718596
  7.2 192.2 %all-gather.3.cloned.1.call-start = ((), (), s32[]{:S(2)}) async-start(), calls=%async_computation.3 | async-start | bytes 8454144 | tf_op jit(solution)/shard_map/all_gather | solution.py:95
  35.3 153.3 %all-to-all-start = ((bf16[128,16,1024]{2,1,0:T(8,128)(2,1)}), bf16[128,16,1024]{2,1,0:T(8,128)(2,1)}, u32[]{:S(2)}, u32[]{:S(2)}) async-start(bf16[128,16,1024]{2,1,0:T(8,128)(2,1)} %convert_element_type.215), calls=%async_computation | async-start | bytes 8388608 | tf_op jit(solution)/shard_map/all_to_all | solution.py:103
  53.5 195.3 %reduce-scatter.4.cloned.1.call-start = ((), (), s32[]{:S(2)}) async-start(), calls=%async_computation.5 | async-start | bytes 2949120
  53.6 91.8 %collective-permute-start = (bf16[2,128,1,128]{3,1,2,0:T(8,128)(2,1)S(1)}, bf16[2,128,1,128]{3,1,2,0:T(8,128)(2,1)S(1)}, u32[]{:S(2)}, u32[]{:S(2)}) collective-permute-start(bf16[2,128,1,128]{3,1,2,0:T(8,128)(2,1)S(1)} %pad_maximum_fusion.2), channel_id=1, source_target_pairs={{0,4},{4,8},{8,12},{12,16},{16,20},{20,24},{24,28},{28,32},{32,36}... | collective-permute-start | bytes 196616 | tf_op jit(solution)/shard_map/ppermute | solution.py:16
  57.0 100.1 %collective-permute-start.1 = (bf16[2,128,1,128]{3,1,2,0:T(8,128)(2,1)S(1)}, bf16[2,128,1,128]{3,1,2,0:T(8,128)(2,1)S(1)}, u32[]{:S(2)}, u32[]{:S(2)}) collective-permute-start(bf16[2,128,1,128]{3,1,2,0:T(8,128)(2,1)S(1)} %pad_maximum_fusion.2), channel_id=1, source_target_pairs={{0,8},{4,12},{8,16},{12,20},{16,24},{20,28},{24,32},{28,36},{32,40... | collective-permute-start | bytes 196616 | tf_op jit(solution)/shard_map/ppermute | solution.py:16
  60.1 126.1 %collective-permute-start.2 = (bf16[2,128,1,128]{3,1,2,0:T(8,128)(2,1)S(1)}, bf16[2,128,1,128]{3,1,2,0:T(8,128)(2,1)S(1)}, u32[]{:S(2)}, u32[]{:S(2)}) collective-permute-start(bf16[2,128,1,128]{3,1,2,0:T(8,128)(2,1)S(1)} %pad_maximum_fusion.2), channel_id=1, source_target_pairs={{0,12},{4,16},{8,20},{12,24},{16,28},{20,32},{24,36},{28,40},{32,4... | collective-permute-start | bytes 196616 | tf_op jit(solution)/shard_map/ppermute | solution.py:16
  63.3 122.9 %collective-permute-start.3 = (bf16[2,128,1,128]{3,1,2,0:T(8,128)(2,1)S(1)}, bf16[2,128,1,128]{3,1,2,0:T(8,128)(2,1)S(1)}, u32[]{:S(2)}, u32[]{:S(2)}) collective-permute-start(bf16[2,128,1,128]{3,1,2,0:T(8,128)(2,1)S(1)} %pad_maximum_fusion.2), channel_id=1, source_target_pairs={{0,16},{4,20},{8,24},{12,28},{16,32},{20,36},{24,40},{28,44},{32,4... | collective-permute-start | bytes 196616 | tf_op jit(solution)/shard_map/ppermute | solution.py:16
  67.7 118.6 %collective-permute-start.4 = (bf16[2,128,1,128]{3,1,2,0:T(8,128)(2,1)S(1)}, bf16[2,128,1,128]{3,1,2,0:T(8,128)(2,1)S(1)}, u32[]{:S(2)}, u32[]{:S(2)}) collective-permute-start(bf16[2,128,1,128]{3,1,2,0:T(8,128)(2,1)S(1)} %pad_maximum_fusion.2), channel_id=1, source_target_pairs={{0,20},{4,24},{8,28},{12,32},{16,36},{20,40},{24,44},{28,48},{32,5... | collective-permute-start | bytes 196616 | tf_op jit(solution)/shard_map/ppermute | solution.py:16
  145.4 40.8 %collective-permute-start.5 = (bf16[2,128,1,128]{3,1,2,0:T(8,128)(2,1)S(1)}, bf16[2,128,1,128]{3,1,2,0:T(8,128)(2,1)S(1)}, u32[]{:S(2)}, u32[]{:S(2)}) collective-permute-start(bf16[2,128,1,128]{3,1,2,0:T(8,128)(2,1)S(1)} %pad_maximum_fusion.2), channel_id=1, source_target_pairs={{0,24},{4,28},{8,32},{12,36},{16,40},{20,44},{24,48},{28,52},{32,5... | collective-permute-start | bytes 196616 | tf_op jit(solution)/shard_map/ppermute | solution.py:16
  157.0 29.3 %copy-start.12 = (bf16[2,128,1,128]{3,1,2,0:T(8,128)(2,1)}, bf16[2,128,1,128]{3,1,2,0:T(8,128)(2,1)S(1)}, u32[]{:S(2)}) copy-start(bf16[2,128,1,128]{3,1,2,0:T(8,128)(2,1)S(1)} %collective-permute-done.1) | copy-start | bytes 196612
  157.0 31.6 %collective-permute-start.6 = (bf16[2,128,1,128]{3,1,2,0:T(8,128)(2,1)S(1)}, bf16[2,128,1,128]{3,1,2,0:T(8,128)(2,1)}, u32[]{:S(2)}, u32[]{:S(2)}) collective-permute-start(bf16[2,128,1,128]{3,1,2,0:T(8,128)(2,1)S(1)} %pad_maximum_fusion.2), channel_id=1, source_target_pairs={{0,28},{4,32},{8,36},{12,40},{16,44},{20,48},{24,52},{28,56},{32,6... | collective-permute-start | bytes 196616 | tf_op jit(solution)/shard_map/ppermute | solution.py:16
  250.2 49.7 %copy-start.11 = (f32[128,8]{0,1:T(8,128)S(1)}, f32[128,8]{0,1:T(8,128)}, u32[]{:S(2)}) copy-start(f32[128,8]{0,1:T(8,128)} %param.15) | copy-start | bytes 12292
  250.2 50.5 %copy-start.7 = (bf16[128,1024]{1,0:T(8,128)(2,1)S(1)}, bf16[128,1024]{1,0:T(8,128)(2,1)}, u32[]{:S(2)}) copy-start(bf16[128,1024]{1,0:T(8,128)(2,1)} %param.13) | copy-start | bytes 786436
  250.2 50.5 %copy-start.10 = (bf16[128,1024]{1,0:T(8,128)(2,1)S(1)}, bf16[128,1024]{1,0:T(8,128)(2,1)}, u32[]{:S(2)}) copy-start(bf16[128,1024]{1,0:T(8,128)(2,1)} %param.17) | copy-start | bytes 786436
  252.6 50.1 %copy-start.21 = (bf16[2,128,1,128]{3,1,2,0:T(8,128)(2,1)S(1)}, bf16[2,128,1,128]{3,1,2,0:T(8,128)(2,1)}, u32[]{:S(2)}) copy-start(bf16[2,128,1,128]{3,1,2,0:T(8,128)(2,1)} %copy-done.20) | copy-start | bytes 196612
  252.6 50.1 %copy-start.19 = (bf16[2,128,1,128]{3,1,2,0:T(8,128)(2,1)S(1)}, bf16[2,128,1,128]{3,1,2,0:T(8,128)(2,1)}, u32[]{:S(2)}) copy-start(bf16[2,128,1,128]{3,1,2,0:T(8,128)(2,1)} %copy-done.18) | copy-start | bytes 196612
  252.6 50.2 %copy-start.17 = (bf16[2,128,1,128]{3,1,2,0:T(8,128)(2,1)S(1)}, bf16[2,128,1,128]{3,1,2,0:T(8,128)(2,1)}, u32[]{:S(2)}) copy-start(bf16[2,128,1,128]{3,1,2,0:T(8,128)(2,1)} %copy-done.16) | copy-start | bytes 196612
  252.6 50.2 %copy-start.15 = (bf16[2,128,1,128]{3,1,2,0:T(8,128)(2,1)S(1)}, bf16[2,128,1,128]{3,1,2,0:T(8,128)(2,1)}, u32[]{:S(2)}) copy-start(bf16[2,128,1,128]{3,1,2,0:T(8,128)(2,1)} %copy-done.14) | copy-start | bytes 196612
  252.6 50.2 %copy-start.13 = (bf16[2,128,1,128]{3,1,2,0:T(8,128)(2,1)S(1)}, bf16[2,128,1,128]{3,1,2,0:T(8,128)(2,1)}, u32[]{:S(2)}) copy-start(bf16[2,128,1,128]{3,1,2,0:T(8,128)(2,1)} %copy-done.12) | copy-start | bytes 196612
  252.6 50.3 %copy-start.8 = (bf16[128,8,128]{2,1,0:T(8,128)(2,1)S(1)}, bf16[128,8,128]{2,1,0:T(8,128)(2,1)}, u32[]{:S(2)}) copy-start(bf16[128,8,128]{2,1,0:T(8,128)(2,1)} %param.21) | copy-start | bytes 786436
  265.6 26.6 %all-to-all-start.1 = ((f32[128,1,12]{2,1,0:T(1,128)}), f32[128,1,12]{2,1,0:T(1,128)S(1)}, u32[]{:S(2)}, u32[]{:S(2)}) async-start(f32[128,1,12]{2,1,0:T(1,128)} %bitcast.12), calls=%async_computation.1 | async-start | bytes 131072 | tf_op jit(solution)/shard_map/all_to_all | solution.py:129
  284.0 39.3 %all-gather.5.cloned.1.call-start = ((), (), s32[]{:S(2)}) async-start(), calls=%async_computation.4 | async-start | bytes 1310720 | tf_op jit(solution)/shard_map/all_gather | solution.py:137
  302.9 25.5 %copy-start.9 = (bf16[2,1024,1,128]{3,1,2,0:T(8,128)(2,1)}, bf16[2,1024,1,128]{3,1,2,0:T(8,128)(2,1)S(1)}, u32[]{:S(2)}) copy-start(bf16[2,1024,1,128]{3,1,2,0:T(8,128)(2,1)S(1)} %constant_dynamic-update-slice_fusion) | copy-start | bytes 1572868
  343.0 27.5 %collective-permute-start.10 = (bf16[2,128,1,128]{3,1,0,2:T(8,128)(2,1)}, bf16[2,128,1,128]{3,1,0,2:T(8,128)(2,1)}, u32[]{:S(2)}, u32[]{:S(2)}) collective-permute-start(bf16[2,128,1,128]{3,1,0,2:T(8,128)(2,1)} %get-tuple-element.75), channel_id=1, source_target_pairs={{16,0},{20,4},{24,8},{28,12},{32,16},{36,20},{40,24},{44,28},{48,3... | collective-permute-start | bytes 196616 | tf_op jit(solution)/shard_map/ppermute | solution.py:16
  350.2 23.3 %collective-permute-start.11 = (bf16[2,128,1,128]{3,1,0,2:T(8,128)(2,1)S(1)}, bf16[2,128,1,128]{3,1,0,2:T(8,128)(2,1)}, u32[]{:S(2)}, u32[]{:S(2)}) collective-permute-start(bf16[2,128,1,128]{3,1,0,2:T(8,128)(2,1)S(1)} %get-tuple-element.74), channel_id=1, source_target_pairs={{20,0},{24,4},{28,8},{32,12},{36,16},{40,20},{44,24},{48,28},{52,3... | collective-permute-start | bytes 196616 | tf_op jit(solution)/shard_map/ppermute | solution.py:16
  355.6 26.7 %copy-start.1 = (bf16[1,768,1024]{2,1,0:T(8,128)(2,1)S(1)}, bf16[1,768,1024]{2,1,0:T(8,128)(2,1)}, u32[]{:S(2)}) copy-start(bf16[1,768,1024]{2,1,0:T(8,128)(2,1)} %param.18) | copy-start | bytes 4718596
  358.9 19.8 %collective-permute-start.12 = (bf16[2,128,1,128]{3,1,0,2:T(8,128)(2,1)S(1)}, bf16[2,128,1,128]{3,1,0,2:T(8,128)(2,1)S(1)}, u32[]{:S(2)}, u32[]{:S(2)}) collective-permute-start(bf16[2,128,1,128]{3,1,0,2:T(8,128)(2,1)S(1)} %get-tuple-element.73), channel_id=1, source_target_pairs={{24,0},{28,4},{32,8},{36,12},{40,16},{44,20},{48,24},{52,28},{56,3... | collective-permute-start | bytes 196616 | tf_op jit(solution)/shard_map/ppermute | solution.py:16
  360.8 17.9 %collective-permute-start.13 = (bf16[2,128,1,128]{3,1,2,0:T(8,128)(2,1)S(1)}, bf16[2,128,1,128]{3,1,2,0:T(8,128)(2,1)S(1)}, u32[]{:S(2)}, u32[]{:S(2)}) collective-permute-start(bf16[2,128,1,128]{3,1,2,0:T(8,128)(2,1)S(1)} %get-tuple-element.72), channel_id=1, source_target_pairs={{28,0},{32,4},{36,8},{40,12},{44,16},{48,20},{52,24},{56,28},{60,3... | collective-permute-start | bytes 196616 | tf_op jit(solution)/shard_map/ppermute | solution.py:16
  367.0 11.7 %collective-permute-start.7 = (bf16[2,128,1,128]{3,1,0,2:T(8,128)(2,1)S(1)}, bf16[2,128,1,128]{3,1,0,2:T(8,128)(2,1)S(1)}, u32[]{:S(2)}, u32[]{:S(2)}) collective-permute-start(bf16[2,128,1,128]{3,1,0,2:T(8,128)(2,1)S(1)} %get-tuple-element.71), channel_id=1, source_target_pairs={{4,0},{8,4},{12,8},{16,12},{20,16},{24,20},{28,24},{32,28},{36,32}... | collective-permute-start | bytes 196616 | tf_op jit(solution)/shard_map/ppermute | solution.py:16
  370.5 8.2 %collective-permute-start.8 = (bf16[2,128,1,128]{3,1,0,2:T(8,128)(2,1)S(1)}, bf16[2,128,1,128]{3,1,0,2:T(8,128)(2,1)S(1)}, u32[]{:S(2)}, u32[]{:S(2)}) collective-permute-start(bf16[2,128,1,128]{3,1,0,2:T(8,128)(2,1)S(1)} %get-tuple-element.77), channel_id=1, source_target_pairs={{8,0},{12,4},{16,8},{20,12},{24,16},{28,20},{32,24},{36,28},{40,32... | collective-permute-start | bytes 196616 | tf_op jit(solution)/shard_map/ppermute | solution.py:16
  373.5 7.2 %collective-permute-start.9 = (bf16[2,128,1,128]{3,1,0,2:T(8,128)(2,1)S(1)}, bf16[2,128,1,128]{3,1,0,2:T(8,128)(2,1)S(1)}, u32[]{:S(2)}, u32[]{:S(2)}) collective-permute-start(bf16[2,128,1,128]{3,1,0,2:T(8,128)(2,1)S(1)} %get-tuple-element.76), channel_id=1, source_target_pairs={{12,0},{16,4},{20,8},{24,12},{28,16},{32,20},{36,24},{40,28},{44,3... | collective-permute-start | bytes 196616 | tf_op jit(solution)/shard_map/ppermute | solution.py:16
  (12 other events, 86.3 us)
Sparse Core Ops, SparseCore 0:
  11.1 188.2 all-gather.2
  216.0 32.7 reduce-scatter.3
  302.0 21.2 all-gather.4

commit v4 on v3

--- a/solution.py
+++ b/solution.py
@@ -14,6 +14,16 @@
     count = lax.axis_size(axis)
     pairs = [(i, i + by) for i in range(count) if 0 <= i + by < count]
     return lax.ppermute(array, axis, pairs)
+
+
+def head_sum(part):
+    count = lax.axis_size("head")
+    step = 1
+    while step < count:
+        pairs = [(i, i ^ step) for i in range(count)]
+        part = part + lax.ppermute(part, "head", pairs)
+        step *= 2
+    return part
 
 
 def attend(queries, upstream, keys_all, values_all, query_pos, key_pos, doc_begin, score_scale):
@@ -86,12 +96,11 @@
     ).astype(jnp.bfloat16)
     send_rows = jnp.dot(pick, out_grad, preferred_element_type=jnp.float32)
     send_weight = jnp.sum(jnp.where(onehot, weights.reshape(-1)[None, :], 0.0), axis=1)
-    weight_plane = (
-        jnp.zeros((experts, pad, features), jnp.float32)
-        .at[:, capacity, :pad]
-        .set(send_weight.reshape(experts, pad))
-    )
-    payload = (send_rows.reshape(experts, pad, features) + weight_plane).astype(jnp.bfloat16)
+    weight_row = jnp.pad(send_weight.reshape(experts, pad), ((0, 0), (0, features - pad)))
+    is_weight = (jnp.arange(pad) == capacity)[None, :, None]
+    payload = jnp.where(
+        is_weight, weight_row[:, None, :], send_rows.reshape(experts, pad, features)
+    ).astype(jnp.bfloat16)
     weight_full = lax.all_gather(out_weight, "seq", axis=1, tiled=True)
     kv_heads = key.shape[1]
     head_dim = key.shape[2]
@@ -125,7 +134,7 @@
     gate_up_grad = jnp.stack([scaled * up * sig * (1.0 + gate * (1.0 - sig)), scaled * act])[
         None
     ].astype(jnp.bfloat16)
-    slot_grad = lax.psum(slot_part, "head")
+    slot_grad = head_sum(slot_part)
     returned = lax.all_to_all(
         slot_grad.reshape(seq_count, capacity), "seq", split_axis=0, concat_axis=0, tiled=True
     )

time: 390 us -> 395 us (1.013)
  waiting for transfers between devices: 154 us -> 168 us
  blocking collectives: 12.9 us -> 0 us
    all_gather x1, waiting for transfers between devices: 10.8 us -> 30.2 us  [per_device(): weight_full = lax.all_gather(out_weight, 'seq', axis=1, tiled=True)]
    psum x1 -> x0, blocking collectives: 12.9 us -> none  [per_device(): slot_grad = lax.psum(slot_part, 'head')]
    add x1 -> x0, local copies, waits for them, and re-layouts: 6.02 us -> none  [per_device(): send_rows.reshape(experts, pad, features) + weight_plane]
    ppermute x14, waiting for transfers between devices: 87.8 us -> 82.3 us  [passed_along(): return lax.ppermute(array, axis, pairs)]
    ppermute x0 -> x2, starting transfers between devices: none -> 5.11 us  [head_sum(): part = part + lax.ppermute(part, 'head', pairs)]
    unnamed x65 -> x69, local copies, waits for them, and re-layouts: 13.7 us -> 18.5 us
    ppermute x0 -> x2, waiting for transfers between devices: none -> 4.14 us  [head_sum(): part = part + lax.ppermute(part, 'head', pairs)]
  transfers between devices with their start and end apart: 19 -> 21, of which waited for: 8 -> 10; matrix products, arithmetic and copies ran while one was open for 10% -> 9% of each run, Pallas kernels for 0% -> 0%
where the time goes in v4:
time: 395 us; the launch traced here: 393 us
  waiting for transfers between devices  168 us (43%)
  starting transfers between devices  117 us (30%)
  local copies, waits for them, and re-layouts  41.8 us (11%)
  matrix products  28.8 us (7%)
  other arithmetic  23 us (6%)
  between operations  14.5 us (4%)
    ppermute x14, waiting for transfers between devices, passed_along(): return lax.ppermute(array, axis, pairs)  82.3 us
    ppermute x14, starting transfers between devices, passed_along(): return lax.ppermute(array, axis, pairs)  75.9 us
    all_gather x1, waiting for transfers between devices, per_device(): weight_full = lax.all_gather(out_weight, 'seq', axis=1, tiled=True)  30.2 us
    unnamed x4, waiting for transfers between devices  29.5 us
    unnamed x69, local copies, waits for them, and re-layouts  18.5 us
    all_to_all x1, starting transfers between devices, per_device(): lax.all_to_all(payload, 'seq', split_axis=0, concat_axis=0, tiled=True)  18.2 us
    all_to_all x1, starting transfers between devices, per_device(): lax.all_to_all(slot_grad.reshape(seq_count, capacity), 'seq', split_axis=...  17.1 us
    all_gather x1, waiting for transfers between devices, per_device(): input_grad = lax.all_gather(input_slice, 'head', axis=1, tiled=True)  14.3 us
  transfers between devices with their start and end apart: 21, of which 10 were waited for; matrix products, arithmetic and copies ran while one was open for 9% of the time, Pallas kernels for 0%

profile of v4, /device:TPU:49, one launch (start us, length us, event | category | flops | bytes accessed | tf_op | source)
XLA Modules:
  0.0 393.3 jit_solution(11854672450621157968)
XLA Ops:
  14.4 7.1 %fusion.22 = bf16[2048,1024]{1,0:T(8,128)(2,1)} fusion(bf16[128,1024]{1,0:T(8,128)(2,1)} %param.11, s32[1024]{0:T(1024)S(1)} %eq.52, s32[1024]{0:T(1024)S(1)} %add_select_fusion), kind=kOutput, calls=%fused_computation.43 | convolution fusion | flops 1076232192 | bytes 4464640 | tf_op jit(solution)/shard_map/dot_general | solution.py:97
  21.4 4.5 %select_convert_fusion = bf16[128,16,1024]{2,1,0:T(8,128)(2,1)} fusion(bf16[128,16,1024]{2,1,0:T(8,128)(2,1)} %bitcast.181, bf16[128,1024]{1,0:T(8,128)(2,1)S(1)} %pad.4, pred[16]{0:T(512)(128)(4,1)S(1)} %iota_compare_fusion.13), kind=kLoop, calls=%fused_computation.1 | loop fusion | flops 2097152 | bytes 8650768 | tf_op jit(solution)/shard_map/convert_element_type | solution.py:103
  26.0 18.2 %all-to-all-start = ((bf16[128,16,1024]{2,1,0:T(8,128)(2,1)}), bf16[128,16,1024]{2,1,0:T(8,128)(2,1)}, u32[]{:S(2)}, u32[]{:S(2)}) async-start(bf16[128,16,1024]{2,1,0:T(8,128)(2,1)} %select_convert_fusion), calls=%async_computation | async-start | bytes 8388608 | tf_op jit(solution)/shard_map/all_to_all | solution.py:112
  44.3 3.4 collective-permute-start
  47.7 3.1 collective-permute-start.1
  50.8 3.2 collective-permute-start.2
  54.0 4.3 %collective-permute-start.3 = (bf16[2,128,1,128]{3,1,2,0:T(8,128)(2,1)S(1)}, bf16[2,128,1,128]{3,1,2,0:T(8,128)(2,1)S(1)}, u32[]{:S(2)}, u32[]{:S(2)}) collective-permute-start(bf16[2,128,1,128]{3,1,2,0:T(8,128)(2,1)S(1)} %pad_maximum_fusion.2), channel_id=1, source_target_pairs={{0,16},{4,20},{8,24},{12,28},{16,32},{20,36},{24,40},{28,44},{32,4... | collective-permute-start | bytes 196616 | tf_op jit(solution)/shard_map/ppermute | solution.py:16
  58.4 2.6 collective-permute-start.4
  61.0 78.7 %collective-permute-done = bf16[2,128,1,128]{3,1,2,0:T(8,128)(2,1)S(1)} collective-permute-done((bf16[2,128,1,128]{3,1,2,0:T(8,128)(2,1)S(1)}, bf16[2,128,1,128]{3,1,2,0:T(8,128)(2,1)S(1)}, u32[]{:S(2)}, u32[]{:S(2)}) %collective-permute-start) | collective-permute-done | bytes 65568 | tf_op jit(solution)/shard_map/ppermute | solution.py:16
  143.4 28.0 %collective-permute-start.6 = (bf16[2,128,1,128]{3,1,2,0:T(8,128)(2,1)S(1)}, bf16[2,128,1,128]{3,1,2,0:T(8,128)(2,1)}, u32[]{:S(2)}, u32[]{:S(2)}) collective-permute-start(bf16[2,128,1,128]{3,1,2,0:T(8,128)(2,1)S(1)} %pad_maximum_fusion.2), channel_id=1, source_target_pairs={{0,28},{4,32},{8,36},{12,40},{16,44},{20,48},{24,52},{28,56},{32,6... | collective-permute-start | bytes 196616 | tf_op jit(solution)/shard_map/ppermute | solution.py:16
  173.4 30.2 %all-gather.3.cloned.1.call-done = bf16[1024,4096]{0,1:T(8,128)(2,1)} async-done(((bf16[1024,32]{0,1:T(8,128)(2,1)}), bf16[1024,4096]{0,1:T(8,128)(2,1)}) %all-gather.3.cloned.1.call-update) | async-done | bytes 8388624 | tf_op jit(solution)/shard_map/all_gather | solution.py:104
  203.6 6.2 %reshape.402 = bf16[1536,1024]{1,0:T(8,128)(2,1)} reshape(bf16[128,12,1024]{2,1,0:T(8,128)(2,1)} %bitcast.176) | data formatting | bytes 6291456 | tf_op jit(solution)/shard_map/reshape | solution.py:116
  209.8 6.0 %fusion.8 = bf16[768,1536]{0,1:T(8,128)(2,1)} fusion(bf16[1536,1024]{1,0:T(8,128)(2,1)} %reshape.402, bf16[1,768,1024]{2,1,0:T(8,128)(2,1)S(1)} %copy-done), kind=kOutput, calls=%fused_computation.17 | convolution fusion | flops 2417098752 | bytes 7077888 | tf_op jit(solution)/shard_map/dot_general | solution.py:120
  215.8 4.3 %copy.125 = bf16[768,1536]{1,0:T(8,128)(2,1)} copy(bf16[768,1536]{0,1:T(8,128)(2,1)} %fusion.8) | data formatting | bytes 4718592
  226.4 28.8 %reduce-scatter.4.cloned.1.call-done = bf16[192,1536]{1,0:T(8,128)(2,1)} async-done(((bf16[768,1536]{1,0:T(8,128)(2,1)}), bf16[192,1536]{1,0:T(8,128)(2,1)}) %reduce-scatter.4.cloned.1.call-update) | async-done | bytes 589840
  255.2 2.2 copy.126
  257.4 3.5 fusion.13
  265.5 3.1 collective-permute-start.8
  268.6 2.8 collective-permute-done.8
  272.1 17.1 %all-to-all-start.1 = ((f32[128,1,12]{2,1,0:T(1,128)}), f32[128,1,12]{2,1,0:T(1,128)S(1)}, u32[]{:S(2)}, u32[]{:S(2)}) async-start(f32[128,1,12]{2,1,0:T(1,128)} %bitcast.11), calls=%async_computation.1 | async-start | bytes 131072 | tf_op jit(solution)/shard_map/all_to_all | solution.py:138
  289.5 8.0 %all-to-all-done.1 = f32[128,1,12]{2,1,0:T(1,128)S(1)} async-done(((f32[128,1,12]{2,1,0:T(1,128)}), f32[128,1,12]{2,1,0:T(1,128)S(1)}, u32[]{:S(2)}, u32[]{:S(2)}) %all-to-all-start.1) | async-done | bytes 6176 | tf_op jit(solution)/shard_map/all_to_all | solution.py:138
  298.9 6.2 %gather_fusion = f32[1024]{0:T(1024)S(1)} fusion(f32[1536]{0:T(1024)S(1)} %reshape.403, s32[1024]{0:T(1024)S(1)} %broadcast_clamp_fusion), kind=kCustom, calls=%fused_computation | custom fusion | bytes 12288 | tf_op jit(solution)/shard_map/jit(_take)/gather | solution.py:141
  314.3 14.3 %all-gather.5.cloned.1.call-done = bf16[128,4096]{1,0:T(8,128)(2,1)} async-done(((bf16[128,1024]{1,0:T(8,128)(2,1)}), bf16[128,4096]{1,0:T(8,128)(2,1)}) %all-gather.5.cloned.1.call-update) | async-done | bytes 1048592 | tf_op jit(solution)/shard_map/all_gather | solution.py:146
  328.6 5.1 %convolution_convert_fusion.1 = bf16[128,1024]{1,0:T(8,128)(2,1)S(1)} fusion(bf16[128,4096]{1,0:T(8,128)(2,1)} %all-gather.5.cloned.1.call-done, bf16[1024,4096]{0,1:T(8,128)(2,1)} %all-gather.3.cloned.1.call-done), kind=kOutput, calls=%fused_computation.49 | convolution fusion | flops 1073872896 | bytes 9699328 | tf_op jit(solution)/shard_map/dot_general | solution.py:147
  335.0 3.5 convert_bitcast_fusion
  338.5 4.2 %copy.113 = bf16[8,128,1024]{2,0,1:T(8,128)(2,1)} copy(bf16[8,128,1024]{1,2,0:T(8,128)(2,1)} %get-tuple-element.52) | data formatting | bytes 4194304 | tf_op jit(solution)/shard_map/reshape.34
  345.1 2.5 fusion.23
  348.3 6.4 %collective-permute-start.10 = (bf16[2,128,1,128]{3,1,0,2:T(8,128)(2,1)}, bf16[2,128,1,128]{3,1,0,2:T(8,128)(2,1)}, u32[]{:S(2)}, u32[]{:S(2)}) collective-permute-start(bf16[2,128,1,128]{3,1,0,2:T(8,128)(2,1)} %get-tuple-element.65), channel_id=1, source_target_pairs={{8,0},{12,4},{16,8},{20,12},{24,16},{28,20},{32,24},{36,28},{40,32... | collective-permute-start | bytes 196616 | tf_op jit(solution)/shard_map/ppermute | solution.py:16
  354.8 4.7 %collective-permute-start.11 = (bf16[2,128,1,128]{3,1,0,2:T(8,128)(2,1)S(1)}, bf16[2,128,1,128]{3,1,0,2:T(8,128)(2,1)}, u32[]{:S(2)}, u32[]{:S(2)}) collective-permute-start(bf16[2,128,1,128]{3,1,0,2:T(8,128)(2,1)S(1)} %get-tuple-element.64), channel_id=1, source_target_pairs={{12,0},{16,4},{20,8},{24,12},{28,16},{32,20},{36,24},{40,28},{44,3... | collective-permute-start | bytes 196616 | tf_op jit(solution)/shard_map/ppermute | solution.py:16
  362.6 3.6 collective-permute-start.12
  368.3 5.4 %collective-permute-start.14 = (bf16[2,128,1,128]{3,1,0,2:T(8,128)(2,1)S(1)}, bf16[2,128,1,128]{3,1,0,2:T(8,128)(2,1)S(1)}, u32[]{:S(2)}, u32[]{:S(2)}) collective-permute-start(bf16[2,128,1,128]{3,1,0,2:T(8,128)(2,1)S(1)} %get-tuple-element.61), channel_id=1, source_target_pairs={{24,0},{28,4},{32,8},{36,12},{40,16},{44,20},{48,24},{52,28},{56,3... | collective-permute-start | bytes 196616 | tf_op jit(solution)/shard_map/ppermute | solution.py:16
  373.7 5.2 %collective-permute-start.15 = (bf16[2,128,1,128]{3,1,2,0:T(8,128)(2,1)S(1)}, bf16[2,128,1,128]{3,1,2,0:T(8,128)(2,1)S(1)}, u32[]{:S(2)}, u32[]{:S(2)}) collective-permute-start(bf16[2,128,1,128]{3,1,2,0:T(8,128)(2,1)S(1)} %get-tuple-element.60), channel_id=1, source_target_pairs={{28,0},{32,4},{36,8},{40,12},{44,16},{48,20},{52,24},{56,28},{60,3... | collective-permute-start | bytes 196616 | tf_op jit(solution)/shard_map/ppermute | solution.py:16
  (152 shorter events, 52.4 us)
Async XLA Ops:
  7.2 202.6 %copy-start = (bf16[1,768,1024]{2,1,0:T(8,128)(2,1)S(1)}, bf16[1,768,1024]{2,1,0:T(8,128)(2,1)}, u32[]{:S(2)}) copy-start(bf16[1,768,1024]{2,1,0:T(8,128)(2,1)} %param.16) | copy-start | bytes 4718596
  7.2 196.5 %all-gather.3.cloned.1.call-start = ((), (), s32[]{:S(2)}) async-start(), calls=%async_computation.3 | async-start | bytes 8454144 | tf_op jit(solution)/shard_map/all_gather | solution.py:104
  26.0 147.4 %all-to-all-start = ((bf16[128,16,1024]{2,1,0:T(8,128)(2,1)}), bf16[128,16,1024]{2,1,0:T(8,128)(2,1)}, u32[]{:S(2)}, u32[]{:S(2)}) async-start(bf16[128,16,1024]{2,1,0:T(8,128)(2,1)} %select_convert_fusion), calls=%async_computation | async-start | bytes 8388608 | tf_op jit(solution)/shard_map/all_to_all | solution.py:112
  44.2 210.9 %reduce-scatter.4.cloned.1.call-start = ((), (), s32[]{:S(2)}) async-start(), calls=%async_computation.5 | async-start | bytes 2949120
  44.3 95.4 %collective-permute-start = (bf16[2,128,1,128]{3,1,2,0:T(8,128)(2,1)S(1)}, bf16[2,128,1,128]{3,1,2,0:T(8,128)(2,1)S(1)}, u32[]{:S(2)}, u32[]{:S(2)}) collective-permute-start(bf16[2,128,1,128]{3,1,2,0:T(8,128)(2,1)S(1)} %pad_maximum_fusion.2), channel_id=1, source_target_pairs={{0,4},{4,8},{8,12},{12,16},{16,20},{20,24},{24,28},{28,32},{32,36}... | collective-permute-start | bytes 196616 | tf_op jit(solution)/shard_map/ppermute | solution.py:16
  47.7 95.8 %collective-permute-start.1 = (bf16[2,128,1,128]{3,1,2,0:T(8,128)(2,1)S(1)}, bf16[2,128,1,128]{3,1,2,0:T(8,128)(2,1)S(1)}, u32[]{:S(2)}, u32[]{:S(2)}) collective-permute-start(bf16[2,128,1,128]{3,1,2,0:T(8,128)(2,1)S(1)} %pad_maximum_fusion.2), channel_id=1, source_target_pairs={{0,8},{4,12},{8,16},{12,20},{16,24},{20,28},{24,32},{28,36},{32,40... | collective-permute-start | bytes 196616 | tf_op jit(solution)/shard_map/ppermute | solution.py:16
  50.8 120.6 %collective-permute-start.2 = (bf16[2,128,1,128]{3,1,2,0:T(8,128)(2,1)S(1)}, bf16[2,128,1,128]{3,1,2,0:T(8,128)(2,1)S(1)}, u32[]{:S(2)}, u32[]{:S(2)}) collective-permute-start(bf16[2,128,1,128]{3,1,2,0:T(8,128)(2,1)S(1)} %pad_maximum_fusion.2), channel_id=1, source_target_pairs={{0,12},{4,16},{8,20},{12,24},{16,28},{20,32},{24,36},{28,40},{32,4... | collective-permute-start | bytes 196616 | tf_op jit(solution)/shard_map/ppermute | solution.py:16
  54.0 117.4 %collective-permute-start.3 = (bf16[2,128,1,128]{3,1,2,0:T(8,128)(2,1)S(1)}, bf16[2,128,1,128]{3,1,2,0:T(8,128)(2,1)S(1)}, u32[]{:S(2)}, u32[]{:S(2)}) collective-permute-start(bf16[2,128,1,128]{3,1,2,0:T(8,128)(2,1)S(1)} %pad_maximum_fusion.2), channel_id=1, source_target_pairs={{0,16},{4,20},{8,24},{12,28},{16,32},{20,36},{24,40},{28,44},{32,4... | collective-permute-start | bytes 196616 | tf_op jit(solution)/shard_map/ppermute | solution.py:16
  58.4 113.1 %collective-permute-start.4 = (bf16[2,128,1,128]{3,1,2,0:T(8,128)(2,1)S(1)}, bf16[2,128,1,128]{3,1,2,0:T(8,128)(2,1)S(1)}, u32[]{:S(2)}, u32[]{:S(2)}) collective-permute-start(bf16[2,128,1,128]{3,1,2,0:T(8,128)(2,1)S(1)} %pad_maximum_fusion.2), channel_id=1, source_target_pairs={{0,20},{4,24},{8,28},{12,32},{16,36},{20,40},{24,44},{28,48},{32,5... | collective-permute-start | bytes 196616 | tf_op jit(solution)/shard_map/ppermute | solution.py:16
  139.8 76.0 %copy-start.10 = (bf16[2,128,1,128]{3,1,2,0:T(8,128)(2,1)}, bf16[2,128,1,128]{3,1,2,0:T(8,128)(2,1)S(1)}, u32[]{:S(2)}) copy-start(bf16[2,128,1,128]{3,1,2,0:T(8,128)(2,1)S(1)} %collective-permute-done) | copy-start | bytes 196612
  139.8 31.7 %collective-permute-start.5 = (bf16[2,128,1,128]{3,1,2,0:T(8,128)(2,1)S(1)}, bf16[2,128,1,128]{3,1,2,0:T(8,128)(2,1)S(1)}, u32[]{:S(2)}, u32[]{:S(2)}) collective-permute-start(bf16[2,128,1,128]{3,1,2,0:T(8,128)(2,1)S(1)} %pad_maximum_fusion.2), channel_id=1, source_target_pairs={{0,24},{4,28},{8,32},{12,36},{16,40},{20,44},{24,48},{28,52},{32,5... | collective-permute-start | bytes 196616 | tf_op jit(solution)/shard_map/ppermute | solution.py:16
  143.4 72.3 %copy-start.12 = (bf16[2,128,1,128]{3,1,2,0:T(8,128)(2,1)}, bf16[2,128,1,128]{3,1,2,0:T(8,128)(2,1)S(1)}, u32[]{:S(2)}) copy-start(bf16[2,128,1,128]{3,1,2,0:T(8,128)(2,1)S(1)} %collective-permute-done.1) | copy-start | bytes 196612
  143.4 30.0 %collective-permute-start.6 = (bf16[2,128,1,128]{3,1,2,0:T(8,128)(2,1)S(1)}, bf16[2,128,1,128]{3,1,2,0:T(8,128)(2,1)}, u32[]{:S(2)}, u32[]{:S(2)}) collective-permute-start(bf16[2,128,1,128]{3,1,2,0:T(8,128)(2,1)S(1)} %pad_maximum_fusion.2), channel_id=1, source_target_pairs={{0,28},{4,32},{8,36},{12,40},{16,44},{20,48},{24,52},{28,56},{32,6... | collective-permute-start | bytes 196616 | tf_op jit(solution)/shard_map/ppermute | solution.py:16
  171.4 44.4 %copy-start.14 = (bf16[2,128,1,128]{3,1,2,0:T(8,128)(2,1)}, bf16[2,128,1,128]{3,1,2,0:T(8,128)(2,1)S(1)}, u32[]{:S(2)}) copy-start(bf16[2,128,1,128]{3,1,2,0:T(8,128)(2,1)S(1)} %collective-permute-done.2) | copy-start | bytes 196612
  257.4 47.8 %copy-start.9 = (f32[128,8]{0,1:T(8,128)S(1)}, f32[128,8]{0,1:T(8,128)}, u32[]{:S(2)}) copy-start(f32[128,8]{0,1:T(8,128)} %param.13) | copy-start | bytes 12292
  257.4 48.6 %copy-start.7 = (bf16[128,1024]{1,0:T(8,128)(2,1)S(1)}, bf16[128,1024]{1,0:T(8,128)(2,1)}, u32[]{:S(2)}) copy-start(bf16[128,1024]{1,0:T(8,128)(2,1)} %param.11) | copy-start | bytes 786436
  260.9 45.1 %copy-start.8 = (bf16[128,1024]{1,0:T(8,128)(2,1)S(1)}, bf16[128,1024]{1,0:T(8,128)(2,1)}, u32[]{:S(2)}) copy-start(bf16[128,1024]{1,0:T(8,128)(2,1)} %param.15) | copy-start | bytes 786436
  260.9 49.7 %copy-start.15 = (bf16[2,128,1,128]{3,1,2,0:T(8,128)(2,1)S(1)}, bf16[2,128,1,128]{3,1,2,0:T(8,128)(2,1)}, u32[]{:S(2)}) copy-start(bf16[2,128,1,128]{3,1,2,0:T(8,128)(2,1)} %copy-done.14) | copy-start | bytes 196612
  260.9 49.7 %copy-start.13 = (bf16[2,128,1,128]{3,1,2,0:T(8,128)(2,1)S(1)}, bf16[2,128,1,128]{3,1,2,0:T(8,128)(2,1)}, u32[]{:S(2)}) copy-start(bf16[2,128,1,128]{3,1,2,0:T(8,128)(2,1)} %copy-done.12) | copy-start | bytes 196612
  260.9 49.7 %copy-start.11 = (bf16[2,128,1,128]{3,1,2,0:T(8,128)(2,1)S(1)}, bf16[2,128,1,128]{3,1,2,0:T(8,128)(2,1)}, u32[]{:S(2)}) copy-start(bf16[2,128,1,128]{3,1,2,0:T(8,128)(2,1)} %copy-done.10) | copy-start | bytes 196612
  260.9 49.7 %copy-start.5 = (bf16[128,8,128]{2,1,0:T(8,128)(2,1)S(1)}, bf16[128,8,128]{2,1,0:T(8,128)(2,1)}, u32[]{:S(2)}) copy-start(bf16[128,8,128]{2,1,0:T(8,128)(2,1)} %param.19) | copy-start | bytes 786436
  260.9 4.5 %collective-permute-start.7 = (f32[1536]{0:T(1024)S(1)}, f32[1536]{0:T(1024)S(1)}, u32[]{:S(2)}, u32[]{:S(2)}) collective-permute-start(f32[1536]{0:T(1024)S(1)} %get-tuple-element.54), channel_id=1, source_target_pairs={{0,1},{1,0},{2,3},{3,2},{4,5},{5,4},{6,7},{7,6},{8,9},{9,8},{10,11... | collective-permute-start | bytes 18440 | tf_op jit(solution)/shard_map/ppermute | solution.py:24
  265.5 5.9 %collective-permute-start.8 = (f32[1536]{0:T(1024)S(1)}, f32[1536]{0:T(1024)S(1)}, u32[]{:S(2)}, u32[]{:S(2)}) collective-permute-start(f32[1536]{0:T(1024)S(1)} %add.141), channel_id=1, source_target_pairs={{0,2},{1,3},{2,0},{3,1},{4,6},{5,7},{6,4},{7,5},{8,10},{9,11},{10,... | collective-permute-start | bytes 18440 | tf_op jit(solution)/shard_map/ppermute | solution.py:24
  272.1 25.4 %all-to-all-start.1 = ((f32[128,1,12]{2,1,0:T(1,128)}), f32[128,1,12]{2,1,0:T(1,128)S(1)}, u32[]{:S(2)}, u32[]{:S(2)}) async-start(f32[128,1,12]{2,1,0:T(1,128)} %bitcast.11), calls=%async_computation.1 | async-start | bytes 131072 | tf_op jit(solution)/shard_map/all_to_all | solution.py:138
  289.3 39.3 %all-gather.5.cloned.1.call-start = ((), (), s32[]{:S(2)}) async-start(), calls=%async_computation.4 | async-start | bytes 1310720 | tf_op jit(solution)/shard_map/all_gather | solution.py:146
  348.3 25.4 %collective-permute-start.10 = (bf16[2,128,1,128]{3,1,0,2:T(8,128)(2,1)}, bf16[2,128,1,128]{3,1,0,2:T(8,128)(2,1)}, u32[]{:S(2)}, u32[]{:S(2)}) collective-permute-start(bf16[2,128,1,128]{3,1,0,2:T(8,128)(2,1)} %get-tuple-element.65), channel_id=1, source_target_pairs={{8,0},{12,4},{16,8},{20,12},{24,16},{28,20},{32,24},{36,28},{40,32... | collective-permute-start | bytes 196616 | tf_op jit(solution)/shard_map/ppermute | solution.py:16
  354.8 24.1 %collective-permute-start.11 = (bf16[2,128,1,128]{3,1,0,2:T(8,128)(2,1)S(1)}, bf16[2,128,1,128]{3,1,0,2:T(8,128)(2,1)}, u32[]{:S(2)}, u32[]{:S(2)}) collective-permute-start(bf16[2,128,1,128]{3,1,0,2:T(8,128)(2,1)S(1)} %get-tuple-element.64), channel_id=1, source_target_pairs={{12,0},{16,4},{20,8},{24,12},{28,16},{32,20},{36,24},{40,28},{44,3... | collective-permute-start | bytes 196616 | tf_op jit(solution)/shard_map/ppermute | solution.py:16
  362.6 21.3 %collective-permute-start.12 = (bf16[2,128,1,128]{3,1,0,2:T(8,128)(2,1)S(1)}, bf16[2,128,1,128]{3,1,0,2:T(8,128)(2,1)S(1)}, u32[]{:S(2)}, u32[]{:S(2)}) collective-permute-start(bf16[2,128,1,128]{3,1,0,2:T(8,128)(2,1)S(1)} %get-tuple-element.63), channel_id=1, source_target_pairs={{16,0},{20,4},{24,8},{28,12},{32,16},{36,20},{40,24},{44,28},{48,3... | collective-permute-start | bytes 196616 | tf_op jit(solution)/shard_map/ppermute | solution.py:16
  366.3 17.7 %collective-permute-start.13 = (bf16[2,128,1,128]{3,1,0,2:T(8,128)(2,1)S(1)}, bf16[2,128,1,128]{3,1,0,2:T(8,128)(2,1)S(1)}, u32[]{:S(2)}, u32[]{:S(2)}) collective-permute-start(bf16[2,128,1,128]{3,1,0,2:T(8,128)(2,1)S(1)} %get-tuple-element.62), channel_id=1, source_target_pairs={{20,0},{24,4},{28,8},{32,12},{36,16},{40,20},{44,24},{48,28},{52,3... | collective-permute-start | bytes 196616 | tf_op jit(solution)/shard_map/ppermute | solution.py:16
  368.3 15.7 %collective-permute-start.14 = (bf16[2,128,1,128]{3,1,0,2:T(8,128)(2,1)S(1)}, bf16[2,128,1,128]{3,1,0,2:T(8,128)(2,1)S(1)}, u32[]{:S(2)}, u32[]{:S(2)}) collective-permute-start(bf16[2,128,1,128]{3,1,0,2:T(8,128)(2,1)S(1)} %get-tuple-element.61), channel_id=1, source_target_pairs={{24,0},{28,4},{32,8},{36,12},{40,16},{44,20},{48,24},{52,28},{56,3... | collective-permute-start | bytes 196616 | tf_op jit(solution)/shard_map/ppermute | solution.py:16
  373.7 10.2 %collective-permute-start.15 = (bf16[2,128,1,128]{3,1,2,0:T(8,128)(2,1)S(1)}, bf16[2,128,1,128]{3,1,2,0:T(8,128)(2,1)S(1)}, u32[]{:S(2)}, u32[]{:S(2)}) collective-permute-start(bf16[2,128,1,128]{3,1,2,0:T(8,128)(2,1)S(1)} %get-tuple-element.60), channel_id=1, source_target_pairs={{28,0},{32,4},{36,8},{40,12},{44,16},{48,20},{52,24},{56,28},{60,3... | collective-permute-start | bytes 196616 | tf_op jit(solution)/shard_map/ppermute | solution.py:16
  378.9 6.2 %collective-permute-start.9 = (bf16[2,128,1,128]{3,1,0,2:T(8,128)(2,1)S(1)}, bf16[2,128,1,128]{3,1,0,2:T(8,128)(2,1)S(1)}, u32[]{:S(2)}, u32[]{:S(2)}) collective-permute-start(bf16[2,128,1,128]{3,1,0,2:T(8,128)(2,1)S(1)} %get-tuple-element.59), channel_id=1, source_target_pairs={{4,0},{8,4},{12,8},{16,12},{20,16},{24,20},{28,24},{32,28},{36,32}... | collective-permute-start | bytes 196616 | tf_op jit(solution)/shard_map/ppermute | solution.py:16
  (16 other events, 268.3 us)
Sparse Core Ops, SparseCore 0:
  11.1 192.4 all-gather.2
  220.2 34.9 reduce-scatter.3
  307.3 21.2 all-gather.4

commit v5 on v4

--- a/solution.py
+++ b/solution.py
@@ -110,20 +110,18 @@
     for distance in range(1, REACH + 1):
         blocks.append(passed_along(paired, "seq", distance))
     sent_payload = lax.all_to_all(payload, "seq", split_axis=0, concat_axis=0, tiled=True)
-    sent_payload, weight_full, blocks = lax.optimization_barrier(
-        (sent_payload, weight_full, tuple(blocks))
-    )
+    sent_payload, blocks = lax.optimization_barrier((sent_payload, tuple(blocks)))
     slot_rows = sent_payload[:, :capacity, :].reshape(slots_all, features)
     sent_weight = sent_payload[:, capacity, :capacity].reshape(slots_all)
     weight_here = w_down[0]
-    raw = lax.psum_scatter(
-        lax.dot_general(
-            weight_here, slot_rows, (((1,), (1,)), ((), ())), preferred_element_type=jnp.float32
-        ).astype(jnp.bfloat16),
-        "head",
-        scatter_dimension=0,
-        tiled=True,
-    ).astype(jnp.float32)
+    head_count = lax.axis_size("head")
+    partial = lax.dot_general(
+        weight_here, slot_rows, (((1,), (1,)), ((), ())), preferred_element_type=jnp.float32
+    ).astype(jnp.bfloat16)
+    received = lax.all_to_all(
+        partial.reshape(head_count, -1, slots_all), "head", split_axis=0, concat_axis=0, tiled=True
+    )
+    raw = jnp.sum(received.astype(jnp.float32), axis=0)
     gate = saved_gu[0, 0].astype(jnp.float32)
     up = saved_gu[0, 1].astype(jnp.float32)
     sig = jax.nn.sigmoid(gate)
@@ -134,6 +132,7 @@
     gate_up_grad = jnp.stack([scaled * up * sig * (1.0 + gate * (1.0 - sig)), scaled * act])[
         None
     ].astype(jnp.bfloat16)
+    slot_part, weight_full = lax.optimization_barrier((slot_part, weight_full))
     slot_grad = head_sum(slot_part)
     returned = lax.all_to_all(
         slot_grad.reshape(seq_count, capacity), "seq", split_axis=0, concat_axis=0, tiled=True

time: 395 us -> 352 us (0.89)
  waiting for transfers between devices: 168 us -> 132 us
  local copies, waits for them, and re-layouts: 41.8 us -> 30.9 us
    all_gather x1, waiting for transfers between devices: 30.2 us -> 0.02 us  [per_device(): weight_full = lax.all_gather(out_weight, 'seq', axis=1, tiled=True)]
    unnamed x4 -> x2, waiting for transfers between devices: 29.5 us -> 0.7 us
    all_to_all x0 -> x1, waiting for transfers between devices: none -> 24.3 us  [per_device(): lax.all_to_all(partial.reshape(head_count, -1, slots_all), 'head', split_...]
    unnamed x69 -> x66, local copies, waits for them, and re-layouts: 18.5 us -> 7.69 us
    all_to_all x0 -> x1, starting transfers between devices: none -> 4.89 us  [per_device(): lax.all_to_all(partial.reshape(head_count, -1, slots_all), 'head', split_...]
    ppermute x14, starting transfers between devices: 75.9 us -> 71.5 us  [passed_along(): return lax.ppermute(array, axis, pairs)]
  transfers between devices with their start and end apart: 21 -> 21, of which waited for: 10 -> 9; matrix products, arithmetic and copies ran while one was open for 9% -> 14% of each run, Pallas kernels for 0% -> 0%
where the time goes in v5:
time: 352 us; the launch traced here: 350 us
  waiting for transfers between devices  132 us (38%)
  starting transfers between devices  118 us (34%)
  local copies, waits for them, and re-layouts  30.9 us (9%)
  matrix products  28.9 us (8%)
  other arithmetic  25.5 us (7%)
  between operations  14.8 us (4%)
    ppermute x14, waiting for transfers between devices, passed_along(): return lax.ppermute(array, axis, pairs)  84.3 us
    ppermute x14, starting transfers between devices, passed_along(): return lax.ppermute(array, axis, pairs)  71.5 us
    all_to_all x1, waiting for transfers between devices, per_device(): lax.all_to_all(partial.reshape(head_count, -1, slots_all), 'head', split_...  24.3 us
    all_to_all x1, starting transfers between devices, per_device(): lax.all_to_all(slot_grad.reshape(seq_count, capacity), 'seq', split_axis=...  18.4 us
    all_to_all x1, starting transfers between devices, per_device(): lax.all_to_all(payload, 'seq', split_axis=0, concat_axis=0, tiled=True)  18.2 us
    all_gather x1, waiting for transfers between devices, per_device(): input_grad = lax.all_gather(input_slice, 'head', axis=1, tiled=True)  13.1 us
    unnamed x66, local copies, waits for them, and re-layouts  7.69 us
    dot_general x1, matrix products, per_device(): send_rows = jnp.dot(pick, out_grad, preferred_element_type=jnp.float32)  7.08 us
  transfers between devices with their start and end apart: 21, of which 9 were waited for; matrix products, arithmetic and copies ran while one was open for 14% of the time, Pallas kernels for 0%

profile of v5, /device:TPU:49, one launch (start us, length us, event | category | flops | bytes accessed | tf_op | source)
XLA Modules:
  0.0 350.2 jit_solution(10527638924851526868)
XLA Ops:
  13.8 7.1 %fusion.13 = bf16[2048,1024]{1,0:T(8,128)(2,1)} fusion(bf16[128,1024]{1,0:T(8,128)(2,1)} %param.11, s32[1024]{0:T(1024)S(1)} %eq.52, s32[1024]{0:T(1024)S(1)} %add_select_fusion), kind=kOutput, calls=%fused_computation.33 | convolution fusion | flops 1076232192 | bytes 4464640 | tf_op jit(solution)/shard_map/dot_general | solution.py:97
  20.9 4.5 %select_convert_fusion = bf16[128,16,1024]{2,1,0:T(8,128)(2,1)} fusion(bf16[128,16,1024]{2,1,0:T(8,128)(2,1)} %bitcast.191, bf16[128,1024]{1,0:T(8,128)(2,1)S(1)} %pad.4, pred[16]{0:T(512)(128)(4,1)S(1)} %iota_compare_fusion.13), kind=kLoop, calls=%fused_computation.1 | loop fusion | flops 2097152 | bytes 8650768 | tf_op jit(solution)/shard_map/convert_element_type | solution.py:103
  25.5 18.2 %all-to-all-start = ((bf16[128,16,1024]{2,1,0:T(8,128)(2,1)}), bf16[128,16,1024]{2,1,0:T(8,128)(2,1)}, u32[]{:S(2)}, u32[]{:S(2)}) async-start(bf16[128,16,1024]{2,1,0:T(8,128)(2,1)} %select_convert_fusion), calls=%async_computation | async-start | bytes 8388608 | tf_op jit(solution)/shard_map/all_to_all | solution.py:112
  43.8 3.4 collective-permute-start
  47.1 3.1 collective-permute-start.1
  50.2 3.2 collective-permute-start.2
  53.5 4.3 %collective-permute-start.3 = (bf16[2,128,1,128]{3,1,2,0:T(8,128)(2,1)S(1)}, bf16[2,128,1,128]{3,1,2,0:T(8,128)(2,1)S(1)}, u32[]{:S(2)}, u32[]{:S(2)}) collective-permute-start(bf16[2,128,1,128]{3,1,2,0:T(8,128)(2,1)S(1)} %pad_maximum_fusion.2), channel_id=1, source_target_pairs={{0,16},{4,20},{8,24},{12,28},{16,32},{20,36},{24,40},{28,44},{32,4... | collective-permute-start | bytes 196616 | tf_op jit(solution)/shard_map/ppermute | solution.py:16
  57.8 2.6 collective-permute-start.4
  60.5 78.4 %collective-permute-done = bf16[2,128,1,128]{3,1,2,0:T(8,128)(2,1)S(1)} collective-permute-done((bf16[2,128,1,128]{3,1,2,0:T(8,128)(2,1)S(1)}, bf16[2,128,1,128]{3,1,2,0:T(8,128)(2,1)S(1)}, u32[]{:S(2)}, u32[]{:S(2)}) %collective-permute-start) | collective-permute-done | bytes 65568 | tf_op jit(solution)/shard_map/ppermute | solution.py:16
  140.8 2.7 collective-permute-done.1
  143.5 23.5 %collective-permute-start.6 = (bf16[2,128,1,128]{3,1,2,0:T(8,128)(2,1)S(1)}, bf16[2,128,1,128]{3,1,2,0:T(8,128)(2,1)S(1)}, u32[]{:S(2)}, u32[]{:S(2)}) collective-permute-start(bf16[2,128,1,128]{3,1,2,0:T(8,128)(2,1)S(1)} %pad_maximum_fusion.2), channel_id=1, source_target_pairs={{0,28},{4,32},{8,36},{12,40},{16,44},{20,48},{24,52},{28,56},{32,6... | collective-permute-start | bytes 196616 | tf_op jit(solution)/shard_map/ppermute | solution.py:16
  168.3 6.2 %reshape.468 = bf16[1536,1024]{1,0:T(8,128)(2,1)} reshape(bf16[128,12,1024]{2,1,0:T(8,128)(2,1)} %bitcast.186) | data formatting | bytes 6291456 | tf_op jit(solution)/shard_map/reshape | solution.py:114
  174.6 5.9 %convolution_convert_fusion = bf16[1536,768]{0,1:T(8,128)(2,1)} fusion(bf16[1536,1024]{1,0:T(8,128)(2,1)} %reshape.468, bf16[1,768,1024]{2,1,0:T(8,128)(2,1)S(1)} %copy-done), kind=kOutput, calls=%fused_computation.16 | convolution fusion | flops 2417098752 | bytes 7077888 | tf_op jit(solution)/shard_map/dot_general | solution.py:118
  180.5 4.9 %all-to-all-start.1 = ((bf16[4,192,1536]{2,1,0:T(8,128)(2,1)}), bf16[4,192,1536]{2,1,0:T(8,128)(2,1)}, u32[]{:S(2)}, u32[]{:S(2)}) async-start(bf16[4,192,1536]{2,1,0:T(8,128)(2,1)} %bitcast.192), calls=%async_computation.1 | async-start | bytes 4718592 | tf_op jit(solution)/shard_map/all_to_all | solution.py:121
  188.3 24.3 %all-to-all-done.1 = bf16[4,192,1536]{2,1,0:T(8,128)(2,1)} async-done(((bf16[4,192,1536]{2,1,0:T(8,128)(2,1)}), bf16[4,192,1536]{2,1,0:T(8,128)(2,1)}, u32[]{:S(2)}, u32[]{:S(2)}) %all-to-all-start.1) | async-done | bytes 2359328 | tf_op jit(solution)/shard_map/all_to_all | solution.py:121
  220.9 2.5 collective-permute-start.8
  224.2 2.5 collective-permute-done.8
  227.5 18.4 %all-to-all-start.2 = ((f32[128,1,12]{2,1,0:T(1,128)}), f32[128,1,12]{2,1,0:T(1,128)}, u32[]{:S(2)}, u32[]{:S(2)}) async-start(f32[128,1,12]{2,1,0:T(1,128)} %bitcast.195), calls=%async_computation.2 | async-start | bytes 131072 | tf_op jit(solution)/shard_map/all_to_all | solution.py:137
  247.8 6.1 %all-to-all-done.2 = f32[128,1,12]{2,1,0:T(1,128)} async-done(((f32[128,1,12]{2,1,0:T(1,128)}), f32[128,1,12]{2,1,0:T(1,128)}, u32[]{:S(2)}, u32[]{:S(2)}) %all-to-all-start.2) | async-done | bytes 6176 | tf_op jit(solution)/shard_map/all_to_all | solution.py:137
  254.4 2.3 reduce.10
  257.7 6.4 %gather_fusion = f32[1024]{0:T(1024)S(1)} fusion(f32[1536]{0:T(1024)S(1)} %reshape.470, s32[1024]{0:T(1024)} %broadcast_clamp_fusion), kind=kCustom, calls=%fused_computation | custom fusion | bytes 12288 | tf_op jit(solution)/shard_map/jit(_take)/gather | solution.py:140
  275.2 13.1 %all-gather.5.cloned.1.call-done = bf16[128,4096]{1,0:T(8,128)(2,1)} async-done(((bf16[128,1024]{1,0:T(8,128)(2,1)}), bf16[128,4096]{1,0:T(8,128)(2,1)}) %all-gather.5.cloned.1.call-update) | async-done | bytes 1048592 | tf_op jit(solution)/shard_map/all_gather | solution.py:145
  288.2 5.1 %convolution_convert_fusion.1 = bf16[128,1024]{1,0:T(8,128)(2,1)S(1)} fusion(bf16[128,4096]{1,0:T(8,128)(2,1)} %all-gather.5.cloned.1.call-done, bf16[1024,4096]{0,1:T(8,128)(2,1)} %all-gather.3.cloned.1.call-done), kind=kOutput, calls=%fused_computation.39 | convolution fusion | flops 1073872896 | bytes 9699328 | tf_op jit(solution)/shard_map/dot_general | solution.py:146
  294.7 3.4 convert_bitcast_fusion
  298.2 4.2 %copy.99 = bf16[8,128,1024]{2,0,1:T(8,128)(2,1)} copy(bf16[8,128,1024]{1,2,0:T(8,128)(2,1)} %get-tuple-element.54) | data formatting | bytes 4194304 | tf_op jit(solution)/shard_map/reshape.35
  304.7 2.4 fusion.14
  307.8 9.5 %collective-permute-start.15 = (bf16[2,128,1,128]{3,1,2,0:T(8,128)(2,1)S(1)}, bf16[2,128,1,128]{3,1,2,0:T(8,128)(2,1)S(1)}, u32[]{:S(2)}, u32[]{:S(2)}) collective-permute-start(bf16[2,128,1,128]{3,1,2,0:T(8,128)(2,1)S(1)} %get-tuple-element.59), channel_id=1, source_target_pairs={{28,0},{32,4},{36,8},{40,12},{44,16},{48,20},{52,24},{56,28},{60,3... | collective-permute-start | bytes 196616 | tf_op jit(solution)/shard_map/ppermute | solution.py:16
  317.3 2.5 collective-permute-start.14
  321.0 5.2 %collective-permute-start.13 = (bf16[2,128,1,128]{3,1,0,2:T(8,128)(2,1)}, bf16[2,128,1,128]{3,1,0,2:T(8,128)(2,1)S(1)}, u32[]{:S(2)}, u32[]{:S(2)}) collective-permute-start(bf16[2,128,1,128]{3,1,0,2:T(8,128)(2,1)} %get-tuple-element.61), channel_id=1, source_target_pairs={{20,0},{24,4},{28,8},{32,12},{36,16},{40,20},{44,24},{48,28},{52,3... | collective-permute-start | bytes 196616 | tf_op jit(solution)/shard_map/ppermute | solution.py:16
  326.2 3.6 %collective-permute-start.12 = (bf16[2,128,1,128]{3,1,0,2:T(8,128)(2,1)}, bf16[2,128,1,128]{3,1,0,2:T(8,128)(2,1)S(1)}, u32[]{:S(2)}, u32[]{:S(2)}) collective-permute-start(bf16[2,128,1,128]{3,1,0,2:T(8,128)(2,1)} %get-tuple-element.62), channel_id=1, source_target_pairs={{16,0},{20,4},{24,8},{28,12},{32,16},{36,20},{40,24},{44,28},{48,3... | collective-permute-start | bytes 196616 | tf_op jit(solution)/shard_map/ppermute | solution.py:16
  329.8 4.4 %collective-permute-start.11 = (bf16[2,128,1,128]{3,1,0,2:T(8,128)(2,1)S(1)}, bf16[2,128,1,128]{3,1,0,2:T(8,128)(2,1)S(1)}, u32[]{:S(2)}, u32[]{:S(2)}) collective-permute-start(bf16[2,128,1,128]{3,1,0,2:T(8,128)(2,1)S(1)} %get-tuple-element.63), channel_id=1, source_target_pairs={{12,0},{16,4},{20,8},{24,12},{28,16},{32,20},{36,24},{40,28},{44,3... | collective-permute-start | bytes 196616 | tf_op jit(solution)/shard_map/ppermute | solution.py:16
  336.2 2.2 collective-permute-start.9
  (149 shorter events, 49.2 us)
Async XLA Ops:
  7.2 167.4 %copy-start = (bf16[1,768,1024]{2,1,0:T(8,128)(2,1)S(1)}, bf16[1,768,1024]{2,1,0:T(8,128)(2,1)}, u32[]{:S(2)}) copy-start(bf16[1,768,1024]{2,1,0:T(8,128)(2,1)} %param.16) | copy-start | bytes 4718596
  7.2 209.3 %all-gather.3.cloned.1.call-start = ((), (), s32[]{:S(2)}) async-start(), calls=%async_computation.3 | async-start | bytes 8454144 | tf_op jit(solution)/shard_map/all_gather | solution.py:104
  25.5 18.3 %copy-start.20 = (bf16[128,1,128]{2,0,1:T(8,128)(2,1)S(1)}, bf16[128,1,128]{2,0,1:T(8,128)(2,1)}, u32[]{:S(2)}) copy-start(bf16[128,1,128]{2,0,1:T(8,128)(2,1)} %param.21) | copy-start | bytes 98308
  25.5 18.3 %copy-start.21 = (bf16[128,1,128]{2,0,1:T(8,128)(2,1)S(1)}, bf16[128,1,128]{2,0,1:T(8,128)(2,1)}, u32[]{:S(2)}) copy-start(bf16[128,1,128]{2,0,1:T(8,128)(2,1)} %param.20) | copy-start | bytes 98308
  25.5 142.8 %all-to-all-start = ((bf16[128,16,1024]{2,1,0:T(8,128)(2,1)}), bf16[128,16,1024]{2,1,0:T(8,128)(2,1)}, u32[]{:S(2)}, u32[]{:S(2)}) async-start(bf16[128,16,1024]{2,1,0:T(8,128)(2,1)} %select_convert_fusion), calls=%async_computation | async-start | bytes 8388608 | tf_op jit(solution)/shard_map/all_to_all | solution.py:112
  43.8 95.1 %collective-permute-start = (bf16[2,128,1,128]{3,1,2,0:T(8,128)(2,1)S(1)}, bf16[2,128,1,128]{3,1,2,0:T(8,128)(2,1)S(1)}, u32[]{:S(2)}, u32[]{:S(2)}) collective-permute-start(bf16[2,128,1,128]{3,1,2,0:T(8,128)(2,1)S(1)} %pad_maximum_fusion.2), channel_id=1, source_target_pairs={{0,4},{4,8},{8,12},{12,16},{16,20},{20,24},{24,28},{28,32},{32,36}... | collective-permute-start | bytes 196616 | tf_op jit(solution)/shard_map/ppermute | solution.py:16
  47.1 96.4 %collective-permute-start.1 = (bf16[2,128,1,128]{3,1,2,0:T(8,128)(2,1)S(1)}, bf16[2,128,1,128]{3,1,2,0:T(8,128)(2,1)S(1)}, u32[]{:S(2)}, u32[]{:S(2)}) collective-permute-start(bf16[2,128,1,128]{3,1,2,0:T(8,128)(2,1)S(1)} %pad_maximum_fusion.2), channel_id=1, source_target_pairs={{0,8},{4,12},{8,16},{12,20},{16,24},{20,28},{24,32},{28,36},{32,40... | collective-permute-start | bytes 196616 | tf_op jit(solution)/shard_map/ppermute | solution.py:16
  50.2 116.8 %collective-permute-start.2 = (bf16[2,128,1,128]{3,1,2,0:T(8,128)(2,1)S(1)}, bf16[2,128,1,128]{3,1,2,0:T(8,128)(2,1)S(1)}, u32[]{:S(2)}, u32[]{:S(2)}) collective-permute-start(bf16[2,128,1,128]{3,1,2,0:T(8,128)(2,1)S(1)} %pad_maximum_fusion.2), channel_id=1, source_target_pairs={{0,12},{4,16},{8,20},{12,24},{16,28},{20,32},{24,36},{28,40},{32,4... | collective-permute-start | bytes 196616 | tf_op jit(solution)/shard_map/ppermute | solution.py:16
  53.5 113.5 %collective-permute-start.3 = (bf16[2,128,1,128]{3,1,2,0:T(8,128)(2,1)S(1)}, bf16[2,128,1,128]{3,1,2,0:T(8,128)(2,1)S(1)}, u32[]{:S(2)}, u32[]{:S(2)}) collective-permute-start(bf16[2,128,1,128]{3,1,2,0:T(8,128)(2,1)S(1)} %pad_maximum_fusion.2), channel_id=1, source_target_pairs={{0,16},{4,20},{8,24},{12,28},{16,32},{20,36},{24,40},{28,44},{32,4... | collective-permute-start | bytes 196616 | tf_op jit(solution)/shard_map/ppermute | solution.py:16
  57.8 109.2 %collective-permute-start.4 = (bf16[2,128,1,128]{3,1,2,0:T(8,128)(2,1)S(1)}, bf16[2,128,1,128]{3,1,2,0:T(8,128)(2,1)S(1)}, u32[]{:S(2)}, u32[]{:S(2)}) collective-permute-start(bf16[2,128,1,128]{3,1,2,0:T(8,128)(2,1)S(1)} %pad_maximum_fusion.2), channel_id=1, source_target_pairs={{0,20},{4,24},{8,28},{12,32},{16,36},{20,40},{24,44},{28,48},{32,5... | collective-permute-start | bytes 196616 | tf_op jit(solution)/shard_map/ppermute | solution.py:16
  138.9 35.7 %copy-start.13 = (bf16[2,128,1,128]{3,1,2,0:T(8,128)(2,1)}, bf16[2,128,1,128]{3,1,2,0:T(8,128)(2,1)S(1)}, u32[]{:S(2)}) copy-start(bf16[2,128,1,128]{3,1,2,0:T(8,128)(2,1)S(1)} %collective-permute-done) | copy-start | bytes 196612
  138.9 28.2 %collective-permute-start.5 = (bf16[2,128,1,128]{3,1,2,0:T(8,128)(2,1)S(1)}, bf16[2,128,1,128]{3,1,2,0:T(8,128)(2,1)S(1)}, u32[]{:S(2)}, u32[]{:S(2)}) collective-permute-start(bf16[2,128,1,128]{3,1,2,0:T(8,128)(2,1)S(1)} %pad_maximum_fusion.2), channel_id=1, source_target_pairs={{0,24},{4,28},{8,32},{12,36},{16,40},{20,44},{24,48},{28,52},{32,5... | collective-permute-start | bytes 196616 | tf_op jit(solution)/shard_map/ppermute | solution.py:16
  143.5 31.0 %copy-start.15 = (bf16[2,128,1,128]{3,1,2,0:T(8,128)(2,1)}, bf16[2,128,1,128]{3,1,2,0:T(8,128)(2,1)S(1)}, u32[]{:S(2)}) copy-start(bf16[2,128,1,128]{3,1,2,0:T(8,128)(2,1)S(1)} %collective-permute-done.1) | copy-start | bytes 196612
  143.5 24.8 %collective-permute-start.6 = (bf16[2,128,1,128]{3,1,2,0:T(8,128)(2,1)S(1)}, bf16[2,128,1,128]{3,1,2,0:T(8,128)(2,1)S(1)}, u32[]{:S(2)}, u32[]{:S(2)}) collective-permute-start(bf16[2,128,1,128]{3,1,2,0:T(8,128)(2,1)S(1)} %pad_maximum_fusion.2), channel_id=1, source_target_pairs={{0,28},{4,32},{8,36},{12,40},{16,44},{20,48},{24,52},{28,56},{32,6... | collective-permute-start | bytes 196616 | tf_op jit(solution)/shard_map/ppermute | solution.py:16
  180.5 32.2 %all-to-all-start.1 = ((bf16[4,192,1536]{2,1,0:T(8,128)(2,1)}), bf16[4,192,1536]{2,1,0:T(8,128)(2,1)}, u32[]{:S(2)}, u32[]{:S(2)}) async-start(bf16[4,192,1536]{2,1,0:T(8,128)(2,1)} %bitcast.192), calls=%async_computation.1 | async-start | bytes 4718592 | tf_op jit(solution)/shard_map/all_to_all | solution.py:121
  216.4 47.8 %copy-start.10 = (f32[128,8]{0,1:T(8,128)S(1)}, f32[128,8]{0,1:T(8,128)}, u32[]{:S(2)}) copy-start(f32[128,8]{0,1:T(8,128)} %param.13) | copy-start | bytes 12292
  216.5 4.4 %collective-permute-start.7 = (f32[1536]{0:T(1024)S(1)}, f32[1536]{0:T(1024)S(1)}, u32[]{:S(2)}, u32[]{:S(2)}) collective-permute-start(f32[1536]{0:T(1024)S(1)} %fusion.22), channel_id=1, source_target_pairs={{0,1},{1,0},{2,3},{3,2},{4,5},{5,4},{6,7},{7,6},{8,9},{9,8},{10,11... | collective-permute-start | bytes 18440 | tf_op jit(solution)/shard_map/ppermute | solution.py:24
  220.9 5.9 %collective-permute-start.8 = (f32[1536]{0:T(1024)S(1)}, f32[1536]{0:T(1024)S(1)}, u32[]{:S(2)}, u32[]{:S(2)}) collective-permute-start(f32[1536]{0:T(1024)S(1)} %add.153), channel_id=1, source_target_pairs={{0,2},{1,3},{2,0},{3,1},{4,6},{5,7},{6,4},{7,5},{8,10},{9,11},{10,... | collective-permute-start | bytes 18440 | tf_op jit(solution)/shard_map/ppermute | solution.py:24
  227.5 26.4 %all-to-all-start.2 = ((f32[128,1,12]{2,1,0:T(1,128)}), f32[128,1,12]{2,1,0:T(1,128)}, u32[]{:S(2)}, u32[]{:S(2)}) async-start(f32[128,1,12]{2,1,0:T(1,128)} %bitcast.195), calls=%async_computation.2 | async-start | bytes 131072 | tf_op jit(solution)/shard_map/all_to_all | solution.py:137
  245.9 42.4 %all-gather.5.cloned.1.call-start = ((), (), s32[]{:S(2)}) async-start(), calls=%async_computation.4 | async-start | bytes 1310720 | tf_op jit(solution)/shard_map/all_gather | solution.py:145
  257.7 11.5 %copy-start.6 = (bf16[128,8,128]{2,1,0:T(8,128)(2,1)S(1)}, bf16[128,8,128]{2,1,0:T(8,128)(2,1)}, u32[]{:S(2)}) copy-start(bf16[128,8,128]{2,1,0:T(8,128)(2,1)} %param.19) | copy-start | bytes 786436
  275.2 18.2 %copy-start.8 = (bf16[2,1024,1,128]{3,1,2,0:T(8,128)(2,1)S(1)}, bf16[2,1024,1,128]{3,1,2,0:T(8,128)(2,1)}, u32[]{:S(2)}) copy-start(bf16[2,1024,1,128]{3,1,2,0:T(8,128)(2,1)} %constant_dynamic-update-slice_fusion) | copy-start | bytes 1572868
  304.7 15.2 %copy-start.5 = (bf16[1,1,192,1536]{3,2,1,0:T(8,128)(2,1)S(1)}, bf16[1,1,192,1536]{3,2,1,0:T(8,128)(2,1)}, u32[]{:S(2)}) copy-start(bf16[1,1,192,1536]{3,2,1,0:T(8,128)(2,1)} %get-tuple-element.57) | copy-start | bytes 1769476
  307.0 31.4 %copy-start.3 = (bf16[8,128,1024]{1,2,0:T(8,128)(2,1)S(1)}, bf16[8,128,1024]{1,2,0:T(8,128)(2,1)}, u32[]{:S(2)}) copy-start(bf16[8,128,1024]{1,2,0:T(8,128)(2,1)} %get-tuple-element.55) | copy-start | bytes 6291460
  307.0 31.4 %copy-start.9 = (bf16[2,1024,1,128]{3,1,2,0:T(8,128)(2,1)S(1)}, bf16[2,1024,1,128]{3,1,2,0:T(8,128)(2,1)}, u32[]{:S(2)}) copy-start(bf16[2,1024,1,128]{3,1,2,0:T(8,128)(2,1)} %constant_dynamic-update-slice_fusion) | copy-start | bytes 1572868
  307.8 26.4 %collective-permute-start.15 = (bf16[2,128,1,128]{3,1,2,0:T(8,128)(2,1)S(1)}, bf16[2,128,1,128]{3,1,2,0:T(8,128)(2,1)S(1)}, u32[]{:S(2)}, u32[]{:S(2)}) collective-permute-start(bf16[2,128,1,128]{3,1,2,0:T(8,128)(2,1)S(1)} %get-tuple-element.59), channel_id=1, source_target_pairs={{28,0},{32,4},{36,8},{40,12},{44,16},{48,20},{52,24},{56,28},{60,3... | collective-permute-start | bytes 196616 | tf_op jit(solution)/shard_map/ppermute | solution.py:16
  317.3 18.9 %collective-permute-start.14 = (bf16[2,128,1,128]{3,1,0,2:T(8,128)(2,1)S(1)}, bf16[2,128,1,128]{3,1,0,2:T(8,128)(2,1)S(1)}, u32[]{:S(2)}, u32[]{:S(2)}) collective-permute-start(bf16[2,128,1,128]{3,1,0,2:T(8,128)(2,1)S(1)} %get-tuple-element.60), channel_id=1, source_target_pairs={{24,0},{28,4},{32,8},{36,12},{40,16},{44,20},{48,24},{52,28},{56,3... | collective-permute-start | bytes 196616 | tf_op jit(solution)/shard_map/ppermute | solution.py:16
  321.0 18.9 %collective-permute-start.13 = (bf16[2,128,1,128]{3,1,0,2:T(8,128)(2,1)}, bf16[2,128,1,128]{3,1,0,2:T(8,128)(2,1)S(1)}, u32[]{:S(2)}, u32[]{:S(2)}) collective-permute-start(bf16[2,128,1,128]{3,1,0,2:T(8,128)(2,1)} %get-tuple-element.61), channel_id=1, source_target_pairs={{20,0},{24,4},{28,8},{32,12},{36,16},{40,20},{44,24},{48,28},{52,3... | collective-permute-start | bytes 196616 | tf_op jit(solution)/shard_map/ppermute | solution.py:16
  326.2 13.7 %collective-permute-start.12 = (bf16[2,128,1,128]{3,1,0,2:T(8,128)(2,1)}, bf16[2,128,1,128]{3,1,0,2:T(8,128)(2,1)S(1)}, u32[]{:S(2)}, u32[]{:S(2)}) collective-permute-start(bf16[2,128,1,128]{3,1,0,2:T(8,128)(2,1)} %get-tuple-element.62), channel_id=1, source_target_pairs={{16,0},{20,4},{24,8},{28,12},{32,16},{36,20},{40,24},{44,28},{48,3... | collective-permute-start | bytes 196616 | tf_op jit(solution)/shard_map/ppermute | solution.py:16
  329.8 10.1 %collective-permute-start.11 = (bf16[2,128,1,128]{3,1,0,2:T(8,128)(2,1)S(1)}, bf16[2,128,1,128]{3,1,0,2:T(8,128)(2,1)S(1)}, u32[]{:S(2)}, u32[]{:S(2)}) collective-permute-start(bf16[2,128,1,128]{3,1,0,2:T(8,128)(2,1)S(1)} %get-tuple-element.63), channel_id=1, source_target_pairs={{12,0},{16,4},{20,8},{24,12},{28,16},{32,20},{36,24},{40,28},{44,3... | collective-permute-start | bytes 196616 | tf_op jit(solution)/shard_map/ppermute | solution.py:16
  334.2 5.7 %collective-permute-start.10 = (bf16[2,128,1,128]{3,1,0,2:T(8,128)(2,1)S(1)}, bf16[2,128,1,128]{3,1,0,2:T(8,128)(2,1)S(1)}, u32[]{:S(2)}, u32[]{:S(2)}) collective-permute-start(bf16[2,128,1,128]{3,1,0,2:T(8,128)(2,1)S(1)} %get-tuple-element.64), channel_id=1, source_target_pairs={{8,0},{12,4},{16,8},{20,12},{24,16},{28,20},{32,24},{36,28},{40,32... | collective-permute-start | bytes 196616 | tf_op jit(solution)/shard_map/ppermute | solution.py:16
  336.2 5.6 %collective-permute-start.9 = (bf16[2,128,1,128]{3,1,0,2:T(8,128)(2,1)S(1)}, bf16[2,128,1,128]{3,1,0,2:T(8,128)(2,1)S(1)}, u32[]{:S(2)}, u32[]{:S(2)}) collective-permute-start(bf16[2,128,1,128]{3,1,0,2:T(8,128)(2,1)S(1)} %get-tuple-element.58), channel_id=1, source_target_pairs={{4,0},{8,4},{12,8},{16,12},{20,16},{24,20},{28,24},{32,28},{36,32}... | collective-permute-start | bytes 196616 | tf_op jit(solution)/shard_map/ppermute | solution.py:16
  (17 other events, 112.7 us)
Sparse Core Ops, SparseCore 0:
  11.1 191.7 all-gather.2
  267.3 20.8 all-gather.4

commit v6 on v5

--- a/solution.py
+++ b/solution.py
@@ -109,8 +109,8 @@
     blocks = [paired]
     for distance in range(1, REACH + 1):
         blocks.append(passed_along(paired, "seq", distance))
+    payload, blocks = lax.optimization_barrier((payload, tuple(blocks)))
     sent_payload = lax.all_to_all(payload, "seq", split_axis=0, concat_axis=0, tiled=True)
-    sent_payload, blocks = lax.optimization_barrier((sent_payload, tuple(blocks)))
     slot_rows = sent_payload[:, :capacity, :].reshape(slots_all, features)
     sent_weight = sent_payload[:, capacity, :capacity].reshape(slots_all)
     weight_here = w_down[0]
@@ -134,10 +134,9 @@
     ].astype(jnp.bfloat16)
     slot_part, weight_full = lax.optimization_barrier((slot_part, weight_full))
     slot_grad = head_sum(slot_part)
-    returned = lax.all_to_all(
-        slot_grad.reshape(seq_count, capacity), "seq", split_axis=0, concat_axis=0, tiled=True
-    )
-    route_grad = jnp.take(returned.reshape(-1), target.reshape(-1)).reshape(tokens_here, top_count)
+    table = lax.all_gather(slot_grad, "seq", axis=0, tiled=True)
+    lookup = expert_ids * slots_all + seq_index * capacity + rank
+    route_grad = jnp.take(table, lookup.reshape(-1)).reshape(tokens_here, top_count)
     logit_grad = weights * (route_grad - jnp.sum(weights * route_grad, axis=1, keepdims=True))
     dense = jnp.einsum("tk,tke->te", logit_grad, hits, precision=highest)
     router_term = jnp.dot(dense, router.astype(jnp.float32), precision=highest)

time: 352 us -> 388 us (1.10)
  blocking collectives: 0 us -> 52.9 us
  starting transfers between devices: 118 us -> 83.8 us
  waiting for transfers between devices: 132 us -> 153 us
  local copies, waits for them, and re-layouts: 30.9 us -> 26 us
    all_to_all x1, waiting for transfers between devices: 0.01 us -> 103 us  [per_device(): lax.all_to_all(payload, 'seq', split_axis=0, concat_axis=0, tiled=True)]
    ppermute x14, waiting for transfers between devices: 84.3 us -> 2.22 us  [passed_along(): return lax.ppermute(array, axis, pairs)]
    all_gather x0 -> x1, blocking collectives: none -> 52.9 us  [per_device(): table = lax.all_gather(slot_grad, 'seq', axis=0, tiled=True)]
    all_to_all x1 -> x0, starting transfers between devices: 18.4 us -> none  [per_device(): lax.all_to_all(slot_grad.reshape(seq_count, capacity), 'seq', split_axis=...]
    ppermute x14, starting transfers between devices: 71.5 us -> 61.1 us  [passed_along(): return lax.ppermute(array, axis, pairs)]
    all_to_all x1 -> x0, waiting for transfers between devices: 6.09 us -> none  [per_device(): lax.all_to_all(slot_grad.reshape(seq_count, capacity), 'seq', split_axis=...]
    all_to_all x1, starting transfers between devices: 18.2 us -> 13.8 us  [per_device(): lax.all_to_all(payload, 'seq', split_axis=0, concat_axis=0, tiled=True)]
    all_to_all x1, waiting for transfers between devices: 24.3 us -> 28.3 us  [per_device(): lax.all_to_all(partial.reshape(head_count, -1, slots_all), 'head', split_...]
  transfers between devices with their start and end apart: 21 -> 20, of which waited for: 9 -> 7; matrix products, arithmetic and copies ran while one was open for 14% -> 12% of each run, Pallas kernels for 0% -> 0%
where the time goes in v6:
time: 388 us; the launch traced here: 386 us
  waiting for transfers between devices  153 us (39%)
  starting transfers between devices  83.8 us (22%)
  blocking collectives  52.9 us (14%)
  matrix products  29.8 us (8%)
  local copies, waits for them, and re-layouts  26 us (7%)
  other arithmetic  26 us (7%)
  between operations  14.7 us (4%)
    all_to_all x1, waiting for transfers between devices, per_device(): lax.all_to_all(payload, 'seq', split_axis=0, concat_axis=0, tiled=True)  103 us
    ppermute x14, starting transfers between devices, passed_along(): return lax.ppermute(array, axis, pairs)  61.1 us
    all_gather x1, blocking collectives, per_device(): table = lax.all_gather(slot_grad, 'seq', axis=0, tiled=True)  52.9 us
    all_to_all x1, waiting for transfers between devices, per_device(): lax.all_to_all(partial.reshape(head_count, -1, slots_all), 'head', split_...  28.3 us
    all_to_all x1, starting transfers between devices, per_device(): lax.all_to_all(payload, 'seq', split_axis=0, concat_axis=0, tiled=True)  13.8 us
    all_gather x1, waiting for transfers between devices, per_device(): input_grad = lax.all_gather(input_slice, 'head', axis=1, tiled=True)  12.3 us
  transfers between devices with their start and end apart: 20, of which 7 were waited for; matrix products, arithmetic and copies ran while one was open for 12% of the time, Pallas kernels for 0%

profile of v6, /device:TPU:49, one launch (start us, length us, event | category | flops | bytes accessed | tf_op | source)
XLA Modules:
  0.0 386.4 jit_solution(18094513720098354549)
XLA Ops:
  8.7 4.6 %collective-permute-start = (bf16[2,128,1,128]{3,1,2,0:T(8,128)(2,1)S(1)}, bf16[2,128,1,128]{3,1,2,0:T(8,128)(2,1)S(1)}, u32[]{:S(2)}, u32[]{:S(2)}) collective-permute-start(bf16[2,128,1,128]{3,1,2,0:T(8,128)(2,1)S(1)} %pad_maximum_fusion.2), channel_id=1, source_target_pairs={{0,4},{4,8},{8,12},{12,16},{16,20},{20,24},{24,28},{28,32},{32,36}... | collective-permute-start | bytes 196616 | tf_op jit(solution)/shard_map/ppermute | solution.py:16
  13.3 4.0 %collective-permute-start.1 = (bf16[2,128,1,128]{3,1,2,0:T(8,128)(2,1)S(1)}, bf16[2,128,1,128]{3,1,2,0:T(8,128)(2,1)S(1)}, u32[]{:S(2)}, u32[]{:S(2)}) collective-permute-start(bf16[2,128,1,128]{3,1,2,0:T(8,128)(2,1)S(1)} %pad_maximum_fusion.2), channel_id=1, source_target_pairs={{0,8},{4,12},{8,16},{12,20},{16,24},{20,28},{24,32},{28,36},{32,40... | collective-permute-start | bytes 196616 | tf_op jit(solution)/shard_map/ppermute | solution.py:16
  17.3 4.0 %collective-permute-start.2 = (bf16[2,128,1,128]{3,1,2,0:T(8,128)(2,1)S(1)}, bf16[2,128,1,128]{3,1,2,0:T(8,128)(2,1)S(1)}, u32[]{:S(2)}, u32[]{:S(2)}) collective-permute-start(bf16[2,128,1,128]{3,1,2,0:T(8,128)(2,1)S(1)} %pad_maximum_fusion.2), channel_id=1, source_target_pairs={{0,12},{4,16},{8,20},{12,24},{16,28},{20,32},{24,36},{28,40},{32,4... | collective-permute-start | bytes 196616 | tf_op jit(solution)/shard_map/ppermute | solution.py:16
  21.3 6.1 %collective-permute-start.3 = (bf16[2,128,1,128]{3,1,2,0:T(8,128)(2,1)S(1)}, bf16[2,128,1,128]{3,1,2,0:T(8,128)(2,1)S(1)}, u32[]{:S(2)}, u32[]{:S(2)}) collective-permute-start(bf16[2,128,1,128]{3,1,2,0:T(8,128)(2,1)S(1)} %pad_maximum_fusion.2), channel_id=1, source_target_pairs={{0,16},{4,20},{8,24},{12,28},{16,32},{20,36},{24,40},{28,44},{32,4... | collective-permute-start | bytes 196616 | tf_op jit(solution)/shard_map/ppermute | solution.py:16
  27.4 4.3 %collective-permute-start.4 = (bf16[2,128,1,128]{3,1,2,0:T(8,128)(2,1)S(1)}, bf16[2,128,1,128]{3,1,2,0:T(8,128)(2,1)S(1)}, u32[]{:S(2)}, u32[]{:S(2)}) collective-permute-start(bf16[2,128,1,128]{3,1,2,0:T(8,128)(2,1)S(1)} %pad_maximum_fusion.2), channel_id=1, source_target_pairs={{0,20},{4,24},{8,28},{12,32},{16,36},{20,40},{24,44},{28,48},{32,5... | collective-permute-start | bytes 196616 | tf_op jit(solution)/shard_map/ppermute | solution.py:16
  37.7 7.1 %fusion.13 = bf16[2048,1024]{1,0:T(8,128)(2,1)} fusion(bf16[128,1024]{1,0:T(8,128)(2,1)} %param.11, s32[1024]{0:T(1024)S(1)} %eq.52, s32[1024]{0:T(1024)S(1)} %add_select_fusion), kind=kOutput, calls=%fused_computation.33 | convolution fusion | flops 1076232192 | bytes 4464640 | tf_op jit(solution)/shard_map/dot_general | solution.py:97
  46.7 6.8 %collective-permute-start.6 = (bf16[2,128,1,128]{3,1,2,0:T(8,128)(2,1)S(1)}, bf16[2,128,1,128]{3,1,2,0:T(8,128)(2,1)S(1)}, u32[]{:S(2)}, u32[]{:S(2)}) collective-permute-start(bf16[2,128,1,128]{3,1,2,0:T(8,128)(2,1)S(1)} %pad_maximum_fusion.2), channel_id=1, source_target_pairs={{0,28},{4,32},{8,36},{12,40},{16,44},{20,48},{24,52},{28,56},{32,6... | collective-permute-start | bytes 196616 | tf_op jit(solution)/shard_map/ppermute | solution.py:16
  53.5 4.5 %select_convert_fusion = bf16[128,16,1024]{2,1,0:T(8,128)(2,1)} fusion(bf16[128,16,1024]{2,1,0:T(8,128)(2,1)} %bitcast.192, bf16[128,1024]{1,0:T(8,128)(2,1)S(1)} %pad.4, pred[16]{0:T(512)(128)(4,1)S(1)} %iota_compare_fusion.13), kind=kLoop, calls=%fused_computation.1 | loop fusion | flops 2097152 | bytes 8650768 | tf_op jit(solution)/shard_map/convert_element_type | solution.py:103
  58.3 13.8 %all-to-all-start = ((bf16[128,16,1024]{2,1,0:T(8,128)(2,1)}), bf16[128,16,1024]{2,1,0:T(8,128)(2,1)}, u32[]{:S(2)}, u32[]{:S(2)}) async-start(bf16[128,16,1024]{2,1,0:T(8,128)(2,1)} %select_convert_fusion), calls=%async_computation | async-start | bytes 8388608 | tf_op jit(solution)/shard_map/all_to_all | solution.py:113
  72.3 103.4 %all-to-all-done = bf16[128,16,1024]{2,1,0:T(8,128)(2,1)} async-done(((bf16[128,16,1024]{2,1,0:T(8,128)(2,1)}), bf16[128,16,1024]{2,1,0:T(8,128)(2,1)}, u32[]{:S(2)}, u32[]{:S(2)}) %all-to-all-start) | async-done | bytes 4194336 | tf_op jit(solution)/shard_map/all_to_all | solution.py:113
  175.7 6.2 %reshape.460 = bf16[1536,1024]{1,0:T(8,128)(2,1)} reshape(bf16[128,12,1024]{2,1,0:T(8,128)(2,1)} %bitcast.186) | data formatting | bytes 6291456 | tf_op jit(solution)/shard_map/reshape | solution.py:114
  181.9 5.9 %convolution_convert_fusion = bf16[1536,768]{0,1:T(8,128)(2,1)} fusion(bf16[1536,1024]{1,0:T(8,128)(2,1)} %reshape.460, bf16[1,768,1024]{2,1,0:T(8,128)(2,1)S(1)} %copy-done), kind=kOutput, calls=%fused_computation.16 | convolution fusion | flops 2417098752 | bytes 7077888 | tf_op jit(solution)/shard_map/dot_general | solution.py:118
  187.8 4.7 %all-to-all-start.1 = ((bf16[4,192,1536]{2,1,0:T(8,128)(2,1)}), bf16[4,192,1536]{2,1,0:T(8,128)(2,1)}, u32[]{:S(2)}, u32[]{:S(2)}) async-start(bf16[4,192,1536]{2,1,0:T(8,128)(2,1)} %bitcast.193), calls=%async_computation.1 | async-start | bytes 4718592 | tf_op jit(solution)/shard_map/all_to_all | solution.py:121
  193.6 28.3 %all-to-all-done.1 = bf16[4,192,1536]{2,1,0:T(8,128)(2,1)} async-done(((bf16[4,192,1536]{2,1,0:T(8,128)(2,1)}), bf16[4,192,1536]{2,1,0:T(8,128)(2,1)}, u32[]{:S(2)}, u32[]{:S(2)}) %all-to-all-start.1) | async-done | bytes 2359328 | tf_op jit(solution)/shard_map/all_to_all | solution.py:121
  221.9 2.1 convert_reduce_fusion
  227.8 2.4 collective-permute-done.7
  232.4 3.8 collective-permute-done.8
  236.2 52.9 %all-gather = f32[128,1,1536]{2,1,0:T(1,128)S(1)} all-gather(f32[1,1,1536]{2,1,0:T(1,128)S(1)} %reshape.479), channel_id=1, replica_groups=mesh['seq'=128,'head'=4] {'seq'}, dimensions={0}, use_global_device_ids=true | all-gather | bytes 792576 | tf_op jit(solution)/shard_map/all_gather | solution.py:137
  289.1 6.1 %gather_fusion = f32[1024]{0:T(1024)S(1)} fusion(f32[196608]{0:T(1024)S(1)} %bitcast.187, s32[1024]{0:T(1024)S(1)} %broadcast_clamp_fusion), kind=kCustom, calls=%fused_computation | custom fusion | bytes 12288 | tf_op jit(solution)/shard_map/jit(_take)/gather | solution.py:139
  298.4 2.1 fusion.15
  309.4 2.7 fusion.19
  312.1 12.3 %all-gather.6.cloned.1.call-done = bf16[128,4096]{1,0:T(8,128)(2,1)} async-done(((bf16[128,1024]{1,0:T(8,128)(2,1)}), bf16[128,4096]{1,0:T(8,128)(2,1)}) %all-gather.6.cloned.1.call-update) | async-done | bytes 1048592 | tf_op jit(solution)/shard_map/all_gather | solution.py:144
  324.4 5.1 %convolution_convert_fusion.1 = bf16[128,1024]{1,0:T(8,128)(2,1)S(1)} fusion(bf16[128,4096]{1,0:T(8,128)(2,1)} %all-gather.6.cloned.1.call-done, bf16[1024,4096]{0,1:T(8,128)(2,1)} %all-gather.4.cloned.1.call-done), kind=kOutput, calls=%fused_computation.39 | convolution fusion | flops 1073872896 | bytes 9699328 | tf_op jit(solution)/shard_map/dot_general | solution.py:145
  330.9 3.4 convert_bitcast_fusion
  334.4 4.2 %copy.99 = bf16[8,128,1024]{2,0,1:T(8,128)(2,1)} copy(bf16[8,128,1024]{1,2,0:T(8,128)(2,1)} %get-tuple-element.54) | data formatting | bytes 4194304 | tf_op jit(solution)/shard_map/reshape.33
  340.9 2.4 fusion.14
  344.0 9.5 %collective-permute-start.15 = (bf16[2,128,1,128]{3,1,2,0:T(8,128)(2,1)S(1)}, bf16[2,128,1,128]{3,1,2,0:T(8,128)(2,1)S(1)}, u32[]{:S(2)}, u32[]{:S(2)}) collective-permute-start(bf16[2,128,1,128]{3,1,2,0:T(8,128)(2,1)S(1)} %get-tuple-element.59), channel_id=1, source_target_pairs={{28,0},{32,4},{36,8},{40,12},{44,16},{48,20},{52,24},{56,28},{60,3... | collective-permute-start | bytes 196616 | tf_op jit(solution)/shard_map/ppermute | solution.py:16
  353.5 2.5 collective-permute-start.14
  357.2 5.2 %collective-permute-start.13 = (bf16[2,128,1,128]{3,1,0,2:T(8,128)(2,1)}, bf16[2,128,1,128]{3,1,0,2:T(8,128)(2,1)S(1)}, u32[]{:S(2)}, u32[]{:S(2)}) collective-permute-start(bf16[2,128,1,128]{3,1,0,2:T(8,128)(2,1)} %get-tuple-element.61), channel_id=1, source_target_pairs={{20,0},{24,4},{28,8},{32,12},{36,16},{40,20},{44,24},{48,28},{52,3... | collective-permute-start | bytes 196616 | tf_op jit(solution)/shard_map/ppermute | solution.py:16
  362.3 3.6 collective-permute-start.12
  366.0 4.4 %collective-permute-start.11 = (bf16[2,128,1,128]{3,1,0,2:T(8,128)(2,1)S(1)}, bf16[2,128,1,128]{3,1,0,2:T(8,128)(2,1)S(1)}, u32[]{:S(2)}, u32[]{:S(2)}) collective-permute-start(bf16[2,128,1,128]{3,1,0,2:T(8,128)(2,1)S(1)} %get-tuple-element.63), channel_id=1, source_target_pairs={{12,0},{16,4},{20,8},{24,12},{28,16},{32,20},{36,24},{40,28},{44,3... | collective-permute-start | bytes 196616 | tf_op jit(solution)/shard_map/ppermute | solution.py:16
  372.4 2.2 collective-permute-start.9
  (127 shorter events, 41.1 us)
Async XLA Ops:
  7.2 174.7 %copy-start = (bf16[1,768,1024]{2,1,0:T(8,128)(2,1)S(1)}, bf16[1,768,1024]{2,1,0:T(8,128)(2,1)}, u32[]{:S(2)}) copy-start(bf16[1,768,1024]{2,1,0:T(8,128)(2,1)} %param.16) | copy-start | bytes 4718596
  7.2 218.5 %all-gather.4.cloned.1.call-start = ((), (), s32[]{:S(2)}) async-start(), calls=%async_computation.2 | async-start | bytes 8454144 | tf_op jit(solution)/shard_map/all_gather | solution.py:104
  8.7 38.0 %copy-start.10 = (bf16[2,128,1,128]{3,1,2,0:T(8,128)(2,1)}, bf16[2,128,1,128]{3,1,2,0:T(8,128)(2,1)S(1)}, u32[]{:S(2)}) copy-start(bf16[2,128,1,128]{3,1,2,0:T(8,128)(2,1)S(1)} %pad_maximum_fusion.2) | copy-start | bytes 196612
  8.7 36.0 %collective-permute-start = (bf16[2,128,1,128]{3,1,2,0:T(8,128)(2,1)S(1)}, bf16[2,128,1,128]{3,1,2,0:T(8,128)(2,1)S(1)}, u32[]{:S(2)}, u32[]{:S(2)}) collective-permute-start(bf16[2,128,1,128]{3,1,2,0:T(8,128)(2,1)S(1)} %pad_maximum_fusion.2), channel_id=1, source_target_pairs={{0,4},{4,8},{8,12},{12,16},{16,20},{20,24},{24,28},{28,32},{32,36}... | collective-permute-start | bytes 196616 | tf_op jit(solution)/shard_map/ppermute | solution.py:16
  13.3 33.4 %collective-permute-start.1 = (bf16[2,128,1,128]{3,1,2,0:T(8,128)(2,1)S(1)}, bf16[2,128,1,128]{3,1,2,0:T(8,128)(2,1)S(1)}, u32[]{:S(2)}, u32[]{:S(2)}) collective-permute-start(bf16[2,128,1,128]{3,1,2,0:T(8,128)(2,1)S(1)} %pad_maximum_fusion.2), channel_id=1, source_target_pairs={{0,8},{4,12},{8,16},{12,20},{16,24},{20,28},{24,32},{28,36},{32,40... | collective-permute-start | bytes 196616 | tf_op jit(solution)/shard_map/ppermute | solution.py:16
  17.3 40.7 %collective-permute-start.2 = (bf16[2,128,1,128]{3,1,2,0:T(8,128)(2,1)S(1)}, bf16[2,128,1,128]{3,1,2,0:T(8,128)(2,1)S(1)}, u32[]{:S(2)}, u32[]{:S(2)}) collective-permute-start(bf16[2,128,1,128]{3,1,2,0:T(8,128)(2,1)S(1)} %pad_maximum_fusion.2), channel_id=1, source_target_pairs={{0,12},{4,16},{8,20},{12,24},{16,28},{20,32},{24,36},{28,40},{32,4... | collective-permute-start | bytes 196616 | tf_op jit(solution)/shard_map/ppermute | solution.py:16
  21.3 36.7 %collective-permute-start.3 = (bf16[2,128,1,128]{3,1,2,0:T(8,128)(2,1)S(1)}, bf16[2,128,1,128]{3,1,2,0:T(8,128)(2,1)S(1)}, u32[]{:S(2)}, u32[]{:S(2)}) collective-permute-start(bf16[2,128,1,128]{3,1,2,0:T(8,128)(2,1)S(1)} %pad_maximum_fusion.2), channel_id=1, source_target_pairs={{0,16},{4,20},{8,24},{12,28},{16,32},{20,36},{24,40},{28,44},{32,4... | collective-permute-start | bytes 196616 | tf_op jit(solution)/shard_map/ppermute | solution.py:16
  27.4 30.6 %collective-permute-start.4 = (bf16[2,128,1,128]{3,1,2,0:T(8,128)(2,1)S(1)}, bf16[2,128,1,128]{3,1,2,0:T(8,128)(2,1)S(1)}, u32[]{:S(2)}, u32[]{:S(2)}) collective-permute-start(bf16[2,128,1,128]{3,1,2,0:T(8,128)(2,1)S(1)} %pad_maximum_fusion.2), channel_id=1, source_target_pairs={{0,20},{4,24},{8,28},{12,32},{16,36},{20,40},{24,44},{28,48},{32,5... | collective-permute-start | bytes 196616 | tf_op jit(solution)/shard_map/ppermute | solution.py:16
  32.5 5.0 %copy-start.9 = (s32[128,8]{1,0:T(8,128)}, s32[128,8]{1,0:T(8,128)S(1)}, u32[]{:S(2)}) copy-start(s32[128,8]{1,0:T(8,128)S(1)} %copy.88) | copy-start | bytes 12292
  44.8 13.2 %copy-start.14 = (bf16[2,128,1,128]{3,1,2,0:T(8,128)(2,1)}, bf16[2,128,1,128]{3,1,2,0:T(8,128)(2,1)S(1)}, u32[]{:S(2)}) copy-start(bf16[2,128,1,128]{3,1,2,0:T(8,128)(2,1)S(1)} %collective-permute-done) | copy-start | bytes 196612
  44.8 13.3 %collective-permute-start.5 = (bf16[2,128,1,128]{3,1,2,0:T(8,128)(2,1)S(1)}, bf16[2,128,1,128]{3,1,2,0:T(8,128)(2,1)S(1)}, u32[]{:S(2)}, u32[]{:S(2)}) collective-permute-start(bf16[2,128,1,128]{3,1,2,0:T(8,128)(2,1)S(1)} %pad_maximum_fusion.2), channel_id=1, source_target_pairs={{0,24},{4,28},{8,32},{12,36},{16,40},{20,44},{24,48},{28,52},{32,5... | collective-permute-start | bytes 196616 | tf_op jit(solution)/shard_map/ppermute | solution.py:16
  46.7 11.6 %collective-permute-start.6 = (bf16[2,128,1,128]{3,1,2,0:T(8,128)(2,1)S(1)}, bf16[2,128,1,128]{3,1,2,0:T(8,128)(2,1)S(1)}, u32[]{:S(2)}, u32[]{:S(2)}) collective-permute-start(bf16[2,128,1,128]{3,1,2,0:T(8,128)(2,1)S(1)} %pad_maximum_fusion.2), channel_id=1, source_target_pairs={{0,28},{4,32},{8,36},{12,40},{16,44},{20,48},{24,52},{28,56},{32,6... | collective-permute-start | bytes 196616 | tf_op jit(solution)/shard_map/ppermute | solution.py:16
  58.3 117.4 %all-to-all-start = ((bf16[128,16,1024]{2,1,0:T(8,128)(2,1)}), bf16[128,16,1024]{2,1,0:T(8,128)(2,1)}, u32[]{:S(2)}, u32[]{:S(2)}) async-start(bf16[128,16,1024]{2,1,0:T(8,128)(2,1)} %select_convert_fusion), calls=%async_computation | async-start | bytes 8388608 | tf_op jit(solution)/shard_map/all_to_all | solution.py:113
  187.8 34.1 %all-to-all-start.1 = ((bf16[4,192,1536]{2,1,0:T(8,128)(2,1)}), bf16[4,192,1536]{2,1,0:T(8,128)(2,1)}, u32[]{:S(2)}, u32[]{:S(2)}) async-start(bf16[4,192,1536]{2,1,0:T(8,128)(2,1)} %bitcast.193), calls=%async_computation.1 | async-start | bytes 4718592 | tf_op jit(solution)/shard_map/all_to_all | solution.py:121
  192.5 132.0 %all-gather.6.cloned.1.call-start = ((), (), s32[]{:S(2)}) async-start(), calls=%async_computation.3 | async-start | bytes 1310720 | tf_op jit(solution)/shard_map/all_gather | solution.py:144
  225.6 69.7 %copy-start.11 = (f32[128,8]{0,1:T(8,128)S(1)}, f32[128,8]{0,1:T(8,128)}, u32[]{:S(2)}) copy-start(f32[128,8]{0,1:T(8,128)} %param.13) | copy-start | bytes 12292
  225.7 4.6 %collective-permute-start.7 = (f32[1536]{0:T(1024)S(1)}, f32[1536]{0:T(1024)S(1)}, u32[]{:S(2)}, u32[]{:S(2)}) collective-permute-start(f32[1536]{0:T(1024)S(1)} %fusion.22), channel_id=1, source_target_pairs={{0,1},{1,0},{2,3},{3,2},{4,5},{5,4},{6,7},{7,6},{8,9},{9,8},{10,11... | collective-permute-start | bytes 18440 | tf_op jit(solution)/shard_map/ppermute | solution.py:24
  230.2 5.9 %collective-permute-start.8 = (f32[1536]{0:T(1024)S(1)}, f32[1536]{0:T(1024)S(1)}, u32[]{:S(2)}, u32[]{:S(2)}) collective-permute-start(f32[1536]{0:T(1024)S(1)} %add.161), channel_id=1, source_target_pairs={{0,2},{1,3},{2,0},{3,1},{4,6},{5,7},{6,4},{7,5},{8,10},{9,11},{10,... | collective-permute-start | bytes 18440 | tf_op jit(solution)/shard_map/ppermute | solution.py:24
  296.1 9.2 %copy-start.15 = (f32[128,8]{0,1:T(8,128)}, f32[128,8]{0,1:T(8,128)S(1)}, u32[]{:S(2)}) copy-start(f32[128,8]{0,1:T(8,128)S(1)} %get-tuple-element.53) | copy-start | bytes 12292
  298.4 8.9 %copy-start.5 = (pred[128,1024]{0,1:T(8,128)(4,1)S(1)}, pred[128,1024]{0,1:T(8,128)(4,1)}, u32[]{:S(2)}) copy-start(pred[128,1024]{0,1:T(8,128)(4,1)} %compare_and_fusion) | copy-start | bytes 393220
  312.1 17.4 %copy-start.7 = (bf16[2,1024,1,128]{3,1,2,0:T(8,128)(2,1)S(1)}, bf16[2,1024,1,128]{3,1,2,0:T(8,128)(2,1)}, u32[]{:S(2)}) copy-start(bf16[2,1024,1,128]{3,1,2,0:T(8,128)(2,1)} %constant_dynamic-update-slice_fusion) | copy-start | bytes 1572868
  324.4 5.1 %copy-start.2 = (f32[1024,128,8]{1,0,2:T(8,128)S(1)}, f32[1024,128,8]{1,0,2:T(8,128)}, u32[]{:S(2)}) copy-start(f32[1024,128,8]{1,0,2:T(8,128)} %copy-done.1) | copy-start | bytes 12582916
  340.8 15.2 %copy-start.4 = (bf16[1,1,192,1536]{3,2,1,0:T(8,128)(2,1)S(1)}, bf16[1,1,192,1536]{3,2,1,0:T(8,128)(2,1)}, u32[]{:S(2)}) copy-start(bf16[1,1,192,1536]{3,2,1,0:T(8,128)(2,1)} %get-tuple-element.57) | copy-start | bytes 1769476
  343.2 31.4 %copy-start.3 = (bf16[8,128,1024]{1,2,0:T(8,128)(2,1)S(1)}, bf16[8,128,1024]{1,2,0:T(8,128)(2,1)}, u32[]{:S(2)}) copy-start(bf16[8,128,1024]{1,2,0:T(8,128)(2,1)} %get-tuple-element.55) | copy-start | bytes 6291460
  343.2 31.4 %copy-start.8 = (bf16[2,1024,1,128]{3,1,2,0:T(8,128)(2,1)S(1)}, bf16[2,1024,1,128]{3,1,2,0:T(8,128)(2,1)}, u32[]{:S(2)}) copy-start(bf16[2,1024,1,128]{3,1,2,0:T(8,128)(2,1)} %constant_dynamic-update-slice_fusion) | copy-start | bytes 1572868
  344.0 26.4 %collective-permute-start.15 = (bf16[2,128,1,128]{3,1,2,0:T(8,128)(2,1)S(1)}, bf16[2,128,1,128]{3,1,2,0:T(8,128)(2,1)S(1)}, u32[]{:S(2)}, u32[]{:S(2)}) collective-permute-start(bf16[2,128,1,128]{3,1,2,0:T(8,128)(2,1)S(1)} %get-tuple-element.59), channel_id=1, source_target_pairs={{28,0},{32,4},{36,8},{40,12},{44,16},{48,20},{52,24},{56,28},{60,3... | collective-permute-start | bytes 196616 | tf_op jit(solution)/shard_map/ppermute | solution.py:16
  353.5 18.9 %collective-permute-start.14 = (bf16[2,128,1,128]{3,1,0,2:T(8,128)(2,1)S(1)}, bf16[2,128,1,128]{3,1,0,2:T(8,128)(2,1)S(1)}, u32[]{:S(2)}, u32[]{:S(2)}) collective-permute-start(bf16[2,128,1,128]{3,1,0,2:T(8,128)(2,1)S(1)} %get-tuple-element.60), channel_id=1, source_target_pairs={{24,0},{28,4},{32,8},{36,12},{40,16},{44,20},{48,24},{52,28},{56,3... | collective-permute-start | bytes 196616 | tf_op jit(solution)/shard_map/ppermute | solution.py:16
  357.2 18.9 %collective-permute-start.13 = (bf16[2,128,1,128]{3,1,0,2:T(8,128)(2,1)}, bf16[2,128,1,128]{3,1,0,2:T(8,128)(2,1)S(1)}, u32[]{:S(2)}, u32[]{:S(2)}) collective-permute-start(bf16[2,128,1,128]{3,1,0,2:T(8,128)(2,1)} %get-tuple-element.61), channel_id=1, source_target_pairs={{20,0},{24,4},{28,8},{32,12},{36,16},{40,20},{44,24},{48,28},{52,3... | collective-permute-start | bytes 196616 | tf_op jit(solution)/shard_map/ppermute | solution.py:16
  362.3 13.7 %collective-permute-start.12 = (bf16[2,128,1,128]{3,1,0,2:T(8,128)(2,1)}, bf16[2,128,1,128]{3,1,0,2:T(8,128)(2,1)S(1)}, u32[]{:S(2)}, u32[]{:S(2)}) collective-permute-start(bf16[2,128,1,128]{3,1,0,2:T(8,128)(2,1)} %get-tuple-element.62), channel_id=1, source_target_pairs={{16,0},{20,4},{24,8},{28,12},{32,16},{36,20},{40,24},{44,28},{48,3... | collective-permute-start | bytes 196616 | tf_op jit(solution)/shard_map/ppermute | solution.py:16
  366.0 10.1 %collective-permute-start.11 = (bf16[2,128,1,128]{3,1,0,2:T(8,128)(2,1)S(1)}, bf16[2,128,1,128]{3,1,0,2:T(8,128)(2,1)S(1)}, u32[]{:S(2)}, u32[]{:S(2)}) collective-permute-start(bf16[2,128,1,128]{3,1,0,2:T(8,128)(2,1)S(1)} %get-tuple-element.63), channel_id=1, source_target_pairs={{12,0},{16,4},{20,8},{24,12},{28,16},{32,20},{36,24},{40,28},{44,3... | collective-permute-start | bytes 196616 | tf_op jit(solution)/shard_map/ppermute | solution.py:16
  370.4 5.7 %collective-permute-start.10 = (bf16[2,128,1,128]{3,1,0,2:T(8,128)(2,1)S(1)}, bf16[2,128,1,128]{3,1,0,2:T(8,128)(2,1)S(1)}, u32[]{:S(2)}, u32[]{:S(2)}) collective-permute-start(bf16[2,128,1,128]{3,1,0,2:T(8,128)(2,1)S(1)} %get-tuple-element.64), channel_id=1, source_target_pairs={{8,0},{12,4},{16,8},{20,12},{24,16},{28,20},{32,24},{36,28},{40,32... | collective-permute-start | bytes 196616 | tf_op jit(solution)/shard_map/ppermute | solution.py:16
  372.4 5.6 %collective-permute-start.9 = (bf16[2,128,1,128]{3,1,0,2:T(8,128)(2,1)S(1)}, bf16[2,128,1,128]{3,1,0,2:T(8,128)(2,1)S(1)}, u32[]{:S(2)}, u32[]{:S(2)}) collective-permute-start(bf16[2,128,1,128]{3,1,0,2:T(8,128)(2,1)S(1)} %get-tuple-element.58), channel_id=1, source_target_pairs={{4,0},{8,4},{12,8},{16,12},{20,16},{24,20},{28,24},{32,28},{36,32}... | collective-permute-start | bytes 196616 | tf_op jit(solution)/shard_map/ppermute | solution.py:16
  (7 other events, 19.6 us)
Sparse Core Ops, SparseCore 0:
  11.1 182.7 all-gather.3
  300.7 23.7 all-gather.5

commit v7 on v5

--- a/solution.py
+++ b/solution.py
@@ -101,7 +101,6 @@
     payload = jnp.where(
         is_weight, weight_row[:, None, :], send_rows.reshape(experts, pad, features)
     ).astype(jnp.bfloat16)
-    weight_full = lax.all_gather(out_weight, "seq", axis=1, tiled=True)
     kv_heads = key.shape[1]
     head_dim = key.shape[2]
     group = query.shape[1] // kv_heads
@@ -110,7 +109,10 @@
     for distance in range(1, REACH + 1):
         blocks.append(passed_along(paired, "seq", distance))
     sent_payload = lax.all_to_all(payload, "seq", split_axis=0, concat_axis=0, tiled=True)
-    sent_payload, blocks = lax.optimization_barrier((sent_payload, tuple(blocks)))
+    sent_payload, blocks, weight_local = lax.optimization_barrier(
+        (sent_payload, tuple(blocks), out_weight)
+    )
+    weight_full = lax.all_gather(weight_local, "seq", axis=1, tiled=True)
     slot_rows = sent_payload[:, :capacity, :].reshape(slots_all, features)
     sent_weight = sent_payload[:, capacity, :capacity].reshape(slots_all)
     weight_here = w_down[0]
@@ -132,7 +134,6 @@
     gate_up_grad = jnp.stack([scaled * up * sig * (1.0 + gate * (1.0 - sig)), scaled * act])[
         None
     ].astype(jnp.bfloat16)
-    slot_part, weight_full = lax.optimization_barrier((slot_part, weight_full))
     slot_grad = head_sum(slot_part)
     returned = lax.all_to_all(
         slot_grad.reshape(seq_count, capacity), "seq", split_axis=0, concat_axis=0, tiled=True
@@ -142,6 +143,7 @@
     dense = jnp.einsum("tk,tke->te", logit_grad, hits, precision=highest)
     router_term = jnp.dot(dense, router.astype(jnp.float32), precision=highest)
     input_slice = (out_grad.astype(jnp.float32) + router_term).astype(jnp.bfloat16)
+    input_slice, weight_full = lax.optimization_barrier((input_slice, weight_full))
     input_grad = lax.all_gather(input_slice, "head", axis=1, tiled=True)
     attn_grad = lax.dot_general(
         input_grad,
@@ -164,11 +166,15 @@
     pieces = jnp.stack([key_part, value_part]).reshape(
         2, REACH + 1, tokens_here, kv_heads, head_dim
     )
-    totals = pieces[:, REACH]
-    for distance in range(1, REACH + 1):
-        totals = totals + passed_along(
-            pieces[:, REACH - distance].astype(jnp.bfloat16), "seq", -distance
+    current = pieces[:, ::-1]
+    width = REACH + 1
+    while width > 1:
+        half = width // 2
+        current = current[:, :half] + passed_along(
+            current[:, half:width].astype(jnp.bfloat16), "seq", -half
         ).astype(jnp.float32)
+        width = half
+    totals = current[:, 0]
     return (
         gate_up_grad,
         route_grad,

time: 352 us -> 354 us (level)
  the two profiles are of different devices: /device:TPU:49 before, /device:TPU:32 now
where the time goes in v7:
time: 354 us; the launch traced here: 352 us
  waiting for transfers between devices  140 us (40%)
  starting transfers between devices  100 us (28%)
  local copies, waits for them, and re-layouts  42.3 us (12%)
  matrix products  30.3 us (9%)
  other arithmetic  24.4 us (7%)
  between operations  14.7 us (4%)
    ppermute x10, waiting for transfers between devices, passed_along(): return lax.ppermute(array, axis, pairs)  92.1 us
    ppermute x10, starting transfers between devices, passed_along(): return lax.ppermute(array, axis, pairs)  54.4 us
    all_to_all x1, waiting for transfers between devices, per_device(): lax.all_to_all(partial.reshape(head_count, -1, slots_all), 'head', split_...  28.5 us
    all_to_all x1, starting transfers between devices, per_device(): lax.all_to_all(payload, 'seq', split_axis=0, concat_axis=0, tiled=True)  17.9 us
    all_to_all x1, starting transfers between devices, per_device(): lax.all_to_all(slot_grad.reshape(seq_count, capacity), 'seq', split_axis=...  17.9 us
    unnamed x56, local copies, waits for them, and re-layouts  16.3 us
    gather x3, local copies, waits for them, and re-layouts, per_device(): jnp.take(returned.reshape(-1), target.reshape(-1))  7.75 us
    ppermute x2, waiting for transfers between devices, head_sum(): part = part + lax.ppermute(part, 'head', pairs)  7.55 us
  transfers between devices with their start and end apart: 17, of which 10 were waited for; matrix products, arithmetic and copies ran while one was open for 15% of the time, Pallas kernels for 0%

profile of v7, /device:TPU:32, one launch (start us, length us, event | category | flops | bytes accessed | tf_op | source)
XLA Modules:
  0.0 352.3 jit_solution(12235253278459984688)
XLA Ops:
  13.2 7.1 %fusion.13 = bf16[2048,1024]{1,0:T(8,128)(2,1)} fusion(bf16[128,1024]{1,0:T(8,128)(2,1)} %param.11, s32[1024]{0:T(1024)S(1)} %eq.52, s32[1024]{0:T(1024)S(1)} %add_select_fusion), kind=kOutput, calls=%fused_computation.30 | convolution fusion | flops 1076232192 | bytes 4464640 | tf_op jit(solution)/shard_map/dot_general | solution.py:97
  20.3 4.6 %select_convert_fusion = bf16[128,16,1024]{2,1,0:T(8,128)(2,1)} fusion(bf16[128,16,1024]{2,1,0:T(8,128)(2,1)} %bitcast.151, bf16[128,1024]{1,0:T(8,128)(2,1)S(1)} %pad.4, pred[16]{0:T(512)(128)(4,1)S(1)} %iota_compare_fusion.13), kind=kLoop, calls=%fused_computation.1 | loop fusion | flops 2097152 | bytes 8650768 | tf_op jit(solution)/shard_map/convert_element_type | solution.py:103
  24.9 17.9 %all-to-all-start = ((bf16[128,16,1024]{2,1,0:T(8,128)(2,1)}), bf16[128,16,1024]{2,1,0:T(8,128)(2,1)}, u32[]{:S(2)}, u32[]{:S(2)}) async-start(bf16[128,16,1024]{2,1,0:T(8,128)(2,1)} %select_convert_fusion), calls=%async_computation | async-start | bytes 8388608 | tf_op jit(solution)/shard_map/all_to_all | solution.py:111
  45.0 3.4 collective-permute-start.1
  48.4 4.2 %collective-permute-start.2 = (bf16[2,128,1,128]{3,1,2,0:T(8,128)(2,1)S(1)}, bf16[2,128,1,128]{3,1,2,0:T(8,128)(2,1)S(1)}, u32[]{:S(2)}, u32[]{:S(2)}) collective-permute-start(bf16[2,128,1,128]{3,1,2,0:T(8,128)(2,1)S(1)} %pad_maximum_fusion.2), channel_id=1, source_target_pairs={{0,12},{4,16},{8,20},{12,24},{16,28},{20,32},{24,36},{28,40},{32,4... | collective-permute-start | bytes 196616 | tf_op jit(solution)/shard_map/ppermute | solution.py:16
  52.5 4.6 %collective-permute-start.3 = (bf16[2,128,1,128]{3,1,2,0:T(8,128)(2,1)S(1)}, bf16[2,128,1,128]{3,1,2,0:T(8,128)(2,1)S(1)}, u32[]{:S(2)}, u32[]{:S(2)}) collective-permute-start(bf16[2,128,1,128]{3,1,2,0:T(8,128)(2,1)S(1)} %pad_maximum_fusion.2), channel_id=1, source_target_pairs={{0,16},{4,20},{8,24},{12,28},{16,32},{20,36},{24,40},{28,44},{32,4... | collective-permute-start | bytes 196616 | tf_op jit(solution)/shard_map/ppermute | solution.py:16
  57.1 2.1 collective-permute-start.4
  59.2 79.5 %collective-permute-done = bf16[2,128,1,128]{3,1,2,0:T(8,128)(2,1)S(1)} collective-permute-done((bf16[2,128,1,128]{3,1,2,0:T(8,128)(2,1)S(1)}, bf16[2,128,1,128]{3,1,2,0:T(8,128)(2,1)S(1)}, u32[]{:S(2)}, u32[]{:S(2)}) %collective-permute-start) | collective-permute-done | bytes 65568 | tf_op jit(solution)/shard_map/ppermute | solution.py:16
  138.7 3.1 collective-permute-start.5
  141.9 20.0 %collective-permute-start.6 = (bf16[2,128,1,128]{3,1,2,0:T(8,128)(2,1)S(1)}, bf16[2,128,1,128]{3,1,2,0:T(8,128)(2,1)}, u32[]{:S(2)}, u32[]{:S(2)}) collective-permute-start(bf16[2,128,1,128]{3,1,2,0:T(8,128)(2,1)S(1)} %pad_maximum_fusion.2), channel_id=1, source_target_pairs={{0,28},{4,32},{8,36},{12,40},{16,44},{20,48},{24,52},{28,56},{32,6... | collective-permute-start | bytes 196616 | tf_op jit(solution)/shard_map/ppermute | solution.py:16
  163.8 6.2 %reshape.381 = bf16[1536,1024]{1,0:T(8,128)(2,1)} reshape(bf16[128,12,1024]{2,1,0:T(8,128)(2,1)} %bitcast.146) | data formatting | bytes 6291456 | tf_op jit(solution)/shard_map/reshape | solution.py:116
  170.0 5.8 %convolution_convert_fusion = bf16[1536,768]{0,1:T(8,128)(2,1)} fusion(bf16[1536,1024]{1,0:T(8,128)(2,1)} %reshape.381, bf16[1,768,1024]{2,1,0:T(8,128)(2,1)S(1)} %copy-done), kind=kOutput, calls=%fused_computation.16 | convolution fusion | flops 2417098752 | bytes 7077888 | tf_op jit(solution)/shard_map/dot_general | solution.py:120
  175.8 4.7 %all-to-all-start.1 = ((bf16[4,192,1536]{2,1,0:T(8,128)(2,1)}), bf16[4,192,1536]{2,1,0:T(8,128)(2,1)}, u32[]{:S(2)}, u32[]{:S(2)}) async-start(bf16[4,192,1536]{2,1,0:T(8,128)(2,1)} %bitcast.152), calls=%async_computation.1 | async-start | bytes 4718592 | tf_op jit(solution)/shard_map/all_to_all | solution.py:123
  181.0 28.5 %all-to-all-done.1 = bf16[4,192,1536]{2,1,0:T(8,128)(2,1)} async-done(((bf16[4,192,1536]{2,1,0:T(8,128)(2,1)}), bf16[4,192,1536]{2,1,0:T(8,128)(2,1)}, u32[]{:S(2)}, u32[]{:S(2)}) %all-to-all-start.1) | async-done | bytes 2359328 | tf_op jit(solution)/shard_map/all_to_all | solution.py:123
  209.5 2.1 convert_reduce_fusion
  213.3 2.6 collective-permute-start.7
  216.0 3.0 collective-permute-done.7
  219.0 2.7 collective-permute-start.8
  221.7 4.5 %collective-permute-done.8 = f32[1536]{0:T(1024)S(1)} collective-permute-done((f32[1536]{0:T(1024)S(1)}, f32[1536]{0:T(1024)S(1)}, u32[]{:S(2)}, u32[]{:S(2)}) %collective-permute-start.8) | collective-permute-done | bytes 6176 | tf_op jit(solution)/shard_map/ppermute | solution.py:24
  227.0 17.9 %all-to-all-start.2 = ((f32[128,1,12]{2,1,0:T(1,128)}), f32[128,1,12]{2,1,0:T(1,128)S(1)}, u32[]{:S(2)}, u32[]{:S(2)}) async-start(f32[128,1,12]{2,1,0:T(1,128)} %bitcast.9), calls=%async_computation.2 | async-start | bytes 131072 | tf_op jit(solution)/shard_map/all_to_all | solution.py:138
  246.7 5.8 %all-to-all-done.2 = f32[128,1,12]{2,1,0:T(1,128)S(1)} async-done(((f32[128,1,12]{2,1,0:T(1,128)}), f32[128,1,12]{2,1,0:T(1,128)S(1)}, u32[]{:S(2)}, u32[]{:S(2)}) %all-to-all-start.2) | async-done | bytes 6176 | tf_op jit(solution)/shard_map/all_to_all | solution.py:138
  253.9 6.2 %gather_fusion = f32[1024]{0:T(1024)S(1)} fusion(f32[1536]{0:T(1024)S(1)} %reshape.383, s32[1024]{0:T(1024)S(1)} %broadcast_clamp_fusion), kind=kCustom, calls=%fused_computation | custom fusion | bytes 12288 | tf_op jit(solution)/shard_map/jit(_take)/gather | solution.py:141
  284.8 6.3 %all-gather.5.cloned.1.call-done = bf16[128,4096]{1,0:T(8,128)(2,1)} async-done(((bf16[128,1024]{1,0:T(8,128)(2,1)}), bf16[128,4096]{1,0:T(8,128)(2,1)}) %all-gather.5.cloned.1.call-update) | async-done | bytes 1048592 | tf_op jit(solution)/shard_map/all_gather | solution.py:147
  291.1 5.1 %convolution_convert_fusion.1 = bf16[128,1024]{1,0:T(8,128)(2,1)S(1)} fusion(bf16[128,4096]{1,0:T(8,128)(2,1)} %all-gather.5.cloned.1.call-done, bf16[1024,4096]{0,1:T(8,128)(2,1)} %all-gather.3.cloned.1.call-done), kind=kOutput, calls=%fused_computation.36 | convolution fusion | flops 1073872896 | bytes 9699328 | tf_op jit(solution)/shard_map/dot_general | solution.py:148
  297.5 3.4 convert_bitcast_fusion
  301.0 4.2 %copy.95 = bf16[8,128,1024]{2,0,1:T(8,128)(2,1)} copy(bf16[8,128,1024]{1,2,0:T(8,128)(2,1)} %get-tuple-element.56) | data formatting | bytes 4194304 | tf_op jit(solution)/shard_map/reshape.35
  305.2 2.9 convolution_bitcast_fusion
  309.3 2.3 fusion.14
  313.2 6.7 %collective-permute-start.9 = (bf16[2,4,128,1,128]{4,2,3,1,0:T(8,128)(2,1)}, bf16[2,4,128,1,128]{4,2,3,1,0:T(8,128)(2,1)S(1)}, u32[]{:S(2)}, u32[]{:S(2)}) collective-permute-start(bf16[2,4,128,1,128]{4,2,3,1,0:T(8,128)(2,1)} %slice.109), channel_id=1, source_target_pairs={{16,0},{20,4},{24,8},{28,12},{32,16},{36,20},{40,24},{44,28},{48,3... | collective-permute-start | bytes 786440 | tf_op jit(solution)/shard_map/ppermute | solution.py:16
  321.8 10.1 %collective-permute-done.9 = bf16[2,4,128,1,128]{4,2,3,1,0:T(8,128)(2,1)S(1)} collective-permute-done((bf16[2,4,128,1,128]{4,2,3,1,0:T(8,128)(2,1)}, bf16[2,4,128,1,128]{4,2,3,1,0:T(8,128)(2,1)S(1)}, u32[]{:S(2)}, u32[]{:S(2)}) %collective-permute-start.9) | collective-permute-done | bytes 262176 | tf_op jit(solution)/shard_map/ppermute | solution.py:16
  332.1 6.1 %collective-permute-start.10 = (bf16[2,2,128,1,128]{4,2,3,1,0:T(8,128)(2,1)S(1)}, bf16[2,2,128,1,128]{4,2,3,1,0:T(8,128)(2,1)S(1)}, u32[]{:S(2)}, u32[]{:S(2)}) collective-permute-start(bf16[2,2,128,1,128]{4,2,3,1,0:T(8,128)(2,1)S(1)} %slice.110), channel_id=1, source_target_pairs={{8,0},{12,4},{16,8},{20,12},{24,16},{28,20},{32,24},{36,28},{40,32... | collective-permute-start | bytes 393224 | tf_op jit(solution)/shard_map/ppermute | solution.py:16
  340.7 2.2 collective-permute-start.11
  (136 shorter events, 51.9 us)
Async XLA Ops:
  7.2 162.8 %copy-start = (bf16[1,768,1024]{2,1,0:T(8,128)(2,1)S(1)}, bf16[1,768,1024]{2,1,0:T(8,128)(2,1)}, u32[]{:S(2)}) copy-start(bf16[1,768,1024]{2,1,0:T(8,128)(2,1)} %param.16) | copy-start | bytes 4718596
  11.3 13.6 %copy-start.21 = (f32[128]{0:T(128)}, f32[128]{0:T(128)S(1)}, u32[]{:S(2)}) copy-start(f32[128]{0:T(128)S(1)} %fusion.50) | copy-start | bytes 1540
  24.9 18.0 %copy-start.18 = (bf16[128,1,128]{2,0,1:T(8,128)(2,1)S(1)}, bf16[128,1,128]{2,0,1:T(8,128)(2,1)}, u32[]{:S(2)}) copy-start(bf16[128,1,128]{2,0,1:T(8,128)(2,1)} %param.21) | copy-start | bytes 98308
  24.9 18.0 %copy-start.19 = (bf16[128,1,128]{2,0,1:T(8,128)(2,1)S(1)}, bf16[128,1,128]{2,0,1:T(8,128)(2,1)}, u32[]{:S(2)}) copy-start(bf16[128,1,128]{2,0,1:T(8,128)(2,1)} %param.20) | copy-start | bytes 98308
  24.9 138.9 %all-to-all-start = ((bf16[128,16,1024]{2,1,0:T(8,128)(2,1)}), bf16[128,16,1024]{2,1,0:T(8,128)(2,1)}, u32[]{:S(2)}, u32[]{:S(2)}) async-start(bf16[128,16,1024]{2,1,0:T(8,128)(2,1)} %select_convert_fusion), calls=%async_computation | async-start | bytes 8388608 | tf_op jit(solution)/shard_map/all_to_all | solution.py:111
  42.8 224.5 %all-gather.3.cloned.1.call-start = ((), (), s32[]{:S(2)}) async-start(), calls=%async_computation.3 | async-start | bytes 8454144 | tf_op jit(solution)/shard_map/all_gather | solution.py:115
  42.9 99.0 %copy-start.10 = (bf16[2,128,1,128]{3,1,2,0:T(8,128)(2,1)}, bf16[2,128,1,128]{3,1,2,0:T(8,128)(2,1)S(1)}, u32[]{:S(2)}) copy-start(bf16[2,128,1,128]{3,1,2,0:T(8,128)(2,1)S(1)} %pad_maximum_fusion.2) | copy-start | bytes 196612
  42.9 95.8 %collective-permute-start = (bf16[2,128,1,128]{3,1,2,0:T(8,128)(2,1)S(1)}, bf16[2,128,1,128]{3,1,2,0:T(8,128)(2,1)S(1)}, u32[]{:S(2)}, u32[]{:S(2)}) collective-permute-start(bf16[2,128,1,128]{3,1,2,0:T(8,128)(2,1)S(1)} %pad_maximum_fusion.2), channel_id=1, source_target_pairs={{0,4},{4,8},{8,12},{12,16},{16,20},{20,24},{24,28},{28,32},{32,36}... | collective-permute-start | bytes 196616 | tf_op jit(solution)/shard_map/ppermute | solution.py:16
  45.0 96.9 %collective-permute-start.1 = (bf16[2,128,1,128]{3,1,2,0:T(8,128)(2,1)S(1)}, bf16[2,128,1,128]{3,1,2,0:T(8,128)(2,1)S(1)}, u32[]{:S(2)}, u32[]{:S(2)}) collective-permute-start(bf16[2,128,1,128]{3,1,2,0:T(8,128)(2,1)S(1)} %pad_maximum_fusion.2), channel_id=1, source_target_pairs={{0,8},{4,12},{8,16},{12,20},{16,24},{20,28},{24,32},{28,36},{32,40... | collective-permute-start | bytes 196616 | tf_op jit(solution)/shard_map/ppermute | solution.py:16
  48.4 113.5 %collective-permute-start.2 = (bf16[2,128,1,128]{3,1,2,0:T(8,128)(2,1)S(1)}, bf16[2,128,1,128]{3,1,2,0:T(8,128)(2,1)S(1)}, u32[]{:S(2)}, u32[]{:S(2)}) collective-permute-start(bf16[2,128,1,128]{3,1,2,0:T(8,128)(2,1)S(1)} %pad_maximum_fusion.2), channel_id=1, source_target_pairs={{0,12},{4,16},{8,20},{12,24},{16,28},{20,32},{24,36},{28,40},{32,4... | collective-permute-start | bytes 196616 | tf_op jit(solution)/shard_map/ppermute | solution.py:16
  52.5 109.4 %collective-permute-start.3 = (bf16[2,128,1,128]{3,1,2,0:T(8,128)(2,1)S(1)}, bf16[2,128,1,128]{3,1,2,0:T(8,128)(2,1)S(1)}, u32[]{:S(2)}, u32[]{:S(2)}) collective-permute-start(bf16[2,128,1,128]{3,1,2,0:T(8,128)(2,1)S(1)} %pad_maximum_fusion.2), channel_id=1, source_target_pairs={{0,16},{4,20},{8,24},{12,28},{16,32},{20,36},{24,40},{28,44},{32,4... | collective-permute-start | bytes 196616 | tf_op jit(solution)/shard_map/ppermute | solution.py:16
  57.1 104.8 %collective-permute-start.4 = (bf16[2,128,1,128]{3,1,2,0:T(8,128)(2,1)S(1)}, bf16[2,128,1,128]{3,1,2,0:T(8,128)(2,1)S(1)}, u32[]{:S(2)}, u32[]{:S(2)}) collective-permute-start(bf16[2,128,1,128]{3,1,2,0:T(8,128)(2,1)S(1)} %pad_maximum_fusion.2), channel_id=1, source_target_pairs={{0,20},{4,24},{8,28},{12,32},{16,36},{20,40},{24,44},{28,48},{32,5... | collective-permute-start | bytes 196616 | tf_op jit(solution)/shard_map/ppermute | solution.py:16
  138.7 23.3 %copy-start.12 = (bf16[2,128,1,128]{3,1,2,0:T(8,128)(2,1)}, bf16[2,128,1,128]{3,1,2,0:T(8,128)(2,1)S(1)}, u32[]{:S(2)}) copy-start(bf16[2,128,1,128]{3,1,2,0:T(8,128)(2,1)S(1)} %collective-permute-done) | copy-start | bytes 196612
  138.7 23.2 %collective-permute-start.5 = (bf16[2,128,1,128]{3,1,2,0:T(8,128)(2,1)S(1)}, bf16[2,128,1,128]{3,1,2,0:T(8,128)(2,1)S(1)}, u32[]{:S(2)}, u32[]{:S(2)}) collective-permute-start(bf16[2,128,1,128]{3,1,2,0:T(8,128)(2,1)S(1)} %pad_maximum_fusion.2), channel_id=1, source_target_pairs={{0,24},{4,28},{8,32},{12,36},{16,40},{20,44},{24,48},{28,52},{32,5... | collective-permute-start | bytes 196616 | tf_op jit(solution)/shard_map/ppermute | solution.py:16
  141.9 20.1 %copy-start.13 = (bf16[2,128,1,128]{3,1,2,0:T(8,128)(2,1)}, bf16[2,128,1,128]{3,1,2,0:T(8,128)(2,1)S(1)}, u32[]{:S(2)}) copy-start(bf16[2,128,1,128]{3,1,2,0:T(8,128)(2,1)S(1)} %collective-permute-done.1) | copy-start | bytes 196612
  141.9 21.9 %collective-permute-start.6 = (bf16[2,128,1,128]{3,1,2,0:T(8,128)(2,1)S(1)}, bf16[2,128,1,128]{3,1,2,0:T(8,128)(2,1)}, u32[]{:S(2)}, u32[]{:S(2)}) collective-permute-start(bf16[2,128,1,128]{3,1,2,0:T(8,128)(2,1)S(1)} %pad_maximum_fusion.2), channel_id=1, source_target_pairs={{0,28},{4,32},{8,36},{12,40},{16,44},{20,48},{24,52},{28,56},{32,6... | collective-permute-start | bytes 196616 | tf_op jit(solution)/shard_map/ppermute | solution.py:16
  175.8 33.8 %all-to-all-start.1 = ((bf16[4,192,1536]{2,1,0:T(8,128)(2,1)}), bf16[4,192,1536]{2,1,0:T(8,128)(2,1)}, u32[]{:S(2)}, u32[]{:S(2)}) async-start(bf16[4,192,1536]{2,1,0:T(8,128)(2,1)} %bitcast.152), calls=%async_computation.1 | async-start | bytes 4718592 | tf_op jit(solution)/shard_map/all_to_all | solution.py:123
  211.6 50.0 %copy-start.11 = (f32[128,8]{0,1:T(8,128)S(1)}, f32[128,8]{0,1:T(8,128)}, u32[]{:S(2)}) copy-start(f32[128,8]{0,1:T(8,128)} %param.13) | copy-start | bytes 12292
  213.3 52.0 %copy-start.9 = (bf16[128,1024]{1,0:T(8,128)(2,1)S(1)}, bf16[128,1024]{1,0:T(8,128)(2,1)}, u32[]{:S(2)}) copy-start(bf16[128,1024]{1,0:T(8,128)(2,1)} %param.11) | copy-start | bytes 786436
  213.3 5.7 %collective-permute-start.7 = (f32[1536]{0:T(1024)S(1)}, f32[1536]{0:T(1024)S(1)}, u32[]{:S(2)}, u32[]{:S(2)}) collective-permute-start(f32[1536]{0:T(1024)S(1)} %fusion.22), channel_id=1, source_target_pairs={{0,1},{1,0},{2,3},{3,2},{4,5},{5,4},{6,7},{7,6},{8,9},{9,8},{10,11... | collective-permute-start | bytes 18440 | tf_op jit(solution)/shard_map/ppermute | solution.py:24
  219.0 7.2 %collective-permute-start.8 = (f32[1536]{0:T(1024)S(1)}, f32[1536]{0:T(1024)S(1)}, u32[]{:S(2)}, u32[]{:S(2)}) collective-permute-start(f32[1536]{0:T(1024)S(1)} %add.141), channel_id=1, source_target_pairs={{0,2},{1,3},{2,0},{3,1},{4,6},{5,7},{6,4},{7,5},{8,10},{9,11},{10,... | collective-permute-start | bytes 18440 | tf_op jit(solution)/shard_map/ppermute | solution.py:24
  227.0 25.5 %all-to-all-start.2 = ((f32[128,1,12]{2,1,0:T(1,128)}), f32[128,1,12]{2,1,0:T(1,128)S(1)}, u32[]{:S(2)}, u32[]{:S(2)}) async-start(f32[128,1,12]{2,1,0:T(1,128)} %bitcast.9), calls=%async_computation.2 | async-start | bytes 131072 | tf_op jit(solution)/shard_map/all_to_all | solution.py:138
  244.8 46.2 %all-gather.5.cloned.1.call-start = ((), (), s32[]{:S(2)}) async-start(), calls=%async_computation.4 | async-start | bytes 1310720 | tf_op jit(solution)/shard_map/all_gather | solution.py:147
  253.9 26.3 %copy-start.6 = (bf16[128,8,128]{2,1,0:T(8,128)(2,1)S(1)}, bf16[128,8,128]{2,1,0:T(8,128)(2,1)}, u32[]{:S(2)}) copy-start(bf16[128,8,128]{2,1,0:T(8,128)(2,1)} %param.19) | copy-start | bytes 786436
  262.4 19.5 %copy-start.20 = (f32[128,8]{0,1:T(8,128)}, f32[128,8]{0,1:T(8,128)S(1)}, u32[]{:S(2)}) copy-start(f32[128,8]{0,1:T(8,128)S(1)} %get-tuple-element.55) | copy-start | bytes 12292
  291.0 5.1 %copy-start.7 = (bf16[2,1024,1,128]{3,1,2,0:T(8,128)(2,1)S(1)}, bf16[2,1024,1,128]{3,1,2,0:T(8,128)(2,1)}, u32[]{:S(2)}) copy-start(bf16[2,1024,1,128]{3,1,2,0:T(8,128)(2,1)} %constant_dynamic-update-slice_fusion) | copy-start | bytes 1572868
  313.2 8.6 %copy-start.5 = (f32[1024,128]{1,0:T(8,128)S(1)}, f32[1024,128]{1,0:T(8,128)}, u32[]{:S(2)}) copy-start(f32[1024,128]{1,0:T(8,128)} %copy-done.4) | copy-start | bytes 1572868
  313.2 18.8 %collective-permute-start.9 = (bf16[2,4,128,1,128]{4,2,3,1,0:T(8,128)(2,1)}, bf16[2,4,128,1,128]{4,2,3,1,0:T(8,128)(2,1)S(1)}, u32[]{:S(2)}, u32[]{:S(2)}) collective-permute-start(bf16[2,4,128,1,128]{4,2,3,1,0:T(8,128)(2,1)} %slice.109), channel_id=1, source_target_pairs={{16,0},{20,4},{24,8},{28,12},{32,16},{36,20},{40,24},{44,28},{48,3... | collective-permute-start | bytes 786440 | tf_op jit(solution)/shard_map/ppermute | solution.py:16
  321.7 21.1 %copy-start.3 = (bf16[8,128,1024]{1,2,0:T(8,128)(2,1)S(1)}, bf16[8,128,1024]{1,2,0:T(8,128)(2,1)}, u32[]{:S(2)}) copy-start(bf16[8,128,1024]{1,2,0:T(8,128)(2,1)} %get-tuple-element.57) | copy-start | bytes 6291460
  321.7 21.1 %copy-start.8 = (bf16[2,1024,1,128]{3,1,2,0:T(8,128)(2,1)S(1)}, bf16[2,1024,1,128]{3,1,2,0:T(8,128)(2,1)}, u32[]{:S(2)}) copy-start(bf16[2,1024,1,128]{3,1,2,0:T(8,128)(2,1)} %constant_dynamic-update-slice_fusion) | copy-start | bytes 1572868
  332.1 8.6 %collective-permute-start.10 = (bf16[2,2,128,1,128]{4,2,3,1,0:T(8,128)(2,1)S(1)}, bf16[2,2,128,1,128]{4,2,3,1,0:T(8,128)(2,1)S(1)}, u32[]{:S(2)}, u32[]{:S(2)}) collective-permute-start(bf16[2,2,128,1,128]{4,2,3,1,0:T(8,128)(2,1)S(1)} %slice.110), channel_id=1, source_target_pairs={{8,0},{12,4},{16,8},{20,12},{24,16},{28,20},{32,24},{36,28},{40,32... | collective-permute-start | bytes 393224 | tf_op jit(solution)/shard_map/ppermute | solution.py:16
  340.7 4.1 %collective-permute-start.11 = (bf16[2,1,128,1,128]{4,2,3,1,0:T(8,128)(2,1)S(1)}, bf16[2,1,128,1,128]{4,2,3,1,0:T(8,128)(2,1)S(1)}, u32[]{:S(2)}, u32[]{:S(2)}) collective-permute-start(bf16[2,1,128,1,128]{4,2,3,1,0:T(8,128)(2,1)S(1)} %slice.111), channel_id=1, source_target_pairs={{4,0},{8,4},{12,8},{16,12},{20,16},{24,20},{28,24},{32,28},{36,32}... | collective-permute-start | bytes 196616 | tf_op jit(solution)/shard_map/ppermute | solution.py:16
  (8 other events, 15.4 us)
Sparse Core Ops, SparseCore 0:
  163.9 95.8 all-gather.2
  267.4 23.5 all-gather.4

commit v8 on v5

--- a/solution.py
+++ b/solution.py
@@ -84,9 +84,8 @@
     before = jnp.dot(earlier, per_token, precision=highest)
     rank = jnp.sum(hits * before[:, None, :], axis=2).astype(jnp.int32)
     target = expert_ids * capacity + rank
-    pad = -(-(capacity + 1) // 16) * 16
-    padded_target = (expert_ids * pad + rank).reshape(-1)
-    onehot = padded_target[None, :] == jnp.arange(experts * pad, dtype=jnp.int32)[:, None]
+    flat_target = target.reshape(-1)
+    onehot = flat_target[None, :] == jnp.arange(experts * capacity, dtype=jnp.int32)[:, None]
     token_of = (
         jnp.arange(tokens_here * top_count, dtype=jnp.int32)[:, None] // top_count
         == jnp.arange(tokens_here, dtype=jnp.int32)[None, :]
@@ -94,13 +93,15 @@
     pick = jnp.dot(
         onehot.astype(jnp.bfloat16), token_of, preferred_element_type=jnp.float32
     ).astype(jnp.bfloat16)
-    send_rows = jnp.dot(pick, out_grad, preferred_element_type=jnp.float32)
+    send_rows = jnp.dot(pick, out_grad, preferred_element_type=jnp.float32).astype(jnp.bfloat16)
     send_weight = jnp.sum(jnp.where(onehot, weights.reshape(-1)[None, :], 0.0), axis=1)
-    weight_row = jnp.pad(send_weight.reshape(experts, pad), ((0, 0), (0, features - pad)))
-    is_weight = (jnp.arange(pad) == capacity)[None, :, None]
-    payload = jnp.where(
-        is_weight, weight_row[:, None, :], send_rows.reshape(experts, pad, features)
-    ).astype(jnp.bfloat16)
+    lanes = 128
+    data_rows = capacity * features // lanes
+    weight_tile = jnp.zeros((experts, 16, lanes), jnp.float32)
+    weight_tile = weight_tile.at[:, 0, :capacity].set(send_weight.reshape(experts, capacity))
+    payload = jnp.concatenate(
+        [send_rows.reshape(experts, data_rows, lanes), weight_tile.astype(jnp.bfloat16)], axis=1
+    )
     weight_full = lax.all_gather(out_weight, "seq", axis=1, tiled=True)
     kv_heads = key.shape[1]
     head_dim = key.shape[2]
@@ -111,8 +112,8 @@
         blocks.append(passed_along(paired, "seq", distance))
     sent_payload = lax.all_to_all(payload, "seq", split_axis=0, concat_axis=0, tiled=True)
     sent_payload, blocks = lax.optimization_barrier((sent_payload, tuple(blocks)))
-    slot_rows = sent_payload[:, :capacity, :].reshape(slots_all, features)
-    sent_weight = sent_payload[:, capacity, :capacity].reshape(slots_all)
+    slot_rows = sent_payload[:, :data_rows, :].reshape(slots_all, features)
+    sent_weight = sent_payload[:, data_rows, :capacity].reshape(slots_all)
     weight_here = w_down[0]
     head_count = lax.axis_size("head")
     partial = lax.dot_general(

time: 352 us -> 360 us (1.023)
  local copies, waits for them, and re-layouts: 30.9 us -> 49.9 us
  waiting for transfers between devices: 132 us -> 121 us
    ppermute x14, waiting for transfers between devices: 84.3 us -> 73.3 us  [passed_along(): return lax.ppermute(array, axis, pairs)]
    gather x3, local copies, waits for them, and re-layouts: 6.54 us -> 13.1 us  [per_device(): jnp.take(returned.reshape(-1), target.reshape(-1))]
    reshape x2, local copies, waits for them, and re-layouts: 6.33 us -> 11.7 us  [the longest x1 5.89 us: per_device(): slot_rows = sent_payload[:, :data_rows, :].reshape(slots_all, features)]
    convert_element_type x1 -> x0, other arithmetic: 4.53 us -> none  [per_device(): payload = jnp.where(is_weight, weight_row[:, None, :], send_rows.reshape(...]
    concatenate x0 -> x1, other arithmetic: none -> 4.06 us  [per_device(): jnp.concatenate([send_rows.reshape(experts, data_rows, lanes), weight_til...]
    slice x0 -> x1, local copies, waits for them, and re-layouts: none -> 3.78 us  [per_device(): slot_rows = sent_payload[:, :data_rows, :].reshape(slots_all, features)]
    all_to_all x1, starting transfers between devices: 18.4 us -> 14.6 us  [per_device(): lax.all_to_all(slot_grad.reshape(seq_count, capacity), 'seq', split_axis=...]
    unnamed x66 -> x62, local copies, waits for them, and re-layouts: 7.69 us -> 9.88 us
  transfers between devices with their start and end apart: 21 -> 21, of which waited for: 9 -> 9; matrix products, arithmetic and copies ran while one was open for 14% -> 16% of each run, Pallas kernels for 0% -> 0%
where the time goes in v8:
time: 360 us; the launch traced here: 358 us
  waiting for transfers between devices  121 us (34%)
  starting transfers between devices  117 us (32%)
  local copies, waits for them, and re-layouts  49.9 us (14%)
  matrix products  28.5 us (8%)
  other arithmetic  26.2 us (7%)
  between operations  14.8 us (4%)
    ppermute x14, starting transfers between devices, passed_along(): return lax.ppermute(array, axis, pairs)  74.6 us
    ppermute x14, waiting for transfers between devices, passed_along(): return lax.ppermute(array, axis, pairs)  73.3 us
    all_to_all x1, waiting for transfers between devices, per_device(): lax.all_to_all(partial.reshape(head_count, -1, slots_all), 'head', split_...  25.4 us
    all_to_all x1, starting transfers between devices, per_device(): lax.all_to_all(payload, 'seq', split_axis=0, concat_axis=0, tiled=True)  18.2 us
    all_to_all x1, starting transfers between devices, per_device(): lax.all_to_all(slot_grad.reshape(seq_count, capacity), 'seq', split_axis=...  14.6 us
    gather x3, local copies, waits for them, and re-layouts, per_device(): jnp.take(returned.reshape(-1), target.reshape(-1))  13.1 us
    all_gather x1, waiting for transfers between devices, per_device(): input_grad = lax.all_gather(input_slice, 'head', axis=1, tiled=True)  11.7 us
    unnamed x62, local copies, waits for them, and re-layouts  9.88 us
  transfers between devices with their start and end apart: 21, of which 9 were waited for; matrix products, arithmetic and copies ran while one was open for 16% of the time, Pallas kernels for 0%

profile of v8, /device:TPU:49, one launch (start us, length us, event | category | flops | bytes accessed | tf_op | source)
XLA Modules:
  0.0 357.5 jit_solution(784806228137078706)
XLA Ops:
  14.2 5.9 %convolution_convert_fusion = bf16[1536,1024]{1,0:T(8,128)(2,1)} fusion(bf16[128,1024]{1,0:T(8,128)(2,1)} %param.13, s32[1024]{0:T(1024)S(1)} %eq.44, s32[1024]{0:T(1024)S(1)} %add_select_fusion), kind=kOutput, calls=%fused_computation.14 | convolution fusion | flops 808779776 | bytes 3416064 | tf_op jit(solution)/shard_map/dot_general | solution.py:96
  20.1 5.8 %reshape.500 = bf16[128,96,128]{2,1,0:T(8,128)(2,1)} reshape(bf16[1536,1024]{1,0:T(8,128)(2,1)} %convolution_convert_fusion) | data formatting | bytes 6291456 | tf_op jit(solution)/shard_map/reshape | solution.py:103
  25.9 4.1 %fusion.7 = bf16[128,112,128]{2,1,0:T(8,128)(2,1)} fusion(bf16[128,1,12]{2,1,0:T(2,128)(2,1)S(1)} %reshape.529, bf16[128,96,128]{2,1,0:T(8,128)(2,1)} %reshape.500), kind=kLoop, calls=%fused_computation.17 | loop fusion | flops 11010048 | bytes 6818816 | tf_op jit(solution)/shard_map/concatenate | solution.py:102
  29.9 18.2 %all-to-all-start = ((bf16[128,112,128]{2,1,0:T(8,128)(2,1)}), bf16[128,112,128]{2,1,0:T(8,128)(2,1)}, u32[]{:S(2)}, u32[]{:S(2)}) async-start(bf16[128,112,128]{2,1,0:T(8,128)(2,1)} %fusion.7), calls=%async_computation | async-start | bytes 7340032 | tf_op jit(solution)/shard_map/all_to_all | solution.py:113
  48.2 3.4 collective-permute-start
  51.5 3.1 collective-permute-start.1
  54.7 3.2 collective-permute-start.2
  57.9 4.3 %collective-permute-start.3 = (bf16[2,128,1,128]{3,1,2,0:T(8,128)(2,1)S(1)}, bf16[2,128,1,128]{3,1,2,0:T(8,128)(2,1)S(1)}, u32[]{:S(2)}, u32[]{:S(2)}) collective-permute-start(bf16[2,128,1,128]{3,1,2,0:T(8,128)(2,1)S(1)} %pad_maximum_fusion.2), channel_id=1, source_target_pairs={{0,16},{4,20},{8,24},{12,28},{16,32},{20,36},{24,40},{28,44},{32,4... | collective-permute-start | bytes 196616 | tf_op jit(solution)/shard_map/ppermute | solution.py:16
  62.3 2.6 collective-permute-start.4
  65.0 66.2 %collective-permute-done = bf16[2,128,1,128]{3,1,2,0:T(8,128)(2,1)S(1)} collective-permute-done((bf16[2,128,1,128]{3,1,2,0:T(8,128)(2,1)S(1)}, bf16[2,128,1,128]{3,1,2,0:T(8,128)(2,1)S(1)}, u32[]{:S(2)}, u32[]{:S(2)}) %collective-permute-start) | collective-permute-done | bytes 65568 | tf_op jit(solution)/shard_map/ppermute | solution.py:16
  133.2 2.8 collective-permute-done.1
  136.0 26.6 %collective-permute-start.6 = (bf16[2,128,1,128]{3,1,2,0:T(8,128)(2,1)S(1)}, bf16[2,128,1,128]{3,1,2,0:T(8,128)(2,1)S(1)}, u32[]{:S(2)}, u32[]{:S(2)}) collective-permute-start(bf16[2,128,1,128]{3,1,2,0:T(8,128)(2,1)S(1)} %pad_maximum_fusion.2), channel_id=1, source_target_pairs={{0,28},{4,32},{8,36},{12,40},{16,44},{20,48},{24,52},{28,56},{32,6... | collective-permute-start | bytes 196616 | tf_op jit(solution)/shard_map/ppermute | solution.py:16
  164.9 3.8 %slice.80 = bf16[128,96,128]{2,1,0:T(8,128)(2,1)} slice(bf16[128,112,128]{2,1,0:T(8,128)(2,1)} %all-to-all-done), slice={[0:128], [0:96], [0:128]} | slice | bytes 6291456 | tf_op jit(solution)/shard_map/slice | solution.py:115
  168.7 5.9 %reshape.502 = bf16[1536,1024]{1,0:T(8,128)(2,1)} reshape(bf16[128,96,128]{2,1,0:T(8,128)(2,1)} %slice.80) | data formatting | bytes 6291456 | tf_op jit(solution)/shard_map/reshape | solution.py:115
  174.6 5.9 %convolution_convert_fusion.1 = bf16[1536,768]{0,1:T(8,128)(2,1)} fusion(bf16[1536,1024]{1,0:T(8,128)(2,1)} %reshape.502, bf16[1,768,1024]{2,1,0:T(8,128)(2,1)S(1)} %copy-done), kind=kOutput, calls=%fused_computation.18 | convolution fusion | flops 2417098752 | bytes 7077888 | tf_op jit(solution)/shard_map/dot_general | solution.py:119
  180.5 5.3 %all-to-all-start.1 = ((bf16[4,192,1536]{2,1,0:T(8,128)(2,1)}), bf16[4,192,1536]{2,1,0:T(8,128)(2,1)}, u32[]{:S(2)}, u32[]{:S(2)}) async-start(bf16[4,192,1536]{2,1,0:T(8,128)(2,1)} %bitcast.189), calls=%async_computation.1 | async-start | bytes 4718592 | tf_op jit(solution)/shard_map/all_to_all | solution.py:122
  188.6 25.4 %all-to-all-done.1 = bf16[4,192,1536]{2,1,0:T(8,128)(2,1)} async-done(((bf16[4,192,1536]{2,1,0:T(8,128)(2,1)}), bf16[4,192,1536]{2,1,0:T(8,128)(2,1)}, u32[]{:S(2)}, u32[]{:S(2)}) %all-to-all-start.1) | async-done | bytes 2359328 | tf_op jit(solution)/shard_map/all_to_all | solution.py:122
  222.3 2.5 collective-permute-start.8
  225.6 2.5 collective-permute-done.8
  228.9 14.6 %all-to-all-start.2 = ((f32[128,1,12]{2,1,0:T(1,128)}), f32[128,1,12]{2,1,0:T(1,128)}, u32[]{:S(2)}, u32[]{:S(2)}) async-start(f32[128,1,12]{2,1,0:T(1,128)} %bitcast.192), calls=%async_computation.2 | async-start | bytes 131072 | tf_op jit(solution)/shard_map/all_to_all | solution.py:138
  246.1 5.7 %all-to-all-done.2 = f32[128,1,12]{2,1,0:T(1,128)} async-done(((f32[128,1,12]{2,1,0:T(1,128)}), f32[128,1,12]{2,1,0:T(1,128)}, u32[]{:S(2)}, u32[]{:S(2)}) %all-to-all-start.2) | async-done | bytes 6176 | tf_op jit(solution)/shard_map/all_to_all | solution.py:138
  255.5 10.8 %gather_fusion = f32[1024]{0:T(1024)} fusion(f32[1536]{0:T(1024)S(1)} %reshape.504, s32[1024]{0:T(1024)} %broadcast_clamp_fusion), kind=kCustom, calls=%fused_computation | custom fusion | bytes 12288 | tf_op jit(solution)/shard_map/jit(_take)/gather | solution.py:141
  283.9 11.7 %all-gather.5.cloned.1.call-done = bf16[128,4096]{1,0:T(8,128)(2,1)} async-done(((bf16[128,1024]{1,0:T(8,128)(2,1)}), bf16[128,4096]{1,0:T(8,128)(2,1)}) %all-gather.5.cloned.1.call-update) | async-done | bytes 1048592 | tf_op jit(solution)/shard_map/all_gather | solution.py:146
  295.5 5.1 %convolution_convert_fusion.2 = bf16[128,1024]{1,0:T(8,128)(2,1)S(1)} fusion(bf16[128,4096]{1,0:T(8,128)(2,1)} %all-gather.5.cloned.1.call-done, bf16[1024,4096]{0,1:T(8,128)(2,1)} %all-gather.3.cloned.1.call-done), kind=kOutput, calls=%fused_computation.41 | convolution fusion | flops 1073872896 | bytes 9699328 | tf_op jit(solution)/shard_map/dot_general | solution.py:147
  302.0 3.4 convert_bitcast_fusion
  305.5 4.2 %copy.113 = bf16[8,128,1024]{2,0,1:T(8,128)(2,1)} copy(bf16[8,128,1024]{1,2,0:T(8,128)(2,1)} %get-tuple-element.71) | data formatting | bytes 4194304 | tf_op jit(solution)/shard_map/reshape.68
  312.0 2.4 fusion.15
  315.1 9.5 %collective-permute-start.15 = (bf16[2,128,1,128]{3,1,2,0:T(8,128)(2,1)S(1)}, bf16[2,128,1,128]{3,1,2,0:T(8,128)(2,1)S(1)}, u32[]{:S(2)}, u32[]{:S(2)}) collective-permute-start(bf16[2,128,1,128]{3,1,2,0:T(8,128)(2,1)S(1)} %get-tuple-element.76), channel_id=1, source_target_pairs={{28,0},{32,4},{36,8},{40,12},{44,16},{48,20},{52,24},{56,28},{60,3... | collective-permute-start | bytes 196616 | tf_op jit(solution)/shard_map/ppermute | solution.py:16
  324.6 2.5 collective-permute-start.14
  328.3 5.2 %collective-permute-start.13 = (bf16[2,128,1,128]{3,1,0,2:T(8,128)(2,1)}, bf16[2,128,1,128]{3,1,0,2:T(8,128)(2,1)S(1)}, u32[]{:S(2)}, u32[]{:S(2)}) collective-permute-start(bf16[2,128,1,128]{3,1,0,2:T(8,128)(2,1)} %get-tuple-element.78), channel_id=1, source_target_pairs={{20,0},{24,4},{28,8},{32,12},{36,16},{40,20},{44,24},{48,28},{52,3... | collective-permute-start | bytes 196616 | tf_op jit(solution)/shard_map/ppermute | solution.py:16
  333.4 3.6 %collective-permute-start.12 = (bf16[2,128,1,128]{3,1,0,2:T(8,128)(2,1)}, bf16[2,128,1,128]{3,1,0,2:T(8,128)(2,1)S(1)}, u32[]{:S(2)}, u32[]{:S(2)}) collective-permute-start(bf16[2,128,1,128]{3,1,0,2:T(8,128)(2,1)} %get-tuple-element.79), channel_id=1, source_target_pairs={{16,0},{20,4},{24,8},{28,12},{32,16},{36,20},{40,24},{44,28},{48,3... | collective-permute-start | bytes 196616 | tf_op jit(solution)/shard_map/ppermute | solution.py:16
  337.1 4.4 %collective-permute-start.11 = (bf16[2,128,1,128]{3,1,0,2:T(8,128)(2,1)S(1)}, bf16[2,128,1,128]{3,1,0,2:T(8,128)(2,1)S(1)}, u32[]{:S(2)}, u32[]{:S(2)}) collective-permute-start(bf16[2,128,1,128]{3,1,0,2:T(8,128)(2,1)S(1)} %get-tuple-element.80), channel_id=1, source_target_pairs={{12,0},{16,4},{20,8},{24,12},{28,16},{32,20},{36,24},{40,28},{44,3... | collective-permute-start | bytes 196616 | tf_op jit(solution)/shard_map/ppermute | solution.py:16
  (144 shorter events, 62.1 us)
Async XLA Ops:
  7.2 167.5 %copy-start = (bf16[1,768,1024]{2,1,0:T(8,128)(2,1)S(1)}, bf16[1,768,1024]{2,1,0:T(8,128)(2,1)}, u32[]{:S(2)}) copy-start(bf16[1,768,1024]{2,1,0:T(8,128)(2,1)} %param.18) | copy-start | bytes 4718596
  7.2 210.7 %all-gather.3.cloned.1.call-start = ((), (), s32[]{:S(2)}) async-start(), calls=%async_computation.3 | async-start | bytes 8454144 | tf_op jit(solution)/shard_map/all_gather | solution.py:105
  29.9 18.2 %copy-start.20 = (bf16[128,1,128]{2,0,1:T(8,128)(2,1)S(1)}, bf16[128,1,128]{2,0,1:T(8,128)(2,1)}, u32[]{:S(2)}) copy-start(bf16[128,1,128]{2,0,1:T(8,128)(2,1)} %param.23) | copy-start | bytes 98308
  29.9 18.2 %copy-start.21 = (bf16[128,1,128]{2,0,1:T(8,128)(2,1)S(1)}, bf16[128,1,128]{2,0,1:T(8,128)(2,1)}, u32[]{:S(2)}) copy-start(bf16[128,1,128]{2,0,1:T(8,128)(2,1)} %param.22) | copy-start | bytes 98308
  29.9 135.0 %all-to-all-start = ((bf16[128,112,128]{2,1,0:T(8,128)(2,1)}), bf16[128,112,128]{2,1,0:T(8,128)(2,1)}, u32[]{:S(2)}, u32[]{:S(2)}) async-start(bf16[128,112,128]{2,1,0:T(8,128)(2,1)} %fusion.7), calls=%async_computation | async-start | bytes 7340032 | tf_op jit(solution)/shard_map/all_to_all | solution.py:113
  48.2 83.1 %collective-permute-start = (bf16[2,128,1,128]{3,1,2,0:T(8,128)(2,1)S(1)}, bf16[2,128,1,128]{3,1,2,0:T(8,128)(2,1)S(1)}, u32[]{:S(2)}, u32[]{:S(2)}) collective-permute-start(bf16[2,128,1,128]{3,1,2,0:T(8,128)(2,1)S(1)} %pad_maximum_fusion.2), channel_id=1, source_target_pairs={{0,4},{4,8},{8,12},{12,16},{16,20},{20,24},{24,28},{28,32},{32,36}... | collective-permute-start | bytes 196616 | tf_op jit(solution)/shard_map/ppermute | solution.py:16
  51.5 84.4 %collective-permute-start.1 = (bf16[2,128,1,128]{3,1,2,0:T(8,128)(2,1)S(1)}, bf16[2,128,1,128]{3,1,2,0:T(8,128)(2,1)S(1)}, u32[]{:S(2)}, u32[]{:S(2)}) collective-permute-start(bf16[2,128,1,128]{3,1,2,0:T(8,128)(2,1)S(1)} %pad_maximum_fusion.2), channel_id=1, source_target_pairs={{0,8},{4,12},{8,16},{12,20},{16,24},{20,28},{24,32},{28,36},{32,40... | collective-permute-start | bytes 196616 | tf_op jit(solution)/shard_map/ppermute | solution.py:16
  54.7 107.9 %collective-permute-start.2 = (bf16[2,128,1,128]{3,1,2,0:T(8,128)(2,1)S(1)}, bf16[2,128,1,128]{3,1,2,0:T(8,128)(2,1)S(1)}, u32[]{:S(2)}, u32[]{:S(2)}) collective-permute-start(bf16[2,128,1,128]{3,1,2,0:T(8,128)(2,1)S(1)} %pad_maximum_fusion.2), channel_id=1, source_target_pairs={{0,12},{4,16},{8,20},{12,24},{16,28},{20,32},{24,36},{28,40},{32,4... | collective-permute-start | bytes 196616 | tf_op jit(solution)/shard_map/ppermute | solution.py:16
  57.9 104.7 %collective-permute-start.3 = (bf16[2,128,1,128]{3,1,2,0:T(8,128)(2,1)S(1)}, bf16[2,128,1,128]{3,1,2,0:T(8,128)(2,1)S(1)}, u32[]{:S(2)}, u32[]{:S(2)}) collective-permute-start(bf16[2,128,1,128]{3,1,2,0:T(8,128)(2,1)S(1)} %pad_maximum_fusion.2), channel_id=1, source_target_pairs={{0,16},{4,20},{8,24},{12,28},{16,32},{20,36},{24,40},{28,44},{32,4... | collective-permute-start | bytes 196616 | tf_op jit(solution)/shard_map/ppermute | solution.py:16
  62.3 100.4 %collective-permute-start.4 = (bf16[2,128,1,128]{3,1,2,0:T(8,128)(2,1)S(1)}, bf16[2,128,1,128]{3,1,2,0:T(8,128)(2,1)S(1)}, u32[]{:S(2)}, u32[]{:S(2)}) collective-permute-start(bf16[2,128,1,128]{3,1,2,0:T(8,128)(2,1)S(1)} %pad_maximum_fusion.2), channel_id=1, source_target_pairs={{0,20},{4,24},{8,28},{12,32},{16,36},{20,40},{24,44},{28,48},{32,5... | collective-permute-start | bytes 196616 | tf_op jit(solution)/shard_map/ppermute | solution.py:16
  131.3 37.5 %copy-start.14 = (bf16[2,128,1,128]{3,1,2,0:T(8,128)(2,1)}, bf16[2,128,1,128]{3,1,2,0:T(8,128)(2,1)S(1)}, u32[]{:S(2)}) copy-start(bf16[2,128,1,128]{3,1,2,0:T(8,128)(2,1)S(1)} %collective-permute-done) | copy-start | bytes 196612
  131.3 31.4 %collective-permute-start.5 = (bf16[2,128,1,128]{3,1,2,0:T(8,128)(2,1)S(1)}, bf16[2,128,1,128]{3,1,2,0:T(8,128)(2,1)S(1)}, u32[]{:S(2)}, u32[]{:S(2)}) collective-permute-start(bf16[2,128,1,128]{3,1,2,0:T(8,128)(2,1)S(1)} %pad_maximum_fusion.2), channel_id=1, source_target_pairs={{0,24},{4,28},{8,32},{12,36},{16,40},{20,44},{24,48},{28,52},{32,5... | collective-permute-start | bytes 196616 | tf_op jit(solution)/shard_map/ppermute | solution.py:16
  136.0 32.7 %copy-start.15 = (bf16[2,128,1,128]{3,1,2,0:T(8,128)(2,1)}, bf16[2,128,1,128]{3,1,2,0:T(8,128)(2,1)S(1)}, u32[]{:S(2)}) copy-start(bf16[2,128,1,128]{3,1,2,0:T(8,128)(2,1)S(1)} %collective-permute-done.1) | copy-start | bytes 196612
  136.0 29.0 %collective-permute-start.6 = (bf16[2,128,1,128]{3,1,2,0:T(8,128)(2,1)S(1)}, bf16[2,128,1,128]{3,1,2,0:T(8,128)(2,1)S(1)}, u32[]{:S(2)}, u32[]{:S(2)}) collective-permute-start(bf16[2,128,1,128]{3,1,2,0:T(8,128)(2,1)S(1)} %pad_maximum_fusion.2), channel_id=1, source_target_pairs={{0,28},{4,32},{8,36},{12,40},{16,44},{20,48},{24,52},{28,56},{32,6... | collective-permute-start | bytes 196616 | tf_op jit(solution)/shard_map/ppermute | solution.py:16
  180.5 33.5 %all-to-all-start.1 = ((bf16[4,192,1536]{2,1,0:T(8,128)(2,1)}), bf16[4,192,1536]{2,1,0:T(8,128)(2,1)}, u32[]{:S(2)}, u32[]{:S(2)}) async-start(bf16[4,192,1536]{2,1,0:T(8,128)(2,1)} %bitcast.189), calls=%async_computation.1 | async-start | bytes 4718592 | tf_op jit(solution)/shard_map/all_to_all | solution.py:122
  217.8 50.8 %copy-start.11 = (f32[128,8]{0,1:T(8,128)S(1)}, f32[128,8]{0,1:T(8,128)}, u32[]{:S(2)}) copy-start(f32[128,8]{0,1:T(8,128)} %param.15) | copy-start | bytes 12292
  217.8 4.4 %collective-permute-start.7 = (f32[1536]{0:T(1024)S(1)}, f32[1536]{0:T(1024)S(1)}, u32[]{:S(2)}, u32[]{:S(2)}) collective-permute-start(f32[1536]{0:T(1024)S(1)} %fusion.23), channel_id=1, source_target_pairs={{0,1},{1,0},{2,3},{3,2},{4,5},{5,4},{6,7},{7,6},{8,9},{9,8},{10,11... | collective-permute-start | bytes 18440 | tf_op jit(solution)/shard_map/ppermute | solution.py:24
  222.3 5.9 %collective-permute-start.8 = (f32[1536]{0:T(1024)S(1)}, f32[1536]{0:T(1024)S(1)}, u32[]{:S(2)}, u32[]{:S(2)}) collective-permute-start(f32[1536]{0:T(1024)S(1)} %add.151), channel_id=1, source_target_pairs={{0,2},{1,3},{2,0},{3,1},{4,6},{5,7},{6,4},{7,5},{8,10},{9,11},{10,... | collective-permute-start | bytes 18440 | tf_op jit(solution)/shard_map/ppermute | solution.py:24
  228.9 22.8 %all-to-all-start.2 = ((f32[128,1,12]{2,1,0:T(1,128)}), f32[128,1,12]{2,1,0:T(1,128)}, u32[]{:S(2)}, u32[]{:S(2)}) async-start(f32[128,1,12]{2,1,0:T(1,128)} %bitcast.192), calls=%async_computation.2 | async-start | bytes 131072 | tf_op jit(solution)/shard_map/all_to_all | solution.py:138
  243.5 52.0 %all-gather.5.cloned.1.call-start = ((), (), s32[]{:S(2)}) async-start(), calls=%async_computation.4 | async-start | bytes 1310720 | tf_op jit(solution)/shard_map/all_gather | solution.py:146
  255.5 16.7 %copy-start.10 = (bf16[128,1024]{1,0:T(8,128)(2,1)S(1)}, bf16[128,1024]{1,0:T(8,128)(2,1)}, u32[]{:S(2)}) copy-start(bf16[128,1024]{1,0:T(8,128)(2,1)} %param.13) | copy-start | bytes 786436
  255.5 22.3 %copy-start.6 = (bf16[128,8,128]{2,1,0:T(8,128)(2,1)S(1)}, bf16[128,8,128]{2,1,0:T(8,128)(2,1)}, u32[]{:S(2)}) copy-start(bf16[128,8,128]{2,1,0:T(8,128)(2,1)} %param.21) | copy-start | bytes 786436
  283.9 16.8 %copy-start.8 = (bf16[2,1024,1,128]{3,1,2,0:T(8,128)(2,1)S(1)}, bf16[2,1024,1,128]{3,1,2,0:T(8,128)(2,1)}, u32[]{:S(2)}) copy-start(bf16[2,1024,1,128]{3,1,2,0:T(8,128)(2,1)} %constant_dynamic-update-slice_fusion) | copy-start | bytes 1572868
  314.3 31.4 %copy-start.3 = (bf16[8,128,1024]{1,2,0:T(8,128)(2,1)S(1)}, bf16[8,128,1024]{1,2,0:T(8,128)(2,1)}, u32[]{:S(2)}) copy-start(bf16[8,128,1024]{1,2,0:T(8,128)(2,1)} %get-tuple-element.72) | copy-start | bytes 6291460
  314.3 31.4 %copy-start.9 = (bf16[2,1024,1,128]{3,1,2,0:T(8,128)(2,1)S(1)}, bf16[2,1024,1,128]{3,1,2,0:T(8,128)(2,1)}, u32[]{:S(2)}) copy-start(bf16[2,1024,1,128]{3,1,2,0:T(8,128)(2,1)} %constant_dynamic-update-slice_fusion) | copy-start | bytes 1572868
  315.1 26.4 %collective-permute-start.15 = (bf16[2,128,1,128]{3,1,2,0:T(8,128)(2,1)S(1)}, bf16[2,128,1,128]{3,1,2,0:T(8,128)(2,1)S(1)}, u32[]{:S(2)}, u32[]{:S(2)}) collective-permute-start(bf16[2,128,1,128]{3,1,2,0:T(8,128)(2,1)S(1)} %get-tuple-element.76), channel_id=1, source_target_pairs={{28,0},{32,4},{36,8},{40,12},{44,16},{48,20},{52,24},{56,28},{60,3... | collective-permute-start | bytes 196616 | tf_op jit(solution)/shard_map/ppermute | solution.py:16
  324.6 18.9 %collective-permute-start.14 = (bf16[2,128,1,128]{3,1,0,2:T(8,128)(2,1)S(1)}, bf16[2,128,1,128]{3,1,0,2:T(8,128)(2,1)S(1)}, u32[]{:S(2)}, u32[]{:S(2)}) collective-permute-start(bf16[2,128,1,128]{3,1,0,2:T(8,128)(2,1)S(1)} %get-tuple-element.77), channel_id=1, source_target_pairs={{24,0},{28,4},{32,8},{36,12},{40,16},{44,20},{48,24},{52,28},{56,3... | collective-permute-start | bytes 196616 | tf_op jit(solution)/shard_map/ppermute | solution.py:16
  328.3 18.9 %collective-permute-start.13 = (bf16[2,128,1,128]{3,1,0,2:T(8,128)(2,1)}, bf16[2,128,1,128]{3,1,0,2:T(8,128)(2,1)S(1)}, u32[]{:S(2)}, u32[]{:S(2)}) collective-permute-start(bf16[2,128,1,128]{3,1,0,2:T(8,128)(2,1)} %get-tuple-element.78), channel_id=1, source_target_pairs={{20,0},{24,4},{28,8},{32,12},{36,16},{40,20},{44,24},{48,28},{52,3... | collective-permute-start | bytes 196616 | tf_op jit(solution)/shard_map/ppermute | solution.py:16
  333.4 13.7 %collective-permute-start.12 = (bf16[2,128,1,128]{3,1,0,2:T(8,128)(2,1)}, bf16[2,128,1,128]{3,1,0,2:T(8,128)(2,1)S(1)}, u32[]{:S(2)}, u32[]{:S(2)}) collective-permute-start(bf16[2,128,1,128]{3,1,0,2:T(8,128)(2,1)} %get-tuple-element.79), channel_id=1, source_target_pairs={{16,0},{20,4},{24,8},{28,12},{32,16},{36,20},{40,24},{44,28},{48,3... | collective-permute-start | bytes 196616 | tf_op jit(solution)/shard_map/ppermute | solution.py:16
  337.1 10.1 %collective-permute-start.11 = (bf16[2,128,1,128]{3,1,0,2:T(8,128)(2,1)S(1)}, bf16[2,128,1,128]{3,1,0,2:T(8,128)(2,1)S(1)}, u32[]{:S(2)}, u32[]{:S(2)}) collective-permute-start(bf16[2,128,1,128]{3,1,0,2:T(8,128)(2,1)S(1)} %get-tuple-element.80), channel_id=1, source_target_pairs={{12,0},{16,4},{20,8},{24,12},{28,16},{32,20},{36,24},{40,28},{44,3... | collective-permute-start | bytes 196616 | tf_op jit(solution)/shard_map/ppermute | solution.py:16
  341.5 5.7 %collective-permute-start.10 = (bf16[2,128,1,128]{3,1,0,2:T(8,128)(2,1)S(1)}, bf16[2,128,1,128]{3,1,0,2:T(8,128)(2,1)S(1)}, u32[]{:S(2)}, u32[]{:S(2)}) collective-permute-start(bf16[2,128,1,128]{3,1,0,2:T(8,128)(2,1)S(1)} %get-tuple-element.81), channel_id=1, source_target_pairs={{8,0},{12,4},{16,8},{20,12},{24,16},{28,20},{32,24},{36,28},{40,32... | collective-permute-start | bytes 196616 | tf_op jit(solution)/shard_map/ppermute | solution.py:16
  343.5 5.6 %collective-permute-start.9 = (bf16[2,128,1,128]{3,1,0,2:T(8,128)(2,1)S(1)}, bf16[2,128,1,128]{3,1,0,2:T(8,128)(2,1)S(1)}, u32[]{:S(2)}, u32[]{:S(2)}) collective-permute-start(bf16[2,128,1,128]{3,1,0,2:T(8,128)(2,1)S(1)} %get-tuple-element.75), channel_id=1, source_target_pairs={{4,0},{8,4},{12,8},{16,12},{20,16},{24,20},{28,24},{32,28},{36,32}... | collective-permute-start | bytes 196616 | tf_op jit(solution)/shard_map/ppermute | solution.py:16
  (15 other events, 80.5 us)
Sparse Core Ops, SparseCore 0:
  11.1 172.5 all-gather.2
  274.3 21.1 all-gather.4

commit v9 on v5

--- a/solution.py
+++ b/solution.py
@@ -132,7 +132,6 @@
     gate_up_grad = jnp.stack([scaled * up * sig * (1.0 + gate * (1.0 - sig)), scaled * act])[
         None
     ].astype(jnp.bfloat16)
-    slot_part, weight_full = lax.optimization_barrier((slot_part, weight_full))
     slot_grad = head_sum(slot_part)
     returned = lax.all_to_all(
         slot_grad.reshape(seq_count, capacity), "seq", split_axis=0, concat_axis=0, tiled=True
@@ -142,6 +141,7 @@
     dense = jnp.einsum("tk,tke->te", logit_grad, hits, precision=highest)
     router_term = jnp.dot(dense, router.astype(jnp.float32), precision=highest)
     input_slice = (out_grad.astype(jnp.float32) + router_term).astype(jnp.bfloat16)
+    input_slice, weight_full = lax.optimization_barrier((input_slice, weight_full))
     input_grad = lax.all_gather(input_slice, "head", axis=1, tiled=True)
     attn_grad = lax.dot_general(
         input_grad,

time: 352 us -> 352 us (level)
  transfers between devices with their start and end apart: 21 -> 21, of which waited for: 9 -> 9; matrix products, arithmetic and copies ran while one was open for 14% -> 18% of each run, Pallas kernels for 0% -> 0%
where the time goes in v9:
time: 352 us; the launch traced here: 350 us
  waiting for transfers between devices  132 us (38%)
  starting transfers between devices  118 us (34%)
  local copies, waits for them, and re-layouts  30.9 us (9%)
  matrix products  28.9 us (8%)
  other arithmetic  25.5 us (7%)
  between operations  14.8 us (4%)
    ppermute x14, waiting for transfers between devices, passed_along(): return lax.ppermute(array, axis, pairs)  84.3 us
    ppermute x14, starting transfers between devices, passed_along(): return lax.ppermute(array, axis, pairs)  71.5 us
    all_to_all x1, waiting for transfers between devices, per_device(): lax.all_to_all(partial.reshape(head_count, -1, slots_all), 'head', split_...  24.3 us
    all_to_all x1, starting transfers between devices, per_device(): lax.all_to_all(slot_grad.reshape(seq_count, capacity), 'seq', split_axis=...  18.4 us
    all_to_all x1, starting transfers between devices, per_device(): lax.all_to_all(payload, 'seq', split_axis=0, concat_axis=0, tiled=True)  18.2 us
    all_gather x1, waiting for transfers between devices, per_device(): input_grad = lax.all_gather(input_slice, 'head', axis=1, tiled=True)  13.1 us
    unnamed x66, local copies, waits for them, and re-layouts  7.69 us
    dot_general x1, matrix products, per_device(): send_rows = jnp.dot(pick, out_grad, preferred_element_type=jnp.float32)  7.08 us
  transfers between devices with their start and end apart: 21, of which 9 were waited for; matrix products, arithmetic and copies ran while one was open for 18% of the time, Pallas kernels for 0%

profile of v9, /device:TPU:49, one launch (start us, length us, event | category | flops | bytes accessed | tf_op | source)
XLA Modules:
  0.0 350.2 jit_solution(14613899760400449053)
XLA Ops:
  13.8 7.1 %fusion.13 = bf16[2048,1024]{1,0:T(8,128)(2,1)} fusion(bf16[128,1024]{1,0:T(8,128)(2,1)} %param.11, s32[1024]{0:T(1024)S(1)} %eq.52, s32[1024]{0:T(1024)S(1)} %add_select_fusion), kind=kOutput, calls=%fused_computation.33 | convolution fusion | flops 1076232192 | bytes 4464640 | tf_op jit(solution)/shard_map/dot_general | solution.py:97
  20.9 4.5 %select_convert_fusion = bf16[128,16,1024]{2,1,0:T(8,128)(2,1)} fusion(bf16[128,16,1024]{2,1,0:T(8,128)(2,1)} %bitcast.191, bf16[128,1024]{1,0:T(8,128)(2,1)S(1)} %pad.4, pred[16]{0:T(512)(128)(4,1)S(1)} %iota_compare_fusion.13), kind=kLoop, calls=%fused_computation.1 | loop fusion | flops 2097152 | bytes 8650768 | tf_op jit(solution)/shard_map/convert_element_type | solution.py:103
  25.5 18.2 %all-to-all-start = ((bf16[128,16,1024]{2,1,0:T(8,128)(2,1)}), bf16[128,16,1024]{2,1,0:T(8,128)(2,1)}, u32[]{:S(2)}, u32[]{:S(2)}) async-start(bf16[128,16,1024]{2,1,0:T(8,128)(2,1)} %select_convert_fusion), calls=%async_computation | async-start | bytes 8388608 | tf_op jit(solution)/shard_map/all_to_all | solution.py:112
  43.8 3.4 collective-permute-start
  47.1 3.1 collective-permute-start.1
  50.2 3.2 collective-permute-start.2
  53.5 4.3 %collective-permute-start.3 = (bf16[2,128,1,128]{3,1,2,0:T(8,128)(2,1)S(1)}, bf16[2,128,1,128]{3,1,2,0:T(8,128)(2,1)S(1)}, u32[]{:S(2)}, u32[]{:S(2)}) collective-permute-start(bf16[2,128,1,128]{3,1,2,0:T(8,128)(2,1)S(1)} %pad_maximum_fusion.2), channel_id=1, source_target_pairs={{0,16},{4,20},{8,24},{12,28},{16,32},{20,36},{24,40},{28,44},{32,4... | collective-permute-start | bytes 196616 | tf_op jit(solution)/shard_map/ppermute | solution.py:16
  57.8 2.6 collective-permute-start.4
  60.5 78.4 %collective-permute-done = bf16[2,128,1,128]{3,1,2,0:T(8,128)(2,1)S(1)} collective-permute-done((bf16[2,128,1,128]{3,1,2,0:T(8,128)(2,1)S(1)}, bf16[2,128,1,128]{3,1,2,0:T(8,128)(2,1)S(1)}, u32[]{:S(2)}, u32[]{:S(2)}) %collective-permute-start) | collective-permute-done | bytes 65568 | tf_op jit(solution)/shard_map/ppermute | solution.py:16
  140.8 2.7 collective-permute-done.1
  143.5 23.5 %collective-permute-start.6 = (bf16[2,128,1,128]{3,1,2,0:T(8,128)(2,1)S(1)}, bf16[2,128,1,128]{3,1,2,0:T(8,128)(2,1)S(1)}, u32[]{:S(2)}, u32[]{:S(2)}) collective-permute-start(bf16[2,128,1,128]{3,1,2,0:T(8,128)(2,1)S(1)} %pad_maximum_fusion.2), channel_id=1, source_target_pairs={{0,28},{4,32},{8,36},{12,40},{16,44},{20,48},{24,52},{28,56},{32,6... | collective-permute-start | bytes 196616 | tf_op jit(solution)/shard_map/ppermute | solution.py:16
  168.3 6.2 %reshape.468 = bf16[1536,1024]{1,0:T(8,128)(2,1)} reshape(bf16[128,12,1024]{2,1,0:T(8,128)(2,1)} %bitcast.186) | data formatting | bytes 6291456 | tf_op jit(solution)/shard_map/reshape | solution.py:114
  174.6 5.9 %convolution_convert_fusion = bf16[1536,768]{0,1:T(8,128)(2,1)} fusion(bf16[1536,1024]{1,0:T(8,128)(2,1)} %reshape.468, bf16[1,768,1024]{2,1,0:T(8,128)(2,1)S(1)} %copy-done), kind=kOutput, calls=%fused_computation.16 | convolution fusion | flops 2417098752 | bytes 7077888 | tf_op jit(solution)/shard_map/dot_general | solution.py:118
  180.5 4.9 %all-to-all-start.1 = ((bf16[4,192,1536]{2,1,0:T(8,128)(2,1)}), bf16[4,192,1536]{2,1,0:T(8,128)(2,1)}, u32[]{:S(2)}, u32[]{:S(2)}) async-start(bf16[4,192,1536]{2,1,0:T(8,128)(2,1)} %bitcast.192), calls=%async_computation.1 | async-start | bytes 4718592 | tf_op jit(solution)/shard_map/all_to_all | solution.py:121
  188.3 24.3 %all-to-all-done.1 = bf16[4,192,1536]{2,1,0:T(8,128)(2,1)} async-done(((bf16[4,192,1536]{2,1,0:T(8,128)(2,1)}), bf16[4,192,1536]{2,1,0:T(8,128)(2,1)}, u32[]{:S(2)}, u32[]{:S(2)}) %all-to-all-start.1) | async-done | bytes 2359328 | tf_op jit(solution)/shard_map/all_to_all | solution.py:121
  220.8 2.5 collective-permute-start.8
  224.2 2.5 collective-permute-done.8
  227.5 18.4 %all-to-all-start.2 = ((f32[128,1,12]{2,1,0:T(1,128)}), f32[128,1,12]{2,1,0:T(1,128)}, u32[]{:S(2)}, u32[]{:S(2)}) async-start(f32[128,1,12]{2,1,0:T(1,128)} %bitcast.195), calls=%async_computation.2 | async-start | bytes 131072 | tf_op jit(solution)/shard_map/all_to_all | solution.py:136
  247.8 6.1 %all-to-all-done.2 = f32[128,1,12]{2,1,0:T(1,128)} async-done(((f32[128,1,12]{2,1,0:T(1,128)}), f32[128,1,12]{2,1,0:T(1,128)}, u32[]{:S(2)}, u32[]{:S(2)}) %all-to-all-start.2) | async-done | bytes 6176 | tf_op jit(solution)/shard_map/all_to_all | solution.py:136
  254.4 2.3 reduce.10
  257.7 6.4 %gather_fusion = f32[1024]{0:T(1024)S(1)} fusion(f32[1536]{0:T(1024)S(1)} %reshape.470, s32[1024]{0:T(1024)} %broadcast_clamp_fusion), kind=kCustom, calls=%fused_computation | custom fusion | bytes 12288 | tf_op jit(solution)/shard_map/jit(_take)/gather | solution.py:139
  275.1 13.1 %all-gather.5.cloned.1.call-done = bf16[128,4096]{1,0:T(8,128)(2,1)} async-done(((bf16[128,1024]{1,0:T(8,128)(2,1)}), bf16[128,4096]{1,0:T(8,128)(2,1)}) %all-gather.5.cloned.1.call-update) | async-done | bytes 1048592 | tf_op jit(solution)/shard_map/all_gather | solution.py:145
  288.2 5.1 %convolution_convert_fusion.1 = bf16[128,1024]{1,0:T(8,128)(2,1)S(1)} fusion(bf16[128,4096]{1,0:T(8,128)(2,1)} %all-gather.5.cloned.1.call-done, bf16[1024,4096]{0,1:T(8,128)(2,1)} %all-gather.3.cloned.1.call-done), kind=kOutput, calls=%fused_computation.39 | convolution fusion | flops 1073872896 | bytes 9699328 | tf_op jit(solution)/shard_map/dot_general | solution.py:146
  294.7 3.4 convert_bitcast_fusion
  298.1 4.2 %copy.99 = bf16[8,128,1024]{2,0,1:T(8,128)(2,1)} copy(bf16[8,128,1024]{1,2,0:T(8,128)(2,1)} %get-tuple-element.54) | data formatting | bytes 4194304 | tf_op jit(solution)/shard_map/reshape.35
  304.6 2.4 fusion.14
  307.8 9.5 %collective-permute-start.15 = (bf16[2,128,1,128]{3,1,2,0:T(8,128)(2,1)S(1)}, bf16[2,128,1,128]{3,1,2,0:T(8,128)(2,1)S(1)}, u32[]{:S(2)}, u32[]{:S(2)}) collective-permute-start(bf16[2,128,1,128]{3,1,2,0:T(8,128)(2,1)S(1)} %get-tuple-element.59), channel_id=1, source_target_pairs={{28,0},{32,4},{36,8},{40,12},{44,16},{48,20},{52,24},{56,28},{60,3... | collective-permute-start | bytes 196616 | tf_op jit(solution)/shard_map/ppermute | solution.py:16
  317.3 2.5 collective-permute-start.14
  321.0 5.2 %collective-permute-start.13 = (bf16[2,128,1,128]{3,1,0,2:T(8,128)(2,1)}, bf16[2,128,1,128]{3,1,0,2:T(8,128)(2,1)S(1)}, u32[]{:S(2)}, u32[]{:S(2)}) collective-permute-start(bf16[2,128,1,128]{3,1,0,2:T(8,128)(2,1)} %get-tuple-element.61), channel_id=1, source_target_pairs={{20,0},{24,4},{28,8},{32,12},{36,16},{40,20},{44,24},{48,28},{52,3... | collective-permute-start | bytes 196616 | tf_op jit(solution)/shard_map/ppermute | solution.py:16
  326.1 3.6 %collective-permute-start.12 = (bf16[2,128,1,128]{3,1,0,2:T(8,128)(2,1)}, bf16[2,128,1,128]{3,1,0,2:T(8,128)(2,1)S(1)}, u32[]{:S(2)}, u32[]{:S(2)}) collective-permute-start(bf16[2,128,1,128]{3,1,0,2:T(8,128)(2,1)} %get-tuple-element.62), channel_id=1, source_target_pairs={{16,0},{20,4},{24,8},{28,12},{32,16},{36,20},{40,24},{44,28},{48,3... | collective-permute-start | bytes 196616 | tf_op jit(solution)/shard_map/ppermute | solution.py:16
  329.8 4.4 %collective-permute-start.11 = (bf16[2,128,1,128]{3,1,0,2:T(8,128)(2,1)S(1)}, bf16[2,128,1,128]{3,1,0,2:T(8,128)(2,1)S(1)}, u32[]{:S(2)}, u32[]{:S(2)}) collective-permute-start(bf16[2,128,1,128]{3,1,0,2:T(8,128)(2,1)S(1)} %get-tuple-element.63), channel_id=1, source_target_pairs={{12,0},{16,4},{20,8},{24,12},{28,16},{32,20},{36,24},{40,28},{44,3... | collective-permute-start | bytes 196616 | tf_op jit(solution)/shard_map/ppermute | solution.py:16
  336.2 2.2 collective-permute-start.9
  (149 shorter events, 49.2 us)
Async XLA Ops:
  7.2 167.4 %copy-start = (bf16[1,768,1024]{2,1,0:T(8,128)(2,1)S(1)}, bf16[1,768,1024]{2,1,0:T(8,128)(2,1)}, u32[]{:S(2)}) copy-start(bf16[1,768,1024]{2,1,0:T(8,128)(2,1)} %param.16) | copy-start | bytes 4718596
  7.2 259.9 %all-gather.3.cloned.1.call-start = ((), (), s32[]{:S(2)}) async-start(), calls=%async_computation.3 | async-start | bytes 8454144 | tf_op jit(solution)/shard_map/all_gather | solution.py:104
  25.5 18.3 %copy-start.20 = (bf16[128,1,128]{2,0,1:T(8,128)(2,1)S(1)}, bf16[128,1,128]{2,0,1:T(8,128)(2,1)}, u32[]{:S(2)}) copy-start(bf16[128,1,128]{2,0,1:T(8,128)(2,1)} %param.21) | copy-start | bytes 98308
  25.5 18.3 %copy-start.21 = (bf16[128,1,128]{2,0,1:T(8,128)(2,1)S(1)}, bf16[128,1,128]{2,0,1:T(8,128)(2,1)}, u32[]{:S(2)}) copy-start(bf16[128,1,128]{2,0,1:T(8,128)(2,1)} %param.20) | copy-start | bytes 98308
  25.5 142.8 %all-to-all-start = ((bf16[128,16,1024]{2,1,0:T(8,128)(2,1)}), bf16[128,16,1024]{2,1,0:T(8,128)(2,1)}, u32[]{:S(2)}, u32[]{:S(2)}) async-start(bf16[128,16,1024]{2,1,0:T(8,128)(2,1)} %select_convert_fusion), calls=%async_computation | async-start | bytes 8388608 | tf_op jit(solution)/shard_map/all_to_all | solution.py:112
  43.8 95.1 %collective-permute-start = (bf16[2,128,1,128]{3,1,2,0:T(8,128)(2,1)S(1)}, bf16[2,128,1,128]{3,1,2,0:T(8,128)(2,1)S(1)}, u32[]{:S(2)}, u32[]{:S(2)}) collective-permute-start(bf16[2,128,1,128]{3,1,2,0:T(8,128)(2,1)S(1)} %pad_maximum_fusion.2), channel_id=1, source_target_pairs={{0,4},{4,8},{8,12},{12,16},{16,20},{20,24},{24,28},{28,32},{32,36}... | collective-permute-start | bytes 196616 | tf_op jit(solution)/shard_map/ppermute | solution.py:16
  47.1 96.4 %collective-permute-start.1 = (bf16[2,128,1,128]{3,1,2,0:T(8,128)(2,1)S(1)}, bf16[2,128,1,128]{3,1,2,0:T(8,128)(2,1)S(1)}, u32[]{:S(2)}, u32[]{:S(2)}) collective-permute-start(bf16[2,128,1,128]{3,1,2,0:T(8,128)(2,1)S(1)} %pad_maximum_fusion.2), channel_id=1, source_target_pairs={{0,8},{4,12},{8,16},{12,20},{16,24},{20,28},{24,32},{28,36},{32,40... | collective-permute-start | bytes 196616 | tf_op jit(solution)/shard_map/ppermute | solution.py:16
  50.2 116.8 %collective-permute-start.2 = (bf16[2,128,1,128]{3,1,2,0:T(8,128)(2,1)S(1)}, bf16[2,128,1,128]{3,1,2,0:T(8,128)(2,1)S(1)}, u32[]{:S(2)}, u32[]{:S(2)}) collective-permute-start(bf16[2,128,1,128]{3,1,2,0:T(8,128)(2,1)S(1)} %pad_maximum_fusion.2), channel_id=1, source_target_pairs={{0,12},{4,16},{8,20},{12,24},{16,28},{20,32},{24,36},{28,40},{32,4... | collective-permute-start | bytes 196616 | tf_op jit(solution)/shard_map/ppermute | solution.py:16
  53.5 113.5 %collective-permute-start.3 = (bf16[2,128,1,128]{3,1,2,0:T(8,128)(2,1)S(1)}, bf16[2,128,1,128]{3,1,2,0:T(8,128)(2,1)S(1)}, u32[]{:S(2)}, u32[]{:S(2)}) collective-permute-start(bf16[2,128,1,128]{3,1,2,0:T(8,128)(2,1)S(1)} %pad_maximum_fusion.2), channel_id=1, source_target_pairs={{0,16},{4,20},{8,24},{12,28},{16,32},{20,36},{24,40},{28,44},{32,4... | collective-permute-start | bytes 196616 | tf_op jit(solution)/shard_map/ppermute | solution.py:16
  57.8 109.2 %collective-permute-start.4 = (bf16[2,128,1,128]{3,1,2,0:T(8,128)(2,1)S(1)}, bf16[2,128,1,128]{3,1,2,0:T(8,128)(2,1)S(1)}, u32[]{:S(2)}, u32[]{:S(2)}) collective-permute-start(bf16[2,128,1,128]{3,1,2,0:T(8,128)(2,1)S(1)} %pad_maximum_fusion.2), channel_id=1, source_target_pairs={{0,20},{4,24},{8,28},{12,32},{16,36},{20,40},{24,44},{28,48},{32,5... | collective-permute-start | bytes 196616 | tf_op jit(solution)/shard_map/ppermute | solution.py:16
  138.9 35.7 %copy-start.13 = (bf16[2,128,1,128]{3,1,2,0:T(8,128)(2,1)}, bf16[2,128,1,128]{3,1,2,0:T(8,128)(2,1)S(1)}, u32[]{:S(2)}) copy-start(bf16[2,128,1,128]{3,1,2,0:T(8,128)(2,1)S(1)} %collective-permute-done) | copy-start | bytes 196612
  138.9 28.2 %collective-permute-start.5 = (bf16[2,128,1,128]{3,1,2,0:T(8,128)(2,1)S(1)}, bf16[2,128,1,128]{3,1,2,0:T(8,128)(2,1)S(1)}, u32[]{:S(2)}, u32[]{:S(2)}) collective-permute-start(bf16[2,128,1,128]{3,1,2,0:T(8,128)(2,1)S(1)} %pad_maximum_fusion.2), channel_id=1, source_target_pairs={{0,24},{4,28},{8,32},{12,36},{16,40},{20,44},{24,48},{28,52},{32,5... | collective-permute-start | bytes 196616 | tf_op jit(solution)/shard_map/ppermute | solution.py:16
  143.5 31.0 %copy-start.15 = (bf16[2,128,1,128]{3,1,2,0:T(8,128)(2,1)}, bf16[2,128,1,128]{3,1,2,0:T(8,128)(2,1)S(1)}, u32[]{:S(2)}) copy-start(bf16[2,128,1,128]{3,1,2,0:T(8,128)(2,1)S(1)} %collective-permute-done.1) | copy-start | bytes 196612
  143.5 24.8 %collective-permute-start.6 = (bf16[2,128,1,128]{3,1,2,0:T(8,128)(2,1)S(1)}, bf16[2,128,1,128]{3,1,2,0:T(8,128)(2,1)S(1)}, u32[]{:S(2)}, u32[]{:S(2)}) collective-permute-start(bf16[2,128,1,128]{3,1,2,0:T(8,128)(2,1)S(1)} %pad_maximum_fusion.2), channel_id=1, source_target_pairs={{0,28},{4,32},{8,36},{12,40},{16,44},{20,48},{24,52},{28,56},{32,6... | collective-permute-start | bytes 196616 | tf_op jit(solution)/shard_map/ppermute | solution.py:16
  180.5 32.2 %all-to-all-start.1 = ((bf16[4,192,1536]{2,1,0:T(8,128)(2,1)}), bf16[4,192,1536]{2,1,0:T(8,128)(2,1)}, u32[]{:S(2)}, u32[]{:S(2)}) async-start(bf16[4,192,1536]{2,1,0:T(8,128)(2,1)} %bitcast.192), calls=%async_computation.1 | async-start | bytes 4718592 | tf_op jit(solution)/shard_map/all_to_all | solution.py:121
  216.4 47.8 %copy-start.10 = (f32[128,8]{0,1:T(8,128)S(1)}, f32[128,8]{0,1:T(8,128)}, u32[]{:S(2)}) copy-start(f32[128,8]{0,1:T(8,128)} %param.13) | copy-start | bytes 12292
  216.4 4.4 %collective-permute-start.7 = (f32[1536]{0:T(1024)S(1)}, f32[1536]{0:T(1024)S(1)}, u32[]{:S(2)}, u32[]{:S(2)}) collective-permute-start(f32[1536]{0:T(1024)S(1)} %fusion.22), channel_id=1, source_target_pairs={{0,1},{1,0},{2,3},{3,2},{4,5},{5,4},{6,7},{7,6},{8,9},{9,8},{10,11... | collective-permute-start | bytes 18440 | tf_op jit(solution)/shard_map/ppermute | solution.py:24
  220.8 5.9 %collective-permute-start.8 = (f32[1536]{0:T(1024)S(1)}, f32[1536]{0:T(1024)S(1)}, u32[]{:S(2)}, u32[]{:S(2)}) collective-permute-start(f32[1536]{0:T(1024)S(1)} %add.153), channel_id=1, source_target_pairs={{0,2},{1,3},{2,0},{3,1},{4,6},{5,7},{6,4},{7,5},{8,10},{9,11},{10,... | collective-permute-start | bytes 18440 | tf_op jit(solution)/shard_map/ppermute | solution.py:24
  227.5 26.4 %all-to-all-start.2 = ((f32[128,1,12]{2,1,0:T(1,128)}), f32[128,1,12]{2,1,0:T(1,128)}, u32[]{:S(2)}, u32[]{:S(2)}) async-start(f32[128,1,12]{2,1,0:T(1,128)} %bitcast.195), calls=%async_computation.2 | async-start | bytes 131072 | tf_op jit(solution)/shard_map/all_to_all | solution.py:136
  245.9 42.4 %all-gather.5.cloned.1.call-start = ((), (), s32[]{:S(2)}) async-start(), calls=%async_computation.4 | async-start | bytes 1310720 | tf_op jit(solution)/shard_map/all_gather | solution.py:145
  257.7 11.5 %copy-start.6 = (bf16[128,8,128]{2,1,0:T(8,128)(2,1)S(1)}, bf16[128,8,128]{2,1,0:T(8,128)(2,1)}, u32[]{:S(2)}) copy-start(bf16[128,8,128]{2,1,0:T(8,128)(2,1)} %param.19) | copy-start | bytes 786436
  275.1 18.2 %copy-start.8 = (bf16[2,1024,1,128]{3,1,2,0:T(8,128)(2,1)S(1)}, bf16[2,1024,1,128]{3,1,2,0:T(8,128)(2,1)}, u32[]{:S(2)}) copy-start(bf16[2,1024,1,128]{3,1,2,0:T(8,128)(2,1)} %constant_dynamic-update-slice_fusion) | copy-start | bytes 1572868
  304.6 15.2 %copy-start.5 = (bf16[1,1,192,1536]{3,2,1,0:T(8,128)(2,1)S(1)}, bf16[1,1,192,1536]{3,2,1,0:T(8,128)(2,1)}, u32[]{:S(2)}) copy-start(bf16[1,1,192,1536]{3,2,1,0:T(8,128)(2,1)} %get-tuple-element.57) | copy-start | bytes 1769476
  307.0 31.4 %copy-start.3 = (bf16[8,128,1024]{1,2,0:T(8,128)(2,1)S(1)}, bf16[8,128,1024]{1,2,0:T(8,128)(2,1)}, u32[]{:S(2)}) copy-start(bf16[8,128,1024]{1,2,0:T(8,128)(2,1)} %get-tuple-element.55) | copy-start | bytes 6291460
  307.0 31.4 %copy-start.9 = (bf16[2,1024,1,128]{3,1,2,0:T(8,128)(2,1)S(1)}, bf16[2,1024,1,128]{3,1,2,0:T(8,128)(2,1)}, u32[]{:S(2)}) copy-start(bf16[2,1024,1,128]{3,1,2,0:T(8,128)(2,1)} %constant_dynamic-update-slice_fusion) | copy-start | bytes 1572868
  307.8 26.4 %collective-permute-start.15 = (bf16[2,128,1,128]{3,1,2,0:T(8,128)(2,1)S(1)}, bf16[2,128,1,128]{3,1,2,0:T(8,128)(2,1)S(1)}, u32[]{:S(2)}, u32[]{:S(2)}) collective-permute-start(bf16[2,128,1,128]{3,1,2,0:T(8,128)(2,1)S(1)} %get-tuple-element.59), channel_id=1, source_target_pairs={{28,0},{32,4},{36,8},{40,12},{44,16},{48,20},{52,24},{56,28},{60,3... | collective-permute-start | bytes 196616 | tf_op jit(solution)/shard_map/ppermute | solution.py:16
  317.3 18.9 %collective-permute-start.14 = (bf16[2,128,1,128]{3,1,0,2:T(8,128)(2,1)S(1)}, bf16[2,128,1,128]{3,1,0,2:T(8,128)(2,1)S(1)}, u32[]{:S(2)}, u32[]{:S(2)}) collective-permute-start(bf16[2,128,1,128]{3,1,0,2:T(8,128)(2,1)S(1)} %get-tuple-element.60), channel_id=1, source_target_pairs={{24,0},{28,4},{32,8},{36,12},{40,16},{44,20},{48,24},{52,28},{56,3... | collective-permute-start | bytes 196616 | tf_op jit(solution)/shard_map/ppermute | solution.py:16
  321.0 18.9 %collective-permute-start.13 = (bf16[2,128,1,128]{3,1,0,2:T(8,128)(2,1)}, bf16[2,128,1,128]{3,1,0,2:T(8,128)(2,1)S(1)}, u32[]{:S(2)}, u32[]{:S(2)}) collective-permute-start(bf16[2,128,1,128]{3,1,0,2:T(8,128)(2,1)} %get-tuple-element.61), channel_id=1, source_target_pairs={{20,0},{24,4},{28,8},{32,12},{36,16},{40,20},{44,24},{48,28},{52,3... | collective-permute-start | bytes 196616 | tf_op jit(solution)/shard_map/ppermute | solution.py:16
  326.1 13.7 %collective-permute-start.12 = (bf16[2,128,1,128]{3,1,0,2:T(8,128)(2,1)}, bf16[2,128,1,128]{3,1,0,2:T(8,128)(2,1)S(1)}, u32[]{:S(2)}, u32[]{:S(2)}) collective-permute-start(bf16[2,128,1,128]{3,1,0,2:T(8,128)(2,1)} %get-tuple-element.62), channel_id=1, source_target_pairs={{16,0},{20,4},{24,8},{28,12},{32,16},{36,20},{40,24},{44,28},{48,3... | collective-permute-start | bytes 196616 | tf_op jit(solution)/shard_map/ppermute | solution.py:16
  329.8 10.1 %collective-permute-start.11 = (bf16[2,128,1,128]{3,1,0,2:T(8,128)(2,1)S(1)}, bf16[2,128,1,128]{3,1,0,2:T(8,128)(2,1)S(1)}, u32[]{:S(2)}, u32[]{:S(2)}) collective-permute-start(bf16[2,128,1,128]{3,1,0,2:T(8,128)(2,1)S(1)} %get-tuple-element.63), channel_id=1, source_target_pairs={{12,0},{16,4},{20,8},{24,12},{28,16},{32,20},{36,24},{40,28},{44,3... | collective-permute-start | bytes 196616 | tf_op jit(solution)/shard_map/ppermute | solution.py:16
  334.2 5.7 %collective-permute-start.10 = (bf16[2,128,1,128]{3,1,0,2:T(8,128)(2,1)S(1)}, bf16[2,128,1,128]{3,1,0,2:T(8,128)(2,1)S(1)}, u32[]{:S(2)}, u32[]{:S(2)}) collective-permute-start(bf16[2,128,1,128]{3,1,0,2:T(8,128)(2,1)S(1)} %get-tuple-element.64), channel_id=1, source_target_pairs={{8,0},{12,4},{16,8},{20,12},{24,16},{28,20},{32,24},{36,28},{40,32... | collective-permute-start | bytes 196616 | tf_op jit(solution)/shard_map/ppermute | solution.py:16
  336.2 5.6 %collective-permute-start.9 = (bf16[2,128,1,128]{3,1,0,2:T(8,128)(2,1)S(1)}, bf16[2,128,1,128]{3,1,0,2:T(8,128)(2,1)S(1)}, u32[]{:S(2)}, u32[]{:S(2)}) collective-permute-start(bf16[2,128,1,128]{3,1,0,2:T(8,128)(2,1)S(1)} %get-tuple-element.58), channel_id=1, source_target_pairs={{4,0},{8,4},{12,8},{16,12},{20,16},{24,20},{28,24},{32,28},{36,32}... | collective-permute-start | bytes 196616 | tf_op jit(solution)/shard_map/ppermute | solution.py:16
  (17 other events, 112.7 us)
Sparse Core Ops, SparseCore 0:
  11.1 191.7 all-gather.2
  267.3 20.8 all-gather.4

commit v10 on v9

--- a/solution.py
+++ b/solution.py
@@ -136,7 +136,11 @@
     returned = lax.all_to_all(
         slot_grad.reshape(seq_count, capacity), "seq", split_axis=0, concat_axis=0, tiled=True
     )
-    route_grad = jnp.take(returned.reshape(-1), target.reshape(-1)).reshape(tokens_here, top_count)
+    flat_returned = returned.reshape(-1)
+    match = target.reshape(-1)[:, None] == jnp.arange(slots_all, dtype=jnp.int32)[None, :]
+    route_grad = jnp.sum(jnp.where(match, flat_returned[None, :], 0.0), axis=1).reshape(
+        tokens_here, top_count
+    )
     logit_grad = weights * (route_grad - jnp.sum(weights * route_grad, axis=1, keepdims=True))
     dense = jnp.einsum("tk,tke->te", logit_grad, hits, precision=highest)
     router_term = jnp.dot(dense, router.astype(jnp.float32), precision=highest)

time: 352 us -> 356 us (1.011)
  waiting for transfers between devices: 132 us -> 127 us
    gather x3 -> x0, local copies, waits for them, and re-layouts: 6.54 us -> none  [per_device(): jnp.take(returned.reshape(-1), target.reshape(-1))]
    unnamed x66 -> x55, local copies, waits for them, and re-layouts: 7.69 us -> 13.8 us
    all_to_all x1, starting transfers between devices: 18.4 us -> 14.7 us  [per_device(): lax.all_to_all(slot_grad.reshape(seq_count, capacity), 'seq', split_axis=...]
  transfers between devices with their start and end apart: 21 -> 21, of which waited for: 9 -> 9; matrix products, arithmetic and copies ran while one was open for 18% -> 19% of each run, Pallas kernels for 0% -> 0%
where the time goes in v10:
time: 356 us; the launch traced here: 354 us
  waiting for transfers between devices  127 us (36%)
  starting transfers between devices  119 us (33%)
  local copies, waits for them, and re-layouts  33.6 us (9%)
  matrix products  31.5 us (9%)
  other arithmetic  28.5 us (8%)
  between operations  14.7 us (4%)
    ppermute x14, waiting for transfers between devices, passed_along(): return lax.ppermute(array, axis, pairs)  83 us
    ppermute x14, starting transfers between devices, passed_along(): return lax.ppermute(array, axis, pairs)  74.7 us
    all_to_all x1, waiting for transfers between devices, per_device(): lax.all_to_all(partial.reshape(head_count, -1, slots_all), 'head', split_...  23.9 us
    all_to_all x1, starting transfers between devices, per_device(): lax.all_to_all(payload, 'seq', split_axis=0, concat_axis=0, tiled=True)  18.2 us
    all_to_all x1, starting transfers between devices, per_device(): lax.all_to_all(slot_grad.reshape(seq_count, capacity), 'seq', split_axis=...  14.7 us
    unnamed x55, local copies, waits for them, and re-layouts  13.8 us
    all_gather x1, waiting for transfers between devices, per_device(): input_grad = lax.all_gather(input_slice, 'head', axis=1, tiled=True)  11.4 us
  transfers between devices with their start and end apart: 21, of which 9 were waited for; matrix products, arithmetic and copies ran while one was open for 19% of the time, Pallas kernels for 0%

profile of v10, /device:TPU:49, one launch (start us, length us, event | category | flops | bytes accessed | tf_op | source)
XLA Modules:
  0.0 353.7 jit_solution(2186504543930853905)
XLA Ops:
  14.4 7.1 %fusion.13 = bf16[2048,1024]{1,0:T(8,128)(2,1)} fusion(bf16[128,1024]{1,0:T(8,128)(2,1)} %param.11, s32[1024]{0:T(1024)S(1)} %eq.67, s32[1024]{0:T(1024)S(1)} %add_select_fusion), kind=kOutput, calls=%fused_computation.34 | convolution fusion | flops 1076232192 | bytes 4464640 | tf_op jit(solution)/shard_map/dot_general | solution.py:97
  21.4 4.5 %select_convert_fusion = bf16[128,16,1024]{2,1,0:T(8,128)(2,1)} fusion(bf16[128,16,1024]{2,1,0:T(8,128)(2,1)} %bitcast.190, bf16[128,1024]{1,0:T(8,128)(2,1)S(1)} %pad.4, pred[16]{0:T(512)(128)(4,1)S(1)} %iota_compare_fusion.14), kind=kLoop, calls=%fused_computation | loop fusion | flops 2097152 | bytes 8650768 | tf_op jit(solution)/shard_map/convert_element_type | solution.py:103
  26.0 18.2 %all-to-all-start = ((bf16[128,16,1024]{2,1,0:T(8,128)(2,1)}), bf16[128,16,1024]{2,1,0:T(8,128)(2,1)}, u32[]{:S(2)}, u32[]{:S(2)}) async-start(bf16[128,16,1024]{2,1,0:T(8,128)(2,1)} %select_convert_fusion), calls=%async_computation | async-start | bytes 8388608 | tf_op jit(solution)/shard_map/all_to_all | solution.py:112
  44.2 3.4 collective-permute-start
  47.6 3.1 collective-permute-start.1
  50.7 3.2 collective-permute-start.2
  54.0 4.3 %collective-permute-start.3 = (bf16[2,128,1,128]{3,1,2,0:T(8,128)(2,1)S(1)}, bf16[2,128,1,128]{3,1,2,0:T(8,128)(2,1)S(1)}, u32[]{:S(2)}, u32[]{:S(2)}) collective-permute-start(bf16[2,128,1,128]{3,1,2,0:T(8,128)(2,1)S(1)} %pad_maximum_fusion.2), channel_id=1, source_target_pairs={{0,16},{4,20},{8,24},{12,28},{16,32},{20,36},{24,40},{28,44},{32,4... | collective-permute-start | bytes 196616 | tf_op jit(solution)/shard_map/ppermute | solution.py:16
  58.3 2.6 collective-permute-start.4
  61.0 77.9 %collective-permute-done = bf16[2,128,1,128]{3,1,2,0:T(8,128)(2,1)S(1)} collective-permute-done((bf16[2,128,1,128]{3,1,2,0:T(8,128)(2,1)S(1)}, bf16[2,128,1,128]{3,1,2,0:T(8,128)(2,1)S(1)}, u32[]{:S(2)}, u32[]{:S(2)}) %collective-permute-start) | collective-permute-done | bytes 65568 | tf_op jit(solution)/shard_map/ppermute | solution.py:16
  140.8 2.8 collective-permute-done.1
  143.6 26.8 %collective-permute-start.6 = (bf16[2,128,1,128]{3,1,2,0:T(8,128)(2,1)S(1)}, bf16[2,128,1,128]{3,1,2,0:T(8,128)(2,1)S(1)}, u32[]{:S(2)}, u32[]{:S(2)}) collective-permute-start(bf16[2,128,1,128]{3,1,2,0:T(8,128)(2,1)S(1)} %pad_maximum_fusion.2), channel_id=1, source_target_pairs={{0,28},{4,32},{8,36},{12,40},{16,44},{20,48},{24,52},{28,56},{32,6... | collective-permute-start | bytes 196616 | tf_op jit(solution)/shard_map/ppermute | solution.py:16
  171.8 6.2 %reshape.431 = bf16[1536,1024]{1,0:T(8,128)(2,1)} reshape(bf16[128,12,1024]{2,1,0:T(8,128)(2,1)} %bitcast.185) | data formatting | bytes 6291456 | tf_op jit(solution)/shard_map/reshape | solution.py:114
  178.0 5.9 %convolution_convert_fusion = bf16[1536,768]{0,1:T(8,128)(2,1)} fusion(bf16[1536,1024]{1,0:T(8,128)(2,1)} %reshape.431, bf16[1,768,1024]{2,1,0:T(8,128)(2,1)S(1)} %copy-done), kind=kOutput, calls=%fused_computation.17 | convolution fusion | flops 2417098752 | bytes 7077888 | tf_op jit(solution)/shard_map/dot_general | solution.py:118
  183.9 5.8 %all-to-all-start.1 = ((bf16[4,192,1536]{2,1,0:T(8,128)(2,1)}), bf16[4,192,1536]{2,1,0:T(8,128)(2,1)}, u32[]{:S(2)}, u32[]{:S(2)}) async-start(bf16[4,192,1536]{2,1,0:T(8,128)(2,1)} %bitcast.191), calls=%async_computation.1 | async-start | bytes 4718592 | tf_op jit(solution)/shard_map/all_to_all | solution.py:121
  193.8 23.9 %all-to-all-done.1 = bf16[4,192,1536]{2,1,0:T(8,128)(2,1)} async-done(((bf16[4,192,1536]{2,1,0:T(8,128)(2,1)}), bf16[4,192,1536]{2,1,0:T(8,128)(2,1)}, u32[]{:S(2)}, u32[]{:S(2)}) %all-to-all-start.1) | async-done | bytes 2359328 | tf_op jit(solution)/shard_map/all_to_all | solution.py:121
  221.5 2.4 collective-permute-start.7
  225.9 3.0 collective-permute-start.8
  232.6 14.7 %all-to-all-start.2 = ((f32[128,1,12]{2,1,0:T(1,128)}), f32[128,1,12]{2,1,0:T(1,128)}, u32[]{:S(2)}, u32[]{:S(2)}) async-start(f32[128,1,12]{2,1,0:T(1,128)} %bitcast.194), calls=%async_computation.2 | async-start | bytes 131072 | tf_op jit(solution)/shard_map/all_to_all | solution.py:136
  249.7 5.7 %all-to-all-done.2 = f32[128,1,12]{2,1,0:T(1,128)} async-done(((f32[128,1,12]{2,1,0:T(1,128)}), f32[128,1,12]{2,1,0:T(1,128)}, u32[]{:S(2)}, u32[]{:S(2)}) %all-to-all-start.2) | async-done | bytes 6176 | tf_op jit(solution)/shard_map/all_to_all | solution.py:136
  255.9 2.3 reduce.10
  279.5 11.4 %all-gather.5.cloned.1.call-done = bf16[128,4096]{1,0:T(8,128)(2,1)} async-done(((bf16[128,1024]{1,0:T(8,128)(2,1)}), bf16[128,4096]{1,0:T(8,128)(2,1)}) %all-gather.5.cloned.1.call-update) | async-done | bytes 1048592 | tf_op jit(solution)/shard_map/all_gather | solution.py:149
  290.9 5.1 %convolution_convert_fusion.1 = bf16[128,1024]{1,0:T(8,128)(2,1)S(1)} fusion(bf16[128,4096]{1,0:T(8,128)(2,1)} %all-gather.5.cloned.1.call-done, bf16[1024,4096]{0,1:T(8,128)(2,1)} %all-gather.3.cloned.1.call-done), kind=kOutput, calls=%fused_computation.40 | convolution fusion | flops 1073872896 | bytes 9699328 | tf_op jit(solution)/shard_map/dot_general | solution.py:150
  296.0 2.2 fusion.1
  298.3 3.4 convert_bitcast_fusion
  301.7 4.2 %copy.96 = bf16[8,128,1024]{2,0,1:T(8,128)(2,1)} copy(bf16[8,128,1024]{1,2,0:T(8,128)(2,1)} %get-tuple-element.52) | data formatting | bytes 4194304 | tf_op jit(solution)/shard_map/reshape.32
  308.2 2.4 fusion.14
  311.4 9.3 %collective-permute-start.15 = (bf16[2,128,1,128]{3,1,2,0:T(8,128)(2,1)S(1)}, bf16[2,128,1,128]{3,1,2,0:T(8,128)(2,1)S(1)}, u32[]{:S(2)}, u32[]{:S(2)}) collective-permute-start(bf16[2,128,1,128]{3,1,2,0:T(8,128)(2,1)S(1)} %get-tuple-element.57), channel_id=1, source_target_pairs={{28,0},{32,4},{36,8},{40,12},{44,16},{48,20},{52,24},{56,28},{60,3... | collective-permute-start | bytes 196616 | tf_op jit(solution)/shard_map/ppermute | solution.py:16
  320.7 2.5 collective-permute-start.14
  324.4 5.2 %collective-permute-start.13 = (bf16[2,128,1,128]{3,1,0,2:T(8,128)(2,1)}, bf16[2,128,1,128]{3,1,0,2:T(8,128)(2,1)S(1)}, u32[]{:S(2)}, u32[]{:S(2)}) collective-permute-start(bf16[2,128,1,128]{3,1,0,2:T(8,128)(2,1)} %get-tuple-element.59), channel_id=1, source_target_pairs={{20,0},{24,4},{28,8},{32,12},{36,16},{40,20},{44,24},{48,28},{52,3... | collective-permute-start | bytes 196616 | tf_op jit(solution)/shard_map/ppermute | solution.py:16
  329.6 3.6 %collective-permute-start.12 = (bf16[2,128,1,128]{3,1,0,2:T(8,128)(2,1)}, bf16[2,128,1,128]{3,1,0,2:T(8,128)(2,1)S(1)}, u32[]{:S(2)}, u32[]{:S(2)}) collective-permute-start(bf16[2,128,1,128]{3,1,0,2:T(8,128)(2,1)} %get-tuple-element.60), channel_id=1, source_target_pairs={{16,0},{20,4},{24,8},{28,12},{32,16},{36,20},{40,24},{44,28},{48,3... | collective-permute-start | bytes 196616 | tf_op jit(solution)/shard_map/ppermute | solution.py:16
  333.2 4.4 %collective-permute-start.11 = (bf16[2,128,1,128]{3,1,0,2:T(8,128)(2,1)S(1)}, bf16[2,128,1,128]{3,1,0,2:T(8,128)(2,1)S(1)}, u32[]{:S(2)}, u32[]{:S(2)}) collective-permute-start(bf16[2,128,1,128]{3,1,0,2:T(8,128)(2,1)S(1)} %get-tuple-element.61), channel_id=1, source_target_pairs={{12,0},{16,4},{20,8},{24,12},{28,16},{32,20},{36,24},{40,28},{44,3... | collective-permute-start | bytes 196616 | tf_op jit(solution)/shard_map/ppermute | solution.py:16
  339.7 2.2 collective-permute-start.9
  (135 shorter events, 59.2 us)
Async XLA Ops:
  7.2 170.8 %copy-start = (bf16[1,768,1024]{2,1,0:T(8,128)(2,1)S(1)}, bf16[1,768,1024]{2,1,0:T(8,128)(2,1)}, u32[]{:S(2)}) copy-start(bf16[1,768,1024]{2,1,0:T(8,128)(2,1)} %param.16) | copy-start | bytes 4718596
  7.2 262.7 %all-gather.3.cloned.1.call-start = ((), (), s32[]{:S(2)}) async-start(), calls=%async_computation.3 | async-start | bytes 8454144 | tf_op jit(solution)/shard_map/all_gather | solution.py:104
  26.0 18.3 %copy-start.17 = (bf16[128,1,128]{2,0,1:T(8,128)(2,1)S(1)}, bf16[128,1,128]{2,0,1:T(8,128)(2,1)}, u32[]{:S(2)}) copy-start(bf16[128,1,128]{2,0,1:T(8,128)(2,1)} %param.21) | copy-start | bytes 98308
  26.0 18.3 %copy-start.18 = (bf16[128,1,128]{2,0,1:T(8,128)(2,1)S(1)}, bf16[128,1,128]{2,0,1:T(8,128)(2,1)}, u32[]{:S(2)}) copy-start(bf16[128,1,128]{2,0,1:T(8,128)(2,1)} %param.20) | copy-start | bytes 98308
  26.0 145.8 %all-to-all-start = ((bf16[128,16,1024]{2,1,0:T(8,128)(2,1)}), bf16[128,16,1024]{2,1,0:T(8,128)(2,1)}, u32[]{:S(2)}, u32[]{:S(2)}) async-start(bf16[128,16,1024]{2,1,0:T(8,128)(2,1)} %select_convert_fusion), calls=%async_computation | async-start | bytes 8388608 | tf_op jit(solution)/shard_map/all_to_all | solution.py:112
  44.2 94.6 %collective-permute-start = (bf16[2,128,1,128]{3,1,2,0:T(8,128)(2,1)S(1)}, bf16[2,128,1,128]{3,1,2,0:T(8,128)(2,1)S(1)}, u32[]{:S(2)}, u32[]{:S(2)}) collective-permute-start(bf16[2,128,1,128]{3,1,2,0:T(8,128)(2,1)S(1)} %pad_maximum_fusion.2), channel_id=1, source_target_pairs={{0,4},{4,8},{8,12},{12,16},{16,20},{20,24},{24,28},{28,32},{32,36}... | collective-permute-start | bytes 196616 | tf_op jit(solution)/shard_map/ppermute | solution.py:16
  47.6 96.0 %collective-permute-start.1 = (bf16[2,128,1,128]{3,1,2,0:T(8,128)(2,1)S(1)}, bf16[2,128,1,128]{3,1,2,0:T(8,128)(2,1)S(1)}, u32[]{:S(2)}, u32[]{:S(2)}) collective-permute-start(bf16[2,128,1,128]{3,1,2,0:T(8,128)(2,1)S(1)} %pad_maximum_fusion.2), channel_id=1, source_target_pairs={{0,8},{4,12},{8,16},{12,20},{16,24},{20,28},{24,32},{28,36},{32,40... | collective-permute-start | bytes 196616 | tf_op jit(solution)/shard_map/ppermute | solution.py:16
  50.7 119.7 %collective-permute-start.2 = (bf16[2,128,1,128]{3,1,2,0:T(8,128)(2,1)S(1)}, bf16[2,128,1,128]{3,1,2,0:T(8,128)(2,1)S(1)}, u32[]{:S(2)}, u32[]{:S(2)}) collective-permute-start(bf16[2,128,1,128]{3,1,2,0:T(8,128)(2,1)S(1)} %pad_maximum_fusion.2), channel_id=1, source_target_pairs={{0,12},{4,16},{8,20},{12,24},{16,28},{20,32},{24,36},{28,40},{32,4... | collective-permute-start | bytes 196616 | tf_op jit(solution)/shard_map/ppermute | solution.py:16
  54.0 116.5 %collective-permute-start.3 = (bf16[2,128,1,128]{3,1,2,0:T(8,128)(2,1)S(1)}, bf16[2,128,1,128]{3,1,2,0:T(8,128)(2,1)S(1)}, u32[]{:S(2)}, u32[]{:S(2)}) collective-permute-start(bf16[2,128,1,128]{3,1,2,0:T(8,128)(2,1)S(1)} %pad_maximum_fusion.2), channel_id=1, source_target_pairs={{0,16},{4,20},{8,24},{12,28},{16,32},{20,36},{24,40},{28,44},{32,4... | collective-permute-start | bytes 196616 | tf_op jit(solution)/shard_map/ppermute | solution.py:16
  58.3 112.2 %collective-permute-start.4 = (bf16[2,128,1,128]{3,1,2,0:T(8,128)(2,1)S(1)}, bf16[2,128,1,128]{3,1,2,0:T(8,128)(2,1)S(1)}, u32[]{:S(2)}, u32[]{:S(2)}) collective-permute-start(bf16[2,128,1,128]{3,1,2,0:T(8,128)(2,1)S(1)} %pad_maximum_fusion.2), channel_id=1, source_target_pairs={{0,20},{4,24},{8,28},{12,32},{16,36},{20,40},{24,44},{28,48},{32,5... | collective-permute-start | bytes 196616 | tf_op jit(solution)/shard_map/ppermute | solution.py:16
  138.8 39.1 %copy-start.11 = (bf16[2,128,1,128]{3,1,2,0:T(8,128)(2,1)}, bf16[2,128,1,128]{3,1,2,0:T(8,128)(2,1)S(1)}, u32[]{:S(2)}) copy-start(bf16[2,128,1,128]{3,1,2,0:T(8,128)(2,1)S(1)} %collective-permute-done) | copy-start | bytes 196612
  138.8 31.7 %collective-permute-start.5 = (bf16[2,128,1,128]{3,1,2,0:T(8,128)(2,1)S(1)}, bf16[2,128,1,128]{3,1,2,0:T(8,128)(2,1)S(1)}, u32[]{:S(2)}, u32[]{:S(2)}) collective-permute-start(bf16[2,128,1,128]{3,1,2,0:T(8,128)(2,1)S(1)} %pad_maximum_fusion.2), channel_id=1, source_target_pairs={{0,24},{4,28},{8,32},{12,36},{16,40},{20,44},{24,48},{28,52},{32,5... | collective-permute-start | bytes 196616 | tf_op jit(solution)/shard_map/ppermute | solution.py:16
  143.6 34.3 %copy-start.12 = (bf16[2,128,1,128]{3,1,2,0:T(8,128)(2,1)}, bf16[2,128,1,128]{3,1,2,0:T(8,128)(2,1)S(1)}, u32[]{:S(2)}) copy-start(bf16[2,128,1,128]{3,1,2,0:T(8,128)(2,1)S(1)} %collective-permute-done.1) | copy-start | bytes 196612
  143.6 28.2 %collective-permute-start.6 = (bf16[2,128,1,128]{3,1,2,0:T(8,128)(2,1)S(1)}, bf16[2,128,1,128]{3,1,2,0:T(8,128)(2,1)S(1)}, u32[]{:S(2)}, u32[]{:S(2)}) collective-permute-start(bf16[2,128,1,128]{3,1,2,0:T(8,128)(2,1)S(1)} %pad_maximum_fusion.2), channel_id=1, source_target_pairs={{0,28},{4,32},{8,36},{12,40},{16,44},{20,48},{24,52},{28,56},{32,6... | collective-permute-start | bytes 196616 | tf_op jit(solution)/shard_map/ppermute | solution.py:16
  183.9 33.8 %all-to-all-start.1 = ((bf16[4,192,1536]{2,1,0:T(8,128)(2,1)}), bf16[4,192,1536]{2,1,0:T(8,128)(2,1)}, u32[]{:S(2)}, u32[]{:S(2)}) async-start(bf16[4,192,1536]{2,1,0:T(8,128)(2,1)} %bitcast.191), calls=%async_computation.1 | async-start | bytes 4718592 | tf_op jit(solution)/shard_map/all_to_all | solution.py:121
  193.8 69.2 %copy-start.8 = (f32[128,8]{0,1:T(8,128)S(1)}, f32[128,8]{0,1:T(8,128)}, u32[]{:S(2)}) copy-start(f32[128,8]{0,1:T(8,128)} %param.13) | copy-start | bytes 12292
  219.8 48.0 %copy-start.7 = (bf16[128,1024]{1,0:T(8,128)(2,1)S(1)}, bf16[128,1024]{1,0:T(8,128)(2,1)}, u32[]{:S(2)}) copy-start(bf16[128,1024]{1,0:T(8,128)(2,1)} %param.11) | copy-start | bytes 786436
  219.8 53.7 %copy-start.6 = (bf16[128,8,128]{2,1,0:T(8,128)(2,1)S(1)}, bf16[128,8,128]{2,1,0:T(8,128)(2,1)}, u32[]{:S(2)}) copy-start(bf16[128,8,128]{2,1,0:T(8,128)(2,1)} %param.19) | copy-start | bytes 786436
  221.5 4.4 %collective-permute-start.7 = (f32[1536]{0:T(1024)S(1)}, f32[1536]{0:T(1024)S(1)}, u32[]{:S(2)}, u32[]{:S(2)}) collective-permute-start(f32[1536]{0:T(1024)S(1)} %fusion.22), channel_id=1, source_target_pairs={{0,1},{1,0},{2,3},{3,2},{4,5},{5,4},{6,7},{7,6},{8,9},{9,8},{10,11... | collective-permute-start | bytes 18440 | tf_op jit(solution)/shard_map/ppermute | solution.py:24
  225.9 5.9 %collective-permute-start.8 = (f32[1536]{0:T(1024)S(1)}, f32[1536]{0:T(1024)S(1)}, u32[]{:S(2)}, u32[]{:S(2)}) collective-permute-start(f32[1536]{0:T(1024)S(1)} %add.129), channel_id=1, source_target_pairs={{0,2},{1,3},{2,0},{3,1},{4,6},{5,7},{6,4},{7,5},{8,10},{9,11},{10,... | collective-permute-start | bytes 18440 | tf_op jit(solution)/shard_map/ppermute | solution.py:24
  232.6 22.9 %all-to-all-start.2 = ((f32[128,1,12]{2,1,0:T(1,128)}), f32[128,1,12]{2,1,0:T(1,128)}, u32[]{:S(2)}, u32[]{:S(2)}) async-start(f32[128,1,12]{2,1,0:T(1,128)} %bitcast.194), calls=%async_computation.2 | async-start | bytes 131072 | tf_op jit(solution)/shard_map/all_to_all | solution.py:136
  247.3 43.7 %all-gather.5.cloned.1.call-start = ((), (), s32[]{:S(2)}) async-start(), calls=%async_computation.4 | async-start | bytes 1310720 | tf_op jit(solution)/shard_map/all_gather | solution.py:149
  263.0 12.2 %copy-start.16 = (f32[128,8]{0,1:T(8,128)}, f32[128,8]{0,1:T(8,128)S(1)}, u32[]{:S(2)}) copy-start(f32[128,8]{0,1:T(8,128)S(1)} %copy.100) | copy-start | bytes 12292
  308.2 15.1 %copy-start.5 = (bf16[1,1,192,1536]{3,2,1,0:T(8,128)(2,1)S(1)}, bf16[1,1,192,1536]{3,2,1,0:T(8,128)(2,1)}, u32[]{:S(2)}) copy-start(bf16[1,1,192,1536]{3,2,1,0:T(8,128)(2,1)} %get-tuple-element.55) | copy-start | bytes 1769476
  310.6 31.3 %copy-start.3 = (bf16[8,128,1024]{1,2,0:T(8,128)(2,1)S(1)}, bf16[8,128,1024]{1,2,0:T(8,128)(2,1)}, u32[]{:S(2)}) copy-start(bf16[8,128,1024]{1,2,0:T(8,128)(2,1)} %get-tuple-element.53) | copy-start | bytes 6291460
  311.4 26.2 %collective-permute-start.15 = (bf16[2,128,1,128]{3,1,2,0:T(8,128)(2,1)S(1)}, bf16[2,128,1,128]{3,1,2,0:T(8,128)(2,1)S(1)}, u32[]{:S(2)}, u32[]{:S(2)}) collective-permute-start(bf16[2,128,1,128]{3,1,2,0:T(8,128)(2,1)S(1)} %get-tuple-element.57), channel_id=1, source_target_pairs={{28,0},{32,4},{36,8},{40,12},{44,16},{48,20},{52,24},{56,28},{60,3... | collective-permute-start | bytes 196616 | tf_op jit(solution)/shard_map/ppermute | solution.py:16
  320.7 18.9 %collective-permute-start.14 = (bf16[2,128,1,128]{3,1,0,2:T(8,128)(2,1)S(1)}, bf16[2,128,1,128]{3,1,0,2:T(8,128)(2,1)S(1)}, u32[]{:S(2)}, u32[]{:S(2)}) collective-permute-start(bf16[2,128,1,128]{3,1,0,2:T(8,128)(2,1)S(1)} %get-tuple-element.58), channel_id=1, source_target_pairs={{24,0},{28,4},{32,8},{36,12},{40,16},{44,20},{48,24},{52,28},{56,3... | collective-permute-start | bytes 196616 | tf_op jit(solution)/shard_map/ppermute | solution.py:16
  324.4 19.8 %collective-permute-start.13 = (bf16[2,128,1,128]{3,1,0,2:T(8,128)(2,1)}, bf16[2,128,1,128]{3,1,0,2:T(8,128)(2,1)S(1)}, u32[]{:S(2)}, u32[]{:S(2)}) collective-permute-start(bf16[2,128,1,128]{3,1,0,2:T(8,128)(2,1)} %get-tuple-element.59), channel_id=1, source_target_pairs={{20,0},{24,4},{28,8},{32,12},{36,16},{40,20},{44,24},{48,28},{52,3... | collective-permute-start | bytes 196616 | tf_op jit(solution)/shard_map/ppermute | solution.py:16
  329.6 14.6 %collective-permute-start.12 = (bf16[2,128,1,128]{3,1,0,2:T(8,128)(2,1)}, bf16[2,128,1,128]{3,1,0,2:T(8,128)(2,1)S(1)}, u32[]{:S(2)}, u32[]{:S(2)}) collective-permute-start(bf16[2,128,1,128]{3,1,0,2:T(8,128)(2,1)} %get-tuple-element.60), channel_id=1, source_target_pairs={{16,0},{20,4},{24,8},{28,12},{32,16},{36,20},{40,24},{44,28},{48,3... | collective-permute-start | bytes 196616 | tf_op jit(solution)/shard_map/ppermute | solution.py:16
  333.2 11.0 %collective-permute-start.11 = (bf16[2,128,1,128]{3,1,0,2:T(8,128)(2,1)S(1)}, bf16[2,128,1,128]{3,1,0,2:T(8,128)(2,1)S(1)}, u32[]{:S(2)}, u32[]{:S(2)}) collective-permute-start(bf16[2,128,1,128]{3,1,0,2:T(8,128)(2,1)S(1)} %get-tuple-element.61), channel_id=1, source_target_pairs={{12,0},{16,4},{20,8},{24,12},{28,16},{32,20},{36,24},{40,28},{44,3... | collective-permute-start | bytes 196616 | tf_op jit(solution)/shard_map/ppermute | solution.py:16
  337.6 6.6 %collective-permute-start.10 = (bf16[2,128,1,128]{3,1,0,2:T(8,128)(2,1)S(1)}, bf16[2,128,1,128]{3,1,0,2:T(8,128)(2,1)S(1)}, u32[]{:S(2)}, u32[]{:S(2)}) collective-permute-start(bf16[2,128,1,128]{3,1,0,2:T(8,128)(2,1)S(1)} %get-tuple-element.62), channel_id=1, source_target_pairs={{8,0},{12,4},{16,8},{20,12},{24,16},{28,20},{32,24},{36,28},{40,32... | collective-permute-start | bytes 196616 | tf_op jit(solution)/shard_map/ppermute | solution.py:16
  339.7 5.6 %collective-permute-start.9 = (bf16[2,128,1,128]{3,1,0,2:T(8,128)(2,1)S(1)}, bf16[2,128,1,128]{3,1,0,2:T(8,128)(2,1)S(1)}, u32[]{:S(2)}, u32[]{:S(2)}) collective-permute-start(bf16[2,128,1,128]{3,1,0,2:T(8,128)(2,1)S(1)} %get-tuple-element.56), channel_id=1, source_target_pairs={{4,0},{8,4},{12,8},{16,12},{20,16},{24,20},{28,24},{32,28},{36,32}... | collective-permute-start | bytes 196616 | tf_op jit(solution)/shard_map/ppermute | solution.py:16
  (11 other events, 46.7 us)
Sparse Core Ops, SparseCore 0:
  11.1 188.6 all-gather.2
  270.0 20.8 all-gather.4

commit v11 on v8

--- a/solution.py
+++ b/solution.py
@@ -133,7 +133,6 @@
     gate_up_grad = jnp.stack([scaled * up * sig * (1.0 + gate * (1.0 - sig)), scaled * act])[
         None
     ].astype(jnp.bfloat16)
-    slot_part, weight_full = lax.optimization_barrier((slot_part, weight_full))
     slot_grad = head_sum(slot_part)
     returned = lax.all_to_all(
         slot_grad.reshape(seq_count, capacity), "seq", split_axis=0, concat_axis=0, tiled=True
@@ -143,6 +142,7 @@
     dense = jnp.einsum("tk,tke->te", logit_grad, hits, precision=highest)
     router_term = jnp.dot(dense, router.astype(jnp.float32), precision=highest)
     input_slice = (out_grad.astype(jnp.float32) + router_term).astype(jnp.bfloat16)
+    input_slice, weight_full = lax.optimization_barrier((input_slice, weight_full))
     input_grad = lax.all_gather(input_slice, "head", axis=1, tiled=True)
     attn_grad = lax.dot_general(
         input_grad,

time: 360 us -> 360 us (level)
  transfers between devices with their start and end apart: 21 -> 21, of which waited for: 9 -> 9; matrix products, arithmetic and copies ran while one was open for 16% -> 22% of each run, Pallas kernels for 0% -> 0%
where the time goes in v11:
time: 360 us; the launch traced here: 357 us
  waiting for transfers between devices  121 us (34%)
  starting transfers between devices  117 us (32%)
  local copies, waits for them, and re-layouts  49.9 us (14%)
  matrix products  28.5 us (8%)
  other arithmetic  26.2 us (7%)
  between operations  14.8 us (4%)
    ppermute x14, starting transfers between devices, passed_along(): return lax.ppermute(array, axis, pairs)  74.6 us
    ppermute x14, waiting for transfers between devices, passed_along(): return lax.ppermute(array, axis, pairs)  73.3 us
    all_to_all x1, waiting for transfers between devices, per_device(): lax.all_to_all(partial.reshape(head_count, -1, slots_all), 'head', split_...  25.4 us
    all_to_all x1, starting transfers between devices, per_device(): lax.all_to_all(payload, 'seq', split_axis=0, concat_axis=0, tiled=True)  18.2 us
    all_to_all x1, starting transfers between devices, per_device(): lax.all_to_all(slot_grad.reshape(seq_count, capacity), 'seq', split_axis=...  14.6 us
    gather x3, local copies, waits for them, and re-layouts, per_device(): jnp.take(returned.reshape(-1), target.reshape(-1))  13.1 us
    all_gather x1, waiting for transfers between devices, per_device(): input_grad = lax.all_gather(input_slice, 'head', axis=1, tiled=True)  11.7 us
    unnamed x62, local copies, waits for them, and re-layouts  9.88 us
  transfers between devices with their start and end apart: 21, of which 9 were waited for; matrix products, arithmetic and copies ran while one was open for 22% of the time, Pallas kernels for 0%

profile of v11, /device:TPU:49, one launch (start us, length us, event | category | flops | bytes accessed | tf_op | source)
XLA Modules:
  0.0 357.5 jit_solution(17907344657264206805)
XLA Ops:
  14.2 5.9 %convolution_convert_fusion = bf16[1536,1024]{1,0:T(8,128)(2,1)} fusion(bf16[128,1024]{1,0:T(8,128)(2,1)} %param.13, s32[1024]{0:T(1024)S(1)} %eq.44, s32[1024]{0:T(1024)S(1)} %add_select_fusion), kind=kOutput, calls=%fused_computation.14 | convolution fusion | flops 808779776 | bytes 3416064 | tf_op jit(solution)/shard_map/dot_general | solution.py:96
  20.1 5.8 %reshape.500 = bf16[128,96,128]{2,1,0:T(8,128)(2,1)} reshape(bf16[1536,1024]{1,0:T(8,128)(2,1)} %convolution_convert_fusion) | data formatting | bytes 6291456 | tf_op jit(solution)/shard_map/reshape | solution.py:103
  25.9 4.1 %fusion.7 = bf16[128,112,128]{2,1,0:T(8,128)(2,1)} fusion(bf16[128,1,12]{2,1,0:T(2,128)(2,1)S(1)} %reshape.529, bf16[128,96,128]{2,1,0:T(8,128)(2,1)} %reshape.500), kind=kLoop, calls=%fused_computation.17 | loop fusion | flops 11010048 | bytes 6818816 | tf_op jit(solution)/shard_map/concatenate | solution.py:102
  29.9 18.2 %all-to-all-start = ((bf16[128,112,128]{2,1,0:T(8,128)(2,1)}), bf16[128,112,128]{2,1,0:T(8,128)(2,1)}, u32[]{:S(2)}, u32[]{:S(2)}) async-start(bf16[128,112,128]{2,1,0:T(8,128)(2,1)} %fusion.7), calls=%async_computation | async-start | bytes 7340032 | tf_op jit(solution)/shard_map/all_to_all | solution.py:113
  48.2 3.4 collective-permute-start
  51.5 3.1 collective-permute-start.1
  54.7 3.2 collective-permute-start.2
  57.9 4.3 %collective-permute-start.3 = (bf16[2,128,1,128]{3,1,2,0:T(8,128)(2,1)S(1)}, bf16[2,128,1,128]{3,1,2,0:T(8,128)(2,1)S(1)}, u32[]{:S(2)}, u32[]{:S(2)}) collective-permute-start(bf16[2,128,1,128]{3,1,2,0:T(8,128)(2,1)S(1)} %pad_maximum_fusion.2), channel_id=1, source_target_pairs={{0,16},{4,20},{8,24},{12,28},{16,32},{20,36},{24,40},{28,44},{32,4... | collective-permute-start | bytes 196616 | tf_op jit(solution)/shard_map/ppermute | solution.py:16
  62.3 2.6 collective-permute-start.4
  65.0 66.2 %collective-permute-done = bf16[2,128,1,128]{3,1,2,0:T(8,128)(2,1)S(1)} collective-permute-done((bf16[2,128,1,128]{3,1,2,0:T(8,128)(2,1)S(1)}, bf16[2,128,1,128]{3,1,2,0:T(8,128)(2,1)S(1)}, u32[]{:S(2)}, u32[]{:S(2)}) %collective-permute-start) | collective-permute-done | bytes 65568 | tf_op jit(solution)/shard_map/ppermute | solution.py:16
  133.2 2.8 collective-permute-done.1
  136.0 26.6 %collective-permute-start.6 = (bf16[2,128,1,128]{3,1,2,0:T(8,128)(2,1)S(1)}, bf16[2,128,1,128]{3,1,2,0:T(8,128)(2,1)S(1)}, u32[]{:S(2)}, u32[]{:S(2)}) collective-permute-start(bf16[2,128,1,128]{3,1,2,0:T(8,128)(2,1)S(1)} %pad_maximum_fusion.2), channel_id=1, source_target_pairs={{0,28},{4,32},{8,36},{12,40},{16,44},{20,48},{24,52},{28,56},{32,6... | collective-permute-start | bytes 196616 | tf_op jit(solution)/shard_map/ppermute | solution.py:16
  164.9 3.8 %slice.80 = bf16[128,96,128]{2,1,0:T(8,128)(2,1)} slice(bf16[128,112,128]{2,1,0:T(8,128)(2,1)} %all-to-all-done), slice={[0:128], [0:96], [0:128]} | slice | bytes 6291456 | tf_op jit(solution)/shard_map/slice | solution.py:115
  168.7 5.9 %reshape.502 = bf16[1536,1024]{1,0:T(8,128)(2,1)} reshape(bf16[128,96,128]{2,1,0:T(8,128)(2,1)} %slice.80) | data formatting | bytes 6291456 | tf_op jit(solution)/shard_map/reshape | solution.py:115
  174.6 5.9 %convolution_convert_fusion.1 = bf16[1536,768]{0,1:T(8,128)(2,1)} fusion(bf16[1536,1024]{1,0:T(8,128)(2,1)} %reshape.502, bf16[1,768,1024]{2,1,0:T(8,128)(2,1)S(1)} %copy-done), kind=kOutput, calls=%fused_computation.18 | convolution fusion | flops 2417098752 | bytes 7077888 | tf_op jit(solution)/shard_map/dot_general | solution.py:119
  180.5 5.3 %all-to-all-start.1 = ((bf16[4,192,1536]{2,1,0:T(8,128)(2,1)}), bf16[4,192,1536]{2,1,0:T(8,128)(2,1)}, u32[]{:S(2)}, u32[]{:S(2)}) async-start(bf16[4,192,1536]{2,1,0:T(8,128)(2,1)} %bitcast.189), calls=%async_computation.1 | async-start | bytes 4718592 | tf_op jit(solution)/shard_map/all_to_all | solution.py:122
  188.6 25.4 %all-to-all-done.1 = bf16[4,192,1536]{2,1,0:T(8,128)(2,1)} async-done(((bf16[4,192,1536]{2,1,0:T(8,128)(2,1)}), bf16[4,192,1536]{2,1,0:T(8,128)(2,1)}, u32[]{:S(2)}, u32[]{:S(2)}) %all-to-all-start.1) | async-done | bytes 2359328 | tf_op jit(solution)/shard_map/all_to_all | solution.py:122
  222.2 2.5 collective-permute-start.8
  225.6 2.5 collective-permute-done.8
  228.9 14.6 %all-to-all-start.2 = ((f32[128,1,12]{2,1,0:T(1,128)}), f32[128,1,12]{2,1,0:T(1,128)}, u32[]{:S(2)}, u32[]{:S(2)}) async-start(f32[128,1,12]{2,1,0:T(1,128)} %bitcast.192), calls=%async_computation.2 | async-start | bytes 131072 | tf_op jit(solution)/shard_map/all_to_all | solution.py:137
  246.0 5.7 %all-to-all-done.2 = f32[128,1,12]{2,1,0:T(1,128)} async-done(((f32[128,1,12]{2,1,0:T(1,128)}), f32[128,1,12]{2,1,0:T(1,128)}, u32[]{:S(2)}, u32[]{:S(2)}) %all-to-all-start.2) | async-done | bytes 6176 | tf_op jit(solution)/shard_map/all_to_all | solution.py:137
  255.5 10.8 %gather_fusion = f32[1024]{0:T(1024)} fusion(f32[1536]{0:T(1024)S(1)} %reshape.504, s32[1024]{0:T(1024)} %broadcast_clamp_fusion), kind=kCustom, calls=%fused_computation | custom fusion | bytes 12288 | tf_op jit(solution)/shard_map/jit(_take)/gather | solution.py:140
  283.8 11.7 %all-gather.5.cloned.1.call-done = bf16[128,4096]{1,0:T(8,128)(2,1)} async-done(((bf16[128,1024]{1,0:T(8,128)(2,1)}), bf16[128,4096]{1,0:T(8,128)(2,1)}) %all-gather.5.cloned.1.call-update) | async-done | bytes 1048592 | tf_op jit(solution)/shard_map/all_gather | solution.py:146
  295.5 5.1 %convolution_convert_fusion.2 = bf16[128,1024]{1,0:T(8,128)(2,1)S(1)} fusion(bf16[128,4096]{1,0:T(8,128)(2,1)} %all-gather.5.cloned.1.call-done, bf16[1024,4096]{0,1:T(8,128)(2,1)} %all-gather.3.cloned.1.call-done), kind=kOutput, calls=%fused_computation.41 | convolution fusion | flops 1073872896 | bytes 9699328 | tf_op jit(solution)/shard_map/dot_general | solution.py:147
  302.0 3.4 convert_bitcast_fusion
  305.4 4.2 %copy.113 = bf16[8,128,1024]{2,0,1:T(8,128)(2,1)} copy(bf16[8,128,1024]{1,2,0:T(8,128)(2,1)} %get-tuple-element.71) | data formatting | bytes 4194304 | tf_op jit(solution)/shard_map/reshape.68
  311.9 2.4 fusion.15
  315.1 9.5 %collective-permute-start.15 = (bf16[2,128,1,128]{3,1,2,0:T(8,128)(2,1)S(1)}, bf16[2,128,1,128]{3,1,2,0:T(8,128)(2,1)S(1)}, u32[]{:S(2)}, u32[]{:S(2)}) collective-permute-start(bf16[2,128,1,128]{3,1,2,0:T(8,128)(2,1)S(1)} %get-tuple-element.76), channel_id=1, source_target_pairs={{28,0},{32,4},{36,8},{40,12},{44,16},{48,20},{52,24},{56,28},{60,3... | collective-permute-start | bytes 196616 | tf_op jit(solution)/shard_map/ppermute | solution.py:16
  324.6 2.5 collective-permute-start.14
  328.2 5.2 %collective-permute-start.13 = (bf16[2,128,1,128]{3,1,0,2:T(8,128)(2,1)}, bf16[2,128,1,128]{3,1,0,2:T(8,128)(2,1)S(1)}, u32[]{:S(2)}, u32[]{:S(2)}) collective-permute-start(bf16[2,128,1,128]{3,1,0,2:T(8,128)(2,1)} %get-tuple-element.78), channel_id=1, source_target_pairs={{20,0},{24,4},{28,8},{32,12},{36,16},{40,20},{44,24},{48,28},{52,3... | collective-permute-start | bytes 196616 | tf_op jit(solution)/shard_map/ppermute | solution.py:16
  333.4 3.6 %collective-permute-start.12 = (bf16[2,128,1,128]{3,1,0,2:T(8,128)(2,1)}, bf16[2,128,1,128]{3,1,0,2:T(8,128)(2,1)S(1)}, u32[]{:S(2)}, u32[]{:S(2)}) collective-permute-start(bf16[2,128,1,128]{3,1,0,2:T(8,128)(2,1)} %get-tuple-element.79), channel_id=1, source_target_pairs={{16,0},{20,4},{24,8},{28,12},{32,16},{36,20},{40,24},{44,28},{48,3... | collective-permute-start | bytes 196616 | tf_op jit(solution)/shard_map/ppermute | solution.py:16
  337.0 4.4 %collective-permute-start.11 = (bf16[2,128,1,128]{3,1,0,2:T(8,128)(2,1)S(1)}, bf16[2,128,1,128]{3,1,0,2:T(8,128)(2,1)S(1)}, u32[]{:S(2)}, u32[]{:S(2)}) collective-permute-start(bf16[2,128,1,128]{3,1,0,2:T(8,128)(2,1)S(1)} %get-tuple-element.80), channel_id=1, source_target_pairs={{12,0},{16,4},{20,8},{24,12},{28,16},{32,20},{36,24},{40,28},{44,3... | collective-permute-start | bytes 196616 | tf_op jit(solution)/shard_map/ppermute | solution.py:16
  (144 shorter events, 62.1 us)
Async XLA Ops:
  7.2 167.5 %copy-start = (bf16[1,768,1024]{2,1,0:T(8,128)(2,1)S(1)}, bf16[1,768,1024]{2,1,0:T(8,128)(2,1)}, u32[]{:S(2)}) copy-start(bf16[1,768,1024]{2,1,0:T(8,128)(2,1)} %param.18) | copy-start | bytes 4718596
  7.2 267.0 %all-gather.3.cloned.1.call-start = ((), (), s32[]{:S(2)}) async-start(), calls=%async_computation.3 | async-start | bytes 8454144 | tf_op jit(solution)/shard_map/all_gather | solution.py:105
  29.9 18.2 %copy-start.20 = (bf16[128,1,128]{2,0,1:T(8,128)(2,1)S(1)}, bf16[128,1,128]{2,0,1:T(8,128)(2,1)}, u32[]{:S(2)}) copy-start(bf16[128,1,128]{2,0,1:T(8,128)(2,1)} %param.23) | copy-start | bytes 98308
  29.9 18.2 %copy-start.21 = (bf16[128,1,128]{2,0,1:T(8,128)(2,1)S(1)}, bf16[128,1,128]{2,0,1:T(8,128)(2,1)}, u32[]{:S(2)}) copy-start(bf16[128,1,128]{2,0,1:T(8,128)(2,1)} %param.22) | copy-start | bytes 98308
  29.9 135.0 %all-to-all-start = ((bf16[128,112,128]{2,1,0:T(8,128)(2,1)}), bf16[128,112,128]{2,1,0:T(8,128)(2,1)}, u32[]{:S(2)}, u32[]{:S(2)}) async-start(bf16[128,112,128]{2,1,0:T(8,128)(2,1)} %fusion.7), calls=%async_computation | async-start | bytes 7340032 | tf_op jit(solution)/shard_map/all_to_all | solution.py:113
  48.2 83.1 %collective-permute-start = (bf16[2,128,1,128]{3,1,2,0:T(8,128)(2,1)S(1)}, bf16[2,128,1,128]{3,1,2,0:T(8,128)(2,1)S(1)}, u32[]{:S(2)}, u32[]{:S(2)}) collective-permute-start(bf16[2,128,1,128]{3,1,2,0:T(8,128)(2,1)S(1)} %pad_maximum_fusion.2), channel_id=1, source_target_pairs={{0,4},{4,8},{8,12},{12,16},{16,20},{20,24},{24,28},{28,32},{32,36}... | collective-permute-start | bytes 196616 | tf_op jit(solution)/shard_map/ppermute | solution.py:16
  51.5 84.4 %collective-permute-start.1 = (bf16[2,128,1,128]{3,1,2,0:T(8,128)(2,1)S(1)}, bf16[2,128,1,128]{3,1,2,0:T(8,128)(2,1)S(1)}, u32[]{:S(2)}, u32[]{:S(2)}) collective-permute-start(bf16[2,128,1,128]{3,1,2,0:T(8,128)(2,1)S(1)} %pad_maximum_fusion.2), channel_id=1, source_target_pairs={{0,8},{4,12},{8,16},{12,20},{16,24},{20,28},{24,32},{28,36},{32,40... | collective-permute-start | bytes 196616 | tf_op jit(solution)/shard_map/ppermute | solution.py:16
  54.7 107.9 %collective-permute-start.2 = (bf16[2,128,1,128]{3,1,2,0:T(8,128)(2,1)S(1)}, bf16[2,128,1,128]{3,1,2,0:T(8,128)(2,1)S(1)}, u32[]{:S(2)}, u32[]{:S(2)}) collective-permute-start(bf16[2,128,1,128]{3,1,2,0:T(8,128)(2,1)S(1)} %pad_maximum_fusion.2), channel_id=1, source_target_pairs={{0,12},{4,16},{8,20},{12,24},{16,28},{20,32},{24,36},{28,40},{32,4... | collective-permute-start | bytes 196616 | tf_op jit(solution)/shard_map/ppermute | solution.py:16
  57.9 104.7 %collective-permute-start.3 = (bf16[2,128,1,128]{3,1,2,0:T(8,128)(2,1)S(1)}, bf16[2,128,1,128]{3,1,2,0:T(8,128)(2,1)S(1)}, u32[]{:S(2)}, u32[]{:S(2)}) collective-permute-start(bf16[2,128,1,128]{3,1,2,0:T(8,128)(2,1)S(1)} %pad_maximum_fusion.2), channel_id=1, source_target_pairs={{0,16},{4,20},{8,24},{12,28},{16,32},{20,36},{24,40},{28,44},{32,4... | collective-permute-start | bytes 196616 | tf_op jit(solution)/shard_map/ppermute | solution.py:16
  62.3 100.4 %collective-permute-start.4 = (bf16[2,128,1,128]{3,1,2,0:T(8,128)(2,1)S(1)}, bf16[2,128,1,128]{3,1,2,0:T(8,128)(2,1)S(1)}, u32[]{:S(2)}, u32[]{:S(2)}) collective-permute-start(bf16[2,128,1,128]{3,1,2,0:T(8,128)(2,1)S(1)} %pad_maximum_fusion.2), channel_id=1, source_target_pairs={{0,20},{4,24},{8,28},{12,32},{16,36},{20,40},{24,44},{28,48},{32,5... | collective-permute-start | bytes 196616 | tf_op jit(solution)/shard_map/ppermute | solution.py:16
  131.3 37.5 %copy-start.14 = (bf16[2,128,1,128]{3,1,2,0:T(8,128)(2,1)}, bf16[2,128,1,128]{3,1,2,0:T(8,128)(2,1)S(1)}, u32[]{:S(2)}) copy-start(bf16[2,128,1,128]{3,1,2,0:T(8,128)(2,1)S(1)} %collective-permute-done) | copy-start | bytes 196612
  131.3 31.4 %collective-permute-start.5 = (bf16[2,128,1,128]{3,1,2,0:T(8,128)(2,1)S(1)}, bf16[2,128,1,128]{3,1,2,0:T(8,128)(2,1)S(1)}, u32[]{:S(2)}, u32[]{:S(2)}) collective-permute-start(bf16[2,128,1,128]{3,1,2,0:T(8,128)(2,1)S(1)} %pad_maximum_fusion.2), channel_id=1, source_target_pairs={{0,24},{4,28},{8,32},{12,36},{16,40},{20,44},{24,48},{28,52},{32,5... | collective-permute-start | bytes 196616 | tf_op jit(solution)/shard_map/ppermute | solution.py:16
  136.0 32.7 %copy-start.15 = (bf16[2,128,1,128]{3,1,2,0:T(8,128)(2,1)}, bf16[2,128,1,128]{3,1,2,0:T(8,128)(2,1)S(1)}, u32[]{:S(2)}) copy-start(bf16[2,128,1,128]{3,1,2,0:T(8,128)(2,1)S(1)} %collective-permute-done.1) | copy-start | bytes 196612
  136.0 29.0 %collective-permute-start.6 = (bf16[2,128,1,128]{3,1,2,0:T(8,128)(2,1)S(1)}, bf16[2,128,1,128]{3,1,2,0:T(8,128)(2,1)S(1)}, u32[]{:S(2)}, u32[]{:S(2)}) collective-permute-start(bf16[2,128,1,128]{3,1,2,0:T(8,128)(2,1)S(1)} %pad_maximum_fusion.2), channel_id=1, source_target_pairs={{0,28},{4,32},{8,36},{12,40},{16,44},{20,48},{24,52},{28,56},{32,6... | collective-permute-start | bytes 196616 | tf_op jit(solution)/shard_map/ppermute | solution.py:16
  180.5 33.5 %all-to-all-start.1 = ((bf16[4,192,1536]{2,1,0:T(8,128)(2,1)}), bf16[4,192,1536]{2,1,0:T(8,128)(2,1)}, u32[]{:S(2)}, u32[]{:S(2)}) async-start(bf16[4,192,1536]{2,1,0:T(8,128)(2,1)} %bitcast.189), calls=%async_computation.1 | async-start | bytes 4718592 | tf_op jit(solution)/shard_map/all_to_all | solution.py:122
  217.8 50.7 %copy-start.11 = (f32[128,8]{0,1:T(8,128)S(1)}, f32[128,8]{0,1:T(8,128)}, u32[]{:S(2)}) copy-start(f32[128,8]{0,1:T(8,128)} %param.15) | copy-start | bytes 12292
  217.8 4.4 %collective-permute-start.7 = (f32[1536]{0:T(1024)S(1)}, f32[1536]{0:T(1024)S(1)}, u32[]{:S(2)}, u32[]{:S(2)}) collective-permute-start(f32[1536]{0:T(1024)S(1)} %fusion.23), channel_id=1, source_target_pairs={{0,1},{1,0},{2,3},{3,2},{4,5},{5,4},{6,7},{7,6},{8,9},{9,8},{10,11... | collective-permute-start | bytes 18440 | tf_op jit(solution)/shard_map/ppermute | solution.py:24
  222.2 5.9 %collective-permute-start.8 = (f32[1536]{0:T(1024)S(1)}, f32[1536]{0:T(1024)S(1)}, u32[]{:S(2)}, u32[]{:S(2)}) collective-permute-start(f32[1536]{0:T(1024)S(1)} %add.151), channel_id=1, source_target_pairs={{0,2},{1,3},{2,0},{3,1},{4,6},{5,7},{6,4},{7,5},{8,10},{9,11},{10,... | collective-permute-start | bytes 18440 | tf_op jit(solution)/shard_map/ppermute | solution.py:24
  228.9 22.8 %all-to-all-start.2 = ((f32[128,1,12]{2,1,0:T(1,128)}), f32[128,1,12]{2,1,0:T(1,128)}, u32[]{:S(2)}, u32[]{:S(2)}) async-start(f32[128,1,12]{2,1,0:T(1,128)} %bitcast.192), calls=%async_computation.2 | async-start | bytes 131072 | tf_op jit(solution)/shard_map/all_to_all | solution.py:137
  243.5 52.0 %all-gather.5.cloned.1.call-start = ((), (), s32[]{:S(2)}) async-start(), calls=%async_computation.4 | async-start | bytes 1310720 | tf_op jit(solution)/shard_map/all_gather | solution.py:146
  255.4 16.7 %copy-start.10 = (bf16[128,1024]{1,0:T(8,128)(2,1)S(1)}, bf16[128,1024]{1,0:T(8,128)(2,1)}, u32[]{:S(2)}) copy-start(bf16[128,1024]{1,0:T(8,128)(2,1)} %param.13) | copy-start | bytes 786436
  255.4 22.3 %copy-start.6 = (bf16[128,8,128]{2,1,0:T(8,128)(2,1)S(1)}, bf16[128,8,128]{2,1,0:T(8,128)(2,1)}, u32[]{:S(2)}) copy-start(bf16[128,8,128]{2,1,0:T(8,128)(2,1)} %param.21) | copy-start | bytes 786436
  283.8 16.8 %copy-start.8 = (bf16[2,1024,1,128]{3,1,2,0:T(8,128)(2,1)S(1)}, bf16[2,1024,1,128]{3,1,2,0:T(8,128)(2,1)}, u32[]{:S(2)}) copy-start(bf16[2,1024,1,128]{3,1,2,0:T(8,128)(2,1)} %constant_dynamic-update-slice_fusion) | copy-start | bytes 1572868
  314.3 31.4 %copy-start.3 = (bf16[8,128,1024]{1,2,0:T(8,128)(2,1)S(1)}, bf16[8,128,1024]{1,2,0:T(8,128)(2,1)}, u32[]{:S(2)}) copy-start(bf16[8,128,1024]{1,2,0:T(8,128)(2,1)} %get-tuple-element.72) | copy-start | bytes 6291460
  314.3 31.4 %copy-start.9 = (bf16[2,1024,1,128]{3,1,2,0:T(8,128)(2,1)S(1)}, bf16[2,1024,1,128]{3,1,2,0:T(8,128)(2,1)}, u32[]{:S(2)}) copy-start(bf16[2,1024,1,128]{3,1,2,0:T(8,128)(2,1)} %constant_dynamic-update-slice_fusion) | copy-start | bytes 1572868
  315.1 26.4 %collective-permute-start.15 = (bf16[2,128,1,128]{3,1,2,0:T(8,128)(2,1)S(1)}, bf16[2,128,1,128]{3,1,2,0:T(8,128)(2,1)S(1)}, u32[]{:S(2)}, u32[]{:S(2)}) collective-permute-start(bf16[2,128,1,128]{3,1,2,0:T(8,128)(2,1)S(1)} %get-tuple-element.76), channel_id=1, source_target_pairs={{28,0},{32,4},{36,8},{40,12},{44,16},{48,20},{52,24},{56,28},{60,3... | collective-permute-start | bytes 196616 | tf_op jit(solution)/shard_map/ppermute | solution.py:16
  324.6 18.9 %collective-permute-start.14 = (bf16[2,128,1,128]{3,1,0,2:T(8,128)(2,1)S(1)}, bf16[2,128,1,128]{3,1,0,2:T(8,128)(2,1)S(1)}, u32[]{:S(2)}, u32[]{:S(2)}) collective-permute-start(bf16[2,128,1,128]{3,1,0,2:T(8,128)(2,1)S(1)} %get-tuple-element.77), channel_id=1, source_target_pairs={{24,0},{28,4},{32,8},{36,12},{40,16},{44,20},{48,24},{52,28},{56,3... | collective-permute-start | bytes 196616 | tf_op jit(solution)/shard_map/ppermute | solution.py:16
  328.2 18.9 %collective-permute-start.13 = (bf16[2,128,1,128]{3,1,0,2:T(8,128)(2,1)}, bf16[2,128,1,128]{3,1,0,2:T(8,128)(2,1)S(1)}, u32[]{:S(2)}, u32[]{:S(2)}) collective-permute-start(bf16[2,128,1,128]{3,1,0,2:T(8,128)(2,1)} %get-tuple-element.78), channel_id=1, source_target_pairs={{20,0},{24,4},{28,8},{32,12},{36,16},{40,20},{44,24},{48,28},{52,3... | collective-permute-start | bytes 196616 | tf_op jit(solution)/shard_map/ppermute | solution.py:16
  333.4 13.7 %collective-permute-start.12 = (bf16[2,128,1,128]{3,1,0,2:T(8,128)(2,1)}, bf16[2,128,1,128]{3,1,0,2:T(8,128)(2,1)S(1)}, u32[]{:S(2)}, u32[]{:S(2)}) collective-permute-start(bf16[2,128,1,128]{3,1,0,2:T(8,128)(2,1)} %get-tuple-element.79), channel_id=1, source_target_pairs={{16,0},{20,4},{24,8},{28,12},{32,16},{36,20},{40,24},{44,28},{48,3... | collective-permute-start | bytes 196616 | tf_op jit(solution)/shard_map/ppermute | solution.py:16
  337.0 10.1 %collective-permute-start.11 = (bf16[2,128,1,128]{3,1,0,2:T(8,128)(2,1)S(1)}, bf16[2,128,1,128]{3,1,0,2:T(8,128)(2,1)S(1)}, u32[]{:S(2)}, u32[]{:S(2)}) collective-permute-start(bf16[2,128,1,128]{3,1,0,2:T(8,128)(2,1)S(1)} %get-tuple-element.80), channel_id=1, source_target_pairs={{12,0},{16,4},{20,8},{24,12},{28,16},{32,20},{36,24},{40,28},{44,3... | collective-permute-start | bytes 196616 | tf_op jit(solution)/shard_map/ppermute | solution.py:16
  341.4 5.7 %collective-permute-start.10 = (bf16[2,128,1,128]{3,1,0,2:T(8,128)(2,1)S(1)}, bf16[2,128,1,128]{3,1,0,2:T(8,128)(2,1)S(1)}, u32[]{:S(2)}, u32[]{:S(2)}) collective-permute-start(bf16[2,128,1,128]{3,1,0,2:T(8,128)(2,1)S(1)} %get-tuple-element.81), channel_id=1, source_target_pairs={{8,0},{12,4},{16,8},{20,12},{24,16},{28,20},{32,24},{36,28},{40,32... | collective-permute-start | bytes 196616 | tf_op jit(solution)/shard_map/ppermute | solution.py:16
  343.5 5.6 %collective-permute-start.9 = (bf16[2,128,1,128]{3,1,0,2:T(8,128)(2,1)S(1)}, bf16[2,128,1,128]{3,1,0,2:T(8,128)(2,1)S(1)}, u32[]{:S(2)}, u32[]{:S(2)}) collective-permute-start(bf16[2,128,1,128]{3,1,0,2:T(8,128)(2,1)S(1)} %get-tuple-element.75), channel_id=1, source_target_pairs={{4,0},{8,4},{12,8},{16,12},{20,16},{24,20},{28,24},{32,28},{36,32}... | collective-permute-start | bytes 196616 | tf_op jit(solution)/shard_map/ppermute | solution.py:16
  (15 other events, 80.5 us)
Sparse Core Ops, SparseCore 0:
  11.1 172.5 all-gather.2
  274.3 21.1 all-gather.4
